TPU v7x, 32 devices: a whole 2x2x4 slice. The times are simulated.
32 devices in a mesh: row: 4 (over y, x), seq: 8 (over z, core).
Axes of the slice: x: 2, y: 2, z: 4, core: 2. Of those that a mesh axis runs over, the one named last changes fastest.
Arguments:
- inputs: float32 [4, 1024, 1536], P('row', 'seq'), may hold values from -6 to 6
- doc_ids: int32 [4, 1024], P('row'), may hold values from 0 to 3, never falling along the last dimension, each value on 1 to 512 neighbouring positions
- w_query: bfloat16 [1536, 1536], replicated, may hold values from -0.15625 to 0.15625
- w_key: bfloat16 [1536, 1536], replicated, may hold values from -0.15625 to 0.15625
- w_value: bfloat16 [1536, 1536], replicated, may hold values from -0.15625 to 0.15625
- w_out: bfloat16 [1536, 1536], replicated, may hold values from -1 to 1
- gain_attn: float32 [1536], replicated, may hold values from 0.25 to 1.75
- gain_ffn: float32 [1536], replicated, may hold values from 0.25 to 1.75
- conv_taps: float32 [16, 6, 11], replicated, may hold values from -0.9 to 0.9
- head_mix: float32 [8, 2, 2], replicated, may hold values from 0.25 to 1.75
- w_gate: bfloat16 [1536, 4096], P('row', 'seq'), may hold values from -0.15625 to 0.15625
- w_up: bfloat16 [1536, 4096], P('row', 'seq'), may hold values from -0.15625 to 0.15625
- w_down: bfloat16 [4096, 1536], P('seq', 'row'), may hold values from -0.09375 to 0.09375
- cotangent: float32 [4, 1024, 1536], P('row', 'seq'), may hold values from -6 to 6
Outputs:
- outputs: float32 [4, 1024, 1536], P('row', 'seq')
- grad_inputs: float32 [4, 1024, 1536], P('row', 'seq')
- grad_w_query: float32 [1536, 1536], P(('row', 'seq'))
- grad_w_key: float32 [1536, 1536], P(('row', 'seq'))
- grad_w_value: float32 [1536, 1536], P(('row', 'seq'))
- grad_w_out: float32 [1536, 1536], P(('row', 'seq'))
- grad_gain_attn: float32 [1536], P(('row', 'seq'))
- grad_gain_ffn: float32 [1536], P(('row', 'seq'))
- grad_taps: float32 [16, 6, 11], replicated
- grad_mix: float32 [8, 2, 2], replicated
- grad_w_gate: float32 [1536, 4096], P('row', 'seq')
- grad_w_up: float32 [1536, 4096], P('row', 'seq')
- grad_w_down: float32 [4096, 1536], P('seq', 'row')
Inputs may be any that keep to these rules, and one draw needn't show every extreme that they name: `doc_ids`: along a row the ids never decrease; each of the 4 ids of a row covers 1 to 512 positions, and one covers exactly 512.
All inputs are finite; a program needn't handle non-finite values.
Results may differ from a plain program's by a relative error of at most 0.017.
Values may be sent and summed in bfloat16 or wider, within the bound.
No kernel may reach another device: no remote copies, remote signals or barrier semaphores. Data moves between devices by JAX's collectives and lax.ppermute only.
A program may use at most 256 MiB of HBM per device.

v0:
```python
import jax
import jax.numpy as jnp
from jax import lax
from jax.sharding import PartitionSpec as P

HEADS = 16
HD = 96
QCONV = 6
KCONV = 11


epsilon = 1e-06


def passed_along(block, axis, distance):
    devices = range(lax.axis_size(axis))
    route = [(i - distance, i) for i in devices if i - distance in devices]
    return lax.ppermute(block, axis, route)


def rms_scale(values):
    return lax.rsqrt(jnp.mean(values * values, axis=-1, keepdims=True) + epsilon)


def project(values, weight):
    return jnp.dot(values, weight, preferred_element_type=jnp.float32)


def contract_rows(left, right):
    return lax.dot_general(
        left, right, (((0,), (0,)), ((), ())), preferred_element_type=jnp.float32
    )


def contract_cols(left, right):
    return lax.dot_general(
        left, right, (((1,), (1,)), ((), ())), preferred_element_type=jnp.float32
    )


def key_conv(padded, taps, row_count, col_count):
    total = jnp.zeros(padded.shape[:2] + (row_count, col_count), jnp.float32)
    for shift_q in range(QCONV):
        for shift_k in range(KCONV):
            weight = taps[:, shift_q, shift_k][None, :, None, None]
            top_q = QCONV - 1 - shift_q
            top_k = KCONV - 1 - shift_k
            total = (
                total + weight * padded[:, :, top_q : top_q + row_count, top_k : top_k + col_count]
            )
    return total


def conv_back(padded, taps, row_count, col_count):
    total = jnp.zeros(padded.shape[:2] + (row_count, col_count), jnp.float32)
    for shift_q in range(QCONV):
        for shift_k in range(KCONV):
            weight = taps[:, shift_q, shift_k][None, :, None, None]
            total = (
                total
                + weight
                * padded[:, :, shift_q : shift_q + row_count, shift_k : shift_k + col_count]
            )
    return total


def tap_grads(grad_conv, padded, row_count, col_count):
    entries = []
    for shift_q in range(QCONV):
        for shift_k in range(KCONV):
            top_q = QCONV - 1 - shift_q
            top_k = KCONV - 1 - shift_k
            piece = padded[:, :, top_q : top_q + row_count, top_k : top_k + col_count]
            entries.append(jnp.sum(grad_conv * piece, axis=(0, 2, 3)))
    return jnp.stack(entries, axis=1).reshape(2, QCONV, KCONV)


def mix_heads(probs, mixing):
    first = mixing[:, 0][None, :, None, None] * probs[:, 0:1]
    second = mixing[:, 1][None, :, None, None] * probs[:, 1:2]
    return first + second


def mix_back(grads, mixing):
    first = mixing[0, :][None, :, None, None] * grads[:, 0:1]
    second = mixing[1, :][None, :, None, None] * grads[:, 1:2]
    return first + second


def shards(
    inputs,
    doc_ids,
    w_query,
    w_key,
    w_value,
    w_out,
    gain_attn,
    gain_ffn,
    conv_taps,
    head_mix,
    w_gate,
    w_up,
    w_down,
    cotangent,
):
    row_dev, block_len, width = inputs.shape
    seq_count = lax.axis_size("seq")
    seq_index = lax.axis_index("seq")
    length = block_len * seq_count
    rim_rows = QCONV - 1
    ext_rows = block_len + rim_rows
    groups = HEADS // 2
    pair_width = 2 * HD
    score_scale = HD ** (-0.5)
    token_count = row_dev * block_len
    flat_in = inputs.reshape(token_count, width)
    scale_one = rms_scale(flat_in)
    normed = (flat_in * scale_one * gain_attn).astype(jnp.bfloat16)
    normed_rows = normed.reshape(row_dev, block_len, width)
    query_own = project(normed_rows, w_query).astype(jnp.bfloat16)
    key_own = project(normed_rows, w_key).astype(jnp.bfloat16)
    value_own = project(normed_rows, w_value).astype(jnp.bfloat16)
    key_full, value_full = (
        lax.all_gather(key_own, "seq", axis=1, tiled=True),
        lax.all_gather(value_own, "seq", axis=1, tiled=True),
    )
    prior = passed_along(query_own[:, block_len - rim_rows :, :], "seq", 1)
    query_ext = jnp.concatenate([prior, query_own], axis=1)
    positions = jnp.arange(length, dtype=jnp.int32)
    ext_pos = seq_index * block_len - rim_rows + jnp.arange(ext_rows, dtype=jnp.int32)
    docs_padded = jnp.pad(doc_ids, ((0, 0), (rim_rows, 0)), constant_values=-1)
    ext_docs = lax.dynamic_slice_in_dim(docs_padded, seq_index * block_len, ext_rows, 1)
    ext_mask = (positions[None, None, :] <= ext_pos[None, :, None]) & (
        ext_docs[:, :, None] == doc_ids[:, None, :]
    )
    own_mask = ext_mask[:, rim_rows:, :]

    def group_slice(values, index):
        part = lax.dynamic_slice_in_dim(values, index * pair_width, pair_width, 2)
        return part.reshape(part.shape[0], part.shape[1], 2, HD)

    def group_scores(index):
        query_grp = group_slice(query_ext, index)
        key_grp = group_slice(key_full, index)
        taps = lax.dynamic_slice_in_dim(conv_taps, index * 2, 2, 0)
        scores = (
            jnp.einsum("rihd,rjhd->rhij", query_grp, key_grp, preferred_element_type=jnp.float32)
            * score_scale
        )
        masked = jnp.where(ext_mask[:, None], scores, 0.0)
        padded = jnp.pad(masked, ((0, 0), (0, 0), (0, 0), (KCONV - 1, 0)))
        conv = key_conv(padded, taps, block_len, length)
        logits = jnp.where(own_mask[:, None], conv, -jnp.inf)
        return (query_grp, key_grp, taps, padded, logits)

    def forward_group(carry, index):
        _, _, _, _, logits = group_scores(index)
        mixing = lax.dynamic_index_in_dim(head_mix, index, 0, keepdims=False)
        highest = jnp.max(logits, axis=-1, keepdims=True)
        expd = jnp.exp(logits - highest)
        denom = jnp.sum(expd, axis=-1, keepdims=True)
        probs = expd / denom
        mixed = mix_heads(probs, mixing).astype(jnp.bfloat16)
        value_grp = group_slice(value_full, index)
        heads = jnp.einsum("rhij,rjhd->rihd", mixed, value_grp, preferred_element_type=jnp.float32)
        carry = lax.dynamic_update_slice_in_dim(
            carry, heads.reshape(row_dev, block_len, pair_width), index * pair_width, 2
        )
        return (carry, (highest + jnp.log(denom))[..., 0])

    heads_all, log_norms = lax.scan(
        forward_group, jnp.zeros((row_dev, block_len, width), jnp.float32), jnp.arange(groups)
    )
    flat_heads = heads_all.astype(jnp.bfloat16).reshape(token_count, width)
    middle = flat_in + project(flat_heads, w_out)
    scale_two = rms_scale(middle)
    normed_ffn = (middle * scale_two * gain_ffn).astype(jnp.bfloat16)
    gate_full, up_full, down_full = (
        lax.all_gather(w_gate, "row", axis=0, tiled=True),
        lax.all_gather(w_up, "row", axis=0, tiled=True),
        lax.all_gather(w_down, "row", axis=1, tiled=True),
    )
    hid_width = gate_full.shape[1]
    joint = jnp.concatenate([gate_full, up_full], axis=1)
    ffn_rows = lax.all_gather(normed_ffn, "seq", axis=0, tiled=True)
    gate_up = project(ffn_rows, joint)
    gate_vals = gate_up[:, :hid_width]
    up_vals = gate_up[:, hid_width:]
    hidden = (jax.nn.silu(gate_vals) * up_vals).astype(jnp.bfloat16)
    ffn_out = lax.psum_scatter(
        project(hidden, down_full).astype(jnp.bfloat16), "seq", scatter_dimension=0, tiled=True
    ).astype(jnp.float32)
    outputs = middle + ffn_out
    cot_flat = cotangent.reshape(token_count, width)
    cot_low = cot_flat.astype(jnp.bfloat16)
    cot_rows = lax.all_gather(cot_low, "seq", axis=0, tiled=True)
    grad_hidden = contract_cols(cot_rows, down_full)
    grad_down_part = contract_rows(hidden, cot_rows)
    sigmoid_gate = jax.nn.sigmoid(gate_vals)
    grad_gate_vals = grad_hidden * up_vals * sigmoid_gate * (1.0 + gate_vals * (1.0 - sigmoid_gate))
    grad_up_vals = grad_hidden * gate_vals * sigmoid_gate
    grad_joint = jnp.concatenate([grad_gate_vals, grad_up_vals], axis=1).astype(jnp.bfloat16)
    grad_joint_w = contract_rows(ffn_rows, grad_joint)
    grad_normed_ffn = lax.psum_scatter(
        contract_cols(grad_joint, joint).astype(jnp.bfloat16),
        "seq",
        scatter_dimension=0,
        tiled=True,
    ).astype(jnp.float32)
    grad_w_gate, grad_w_up, grad_w_down = (
        lax.psum_scatter(
            grad_joint_w[:, :hid_width].astype(jnp.bfloat16), "row", scatter_dimension=0, tiled=True
        ).astype(jnp.float32),
        lax.psum_scatter(
            grad_joint_w[:, hid_width:].astype(jnp.bfloat16), "row", scatter_dimension=0, tiled=True
        ).astype(jnp.float32),
        lax.psum_scatter(
            grad_down_part.astype(jnp.bfloat16), "row", scatter_dimension=1, tiled=True
        ).astype(jnp.float32),
    )
    gain_ffn_part = jnp.sum(grad_normed_ffn * middle * scale_two, axis=0)
    scaled_two = grad_normed_ffn * gain_ffn
    grad_middle = (
        cot_flat
        + scale_two * scaled_two
        - middle * scale_two**3 * jnp.mean(scaled_two * middle, axis=-1, keepdims=True)
    )
    grad_attn = grad_middle.astype(jnp.bfloat16)
    grad_out_part = contract_rows(flat_heads, grad_attn)
    grad_heads = (
        contract_cols(grad_attn, w_out).astype(jnp.bfloat16).reshape(row_dev, block_len, width)
    )

    def backward_group(carry, index):
        query_buf, key_buf, value_buf = carry
        query_grp, key_grp, taps, padded, logits = group_scores(index)
        mixing = lax.dynamic_index_in_dim(head_mix, index, 0, keepdims=False)
        log_norm = lax.dynamic_index_in_dim(log_norms, index, 0, keepdims=False)
        probs = jnp.exp(logits - log_norm[..., None])
        mixed = mix_heads(probs, mixing).astype(jnp.bfloat16)
        grad_grp = group_slice(grad_heads, index)
        value_grp = group_slice(value_full, index)
        grad_mixed = jnp.einsum(
            "rihd,rjhd->rhij", grad_grp, value_grp, preferred_element_type=jnp.float32
        )
        grad_value_grp = jnp.einsum(
            "rhij,rihd->rjhd", mixed, grad_grp, preferred_element_type=jnp.float32
        )
        grad_mix_grp = jnp.stack(
            [
                jnp.sum(grad_mixed * probs[:, 0:1], axis=(0, 2, 3)),
                jnp.sum(grad_mixed * probs[:, 1:2], axis=(0, 2, 3)),
            ],
            axis=1,
        )
        grad_probs = mix_back(grad_mixed, mixing)
        inner = jnp.sum(grad_probs * probs, axis=-1, keepdims=True)
        grad_conv = probs * (grad_probs - inner)
        grad_taps_grp = tap_grads(grad_conv, padded, block_len, length)
        following = passed_along(
            grad_conv[:, :, :rim_rows, :].astype(jnp.bfloat16), "seq", -1
        ).astype(jnp.float32)
        joined = jnp.concatenate([grad_conv, following], axis=2)
        joined = jnp.pad(joined, ((0, 0), (0, 0), (0, 0), (0, KCONV - 1)))
        grad_masked = conv_back(joined, taps, block_len, length)
        grad_scores = jnp.where(own_mask[:, None], grad_masked, 0.0).astype(jnp.bfloat16)
        query_own_grp = query_grp[:, rim_rows:]
        grad_query_grp = (
            jnp.einsum("rhij,rjhd->rihd", grad_scores, key_grp, preferred_element_type=jnp.float32)
            * score_scale
        )
        grad_key_grp = (
            jnp.einsum(
                "rhij,rihd->rjhd", grad_scores, query_own_grp, preferred_element_type=jnp.float32
            )
            * score_scale
        )
        query_buf = lax.dynamic_update_slice_in_dim(
            query_buf, grad_query_grp.reshape(row_dev, block_len, pair_width), index * pair_width, 2
        )
        key_buf = lax.dynamic_update_slice_in_dim(
            key_buf, grad_key_grp.reshape(row_dev, length, pair_width), index * pair_width, 2
        )
        value_buf = lax.dynamic_update_slice_in_dim(
            value_buf, grad_value_grp.reshape(row_dev, length, pair_width), index * pair_width, 2
        )
        return ((query_buf, key_buf, value_buf), (grad_taps_grp, grad_mix_grp))

    start_bufs = (
        jnp.zeros((row_dev, block_len, width), jnp.float32),
        jnp.zeros((row_dev, length, width), jnp.float32),
        jnp.zeros((row_dev, length, width), jnp.float32),
    )
    (grad_query_sum, grad_key_sum, grad_value_sum), (taps_parts, mix_parts) = lax.scan(
        backward_group, start_bufs, jnp.arange(groups)
    )
    grad_key_own, grad_value_own = (
        lax.psum_scatter(
            grad_key_sum.astype(jnp.bfloat16), "seq", scatter_dimension=1, tiled=True
        ).astype(jnp.float32),
        lax.psum_scatter(
            grad_value_sum.astype(jnp.bfloat16), "seq", scatter_dimension=1, tiled=True
        ).astype(jnp.float32),
    )
    grad_query_low = grad_query_sum.astype(jnp.bfloat16).reshape(token_count, width)
    grad_key_low = grad_key_own.astype(jnp.bfloat16).reshape(token_count, width)
    grad_value_low = grad_value_own.astype(jnp.bfloat16).reshape(token_count, width)
    grad_query_w = contract_rows(normed, grad_query_low)
    grad_key_w = contract_rows(normed, grad_key_low)
    grad_value_w = contract_rows(normed, grad_value_low)
    grad_normed = (
        contract_cols(grad_query_low, w_query)
        + contract_cols(grad_key_low, w_key)
        + contract_cols(grad_value_low, w_value)
    )
    gain_attn_part = jnp.sum(grad_normed * flat_in * scale_one, axis=0)
    scaled_one = grad_normed * gain_attn
    grad_inputs = (
        grad_middle
        + scale_one * scaled_one
        - flat_in * scale_one**3 * jnp.mean(scaled_one * flat_in, axis=-1, keepdims=True)
    )
    grad_w_query, grad_w_key, grad_w_value, grad_w_out, grad_gain_attn, grad_gain_ffn = (
        lax.psum_scatter(grad_query_w, ("row", "seq"), scatter_dimension=0, tiled=True),
        lax.psum_scatter(grad_key_w, ("row", "seq"), scatter_dimension=0, tiled=True),
        lax.psum_scatter(grad_value_w, ("row", "seq"), scatter_dimension=0, tiled=True),
        lax.psum_scatter(grad_out_part, ("row", "seq"), scatter_dimension=0, tiled=True),
        lax.psum_scatter(gain_attn_part, ("row", "seq"), scatter_dimension=0, tiled=True),
        lax.psum_scatter(gain_ffn_part, ("row", "seq"), scatter_dimension=0, tiled=True),
    )
    grad_taps, grad_mix = lax.psum(
        (taps_parts.reshape(HEADS, QCONV, KCONV), mix_parts), ("row", "seq")
    )
    return (
        outputs.reshape(row_dev, block_len, width),
        grad_inputs.reshape(row_dev, block_len, width),
        grad_w_query,
        grad_w_key,
        grad_w_value,
        grad_w_out,
        grad_gain_attn,
        grad_gain_ffn,
        grad_taps,
        grad_mix,
        grad_w_gate,
        grad_w_up,
        grad_w_down,
    )


def solution(mesh):
    return jax.shard_map(
        shards,
        mesh=mesh,
        in_specs=(
            P("row", "seq", None),
            P("row", None),
            P(),
            P(),
            P(),
            P(),
            P(),
            P(),
            P(),
            P(),
            P("row", "seq"),
            P("row", "seq"),
            P("seq", "row"),
            P("row", "seq", None),
        ),
        out_specs=(
            P("row", "seq", None),
            P("row", "seq", None),
            P(("row", "seq"), None),
            P(("row", "seq"), None),
            P(("row", "seq"), None),
            P(("row", "seq"), None),
            P(("row", "seq")),
            P(("row", "seq")),
            P(),
            P(),
            P("row", "seq"),
            P("row", "seq"),
            P("seq", "row"),
        ),
        check_vma=False,
    )
```

profile of v0, /device:TPU:0, one launch (start us, length us, event | category | flops | bytes accessed | tf_op | source)
XLA Modules:
  0.0 2029.0 jit_solution(5315049456871664817)
XLA Ops:
  26.9 29.1 %all-gather.22.cloned.1.call-done = bf16[1024,1536]{1,0:T(8,128)(2,1)} async-done(((bf16[128,1536]{1,0:T(8,128)(2,1)}), bf16[1024,1536]{1,0:T(8,128)(2,1)}) %all-gather.22.cloned.1.call-update) | async-done | bytes 3145744 | tf_op jit(solution)/shard_map/all_gather | solution.py:124
  60.7 34.9 %all-gather.20.cloned.1.call-done = bf16[1024,1536]{1,0:T(8,128)(2,1)} async-done(((bf16[128,1536]{1,0:T(8,128)(2,1)}), bf16[1024,1536]{1,0:T(8,128)(2,1)}) %all-gather.20.cloned.1.call-update) | async-done | bytes 3145744 | tf_op jit(solution)/shard_map/all_gather | solution.py:125
  101.1 214.6 %while.36 = (s32[]{:T(128)}, bf16[1,128,1536]{1,2,0:T(8,128)(2,1)}, f32[8,1,2,128]{3,2,1,0:T(2,128)}, s32[8]{0:T(128)S(1)}, bf16[1,1024,1536]{1,2,0:T(8,128)(2,1...) while((s32[]{:T(128)}, bf16[1,128,1536]{1,2,0:T(8,128)(2,1)}, ...), condition=%wide.region_4.5_spmd.clone, body=%wide.region_1.4_spmd.clone.sunk | while | flops 140544784 | bytes 19049572 | solution.py:171
  327.6 29.9 %all-gather.10.cloned.1.call-done = bf16[1024,1536]{1,0:T(8,128)(2,1)} async-done(((bf16[128,1536]{1,0:T(8,128)(2,1)}), bf16[1024,1536]{1,0:T(8,128)(2,1)}) %all-gather.10.cloned.1.call-update) | async-done | bytes 3145744 | tf_op jit(solution)/shard_map/all_gather | solution.py:185
  365.8 23.1 %all-gather.16.cloned.1.call-done = bf16[512,1536]{1,0:T(8,128)(2,1)} async-done(((bf16[512,384]{1,0:T(8,128)(2,1)}), bf16[512,1536]{1,0:T(8,128)(2,1)}) %all-gather.16.cloned.1.call-update) | async-done | bytes 1572880 | tf_op jit(solution)/shard_map/all_gather | solution.py:181
  388.9 40.5 %all-gather.18.cloned.1.call-done = bf16[1024,1536]{1,0:T(8,128)(2,1)} async-done(((bf16[128,1536]{1,0:T(8,128)(2,1)}), bf16[1024,1536]{1,0:T(8,128)(2,1)}) %all-gather.18.cloned.1.call-update) | async-done | bytes 3145744 | tf_op jit(solution)/shard_map/all_gather | solution.py:196
  448.3 34.0 %reduce-scatter.20.cloned.1.call-done = bf16[128,1536]{1,0:T(8,128)(2,1)} async-done(((bf16[1024,1536]{1,0:T(8,128)(2,1)}), bf16[128,1536]{1,0:T(8,128)(2,1)}) %reduce-scatter.20.cloned.1.call-update) | async-done | bytes 393232 | tf_op jit(solution)/shard_map/reduce_scatter | solution.py:204
  484.2 40.3 %reduce-scatter.18.cloned.1.call-done = bf16[128,1536]{1,0:T(8,128)(2,1)} async-done(((bf16[1024,1536]{1,0:T(8,128)(2,1)}), bf16[128,1536]{1,0:T(8,128)(2,1)}) %reduce-scatter.18.cloned.1.call-update) | async-done | bytes 393232 | tf_op jit(solution)/shard_map/reduce_scatter | solution.py:190
  536.2 705.5 %while.37 = (s32[]{:T(128)}, bf16[1,128,1536]{1,2,0:T(8,128)(2,1)}, bf16[1,1024,1536]{1,2,0:T(8,128)(2,1)}, bf16[1,1024,1536]{1,2,0:T(8,128)(2,1)}, f32[8,2,6,11...) while((s32[]{:T(128)}, bf16[1,128,1536]{1,2,0:T(8,128)(2,1)}, ...), condition=%wide.region_79.80_spmd.clone, body=%wide.region_9.79_spmd.clone.sunk | while | flops 365664896 | bytes 71641472 | solution.py:294
  563.8 19.9 multiply_reduce_fusion.76
  650.0 19.9 multiply_reduce_fusion.76
  736.3 19.9 multiply_reduce_fusion.76
  822.4 19.9 multiply_reduce_fusion.76
  908.7 19.9 multiply_reduce_fusion.76
  1167.4 19.9 multiply_reduce_fusion.76
  1318.8 34.6 %reduce-scatter.34.cloned.1.call-done = bf16[128,1536]{1,0:T(8,128)(2,1)} async-done(((bf16[1024,1536]{1,0:T(8,128)(2,1)}), bf16[128,1536]{1,0:T(8,128)(2,1)}) %reduce-scatter.34.cloned.1.call-update) | async-done | bytes 393232
  1360.6 26.1 %reduce-scatter.38.cloned.1.call-done = bf16[384,512]{1,0:T(8,128)(2,1)} async-done(((bf16[1536,512]{1,0:T(8,128)(2,1)}), bf16[384,512]{1,0:T(8,128)(2,1)}) %reduce-scatter.38.cloned.1.call-update) | async-done | bytes 393232
  1388.8 32.0 %reduce-scatter.30.cloned.1.call-done = bf16[384,512]{1,0:T(8,128)(2,1)} async-done(((bf16[1536,512]{1,0:T(8,128)(2,1)}), bf16[384,512]{1,0:T(8,128)(2,1)}) %reduce-scatter.30.cloned.1.call-update) | async-done | bytes 393232 | tf_op jit(solution)/shard_map/reduce_scatter | solution.py:211
  1422.8 32.0 %reduce-scatter.32.cloned.1.call-done = bf16[384,512]{1,0:T(8,128)(2,1)} async-done(((bf16[1536,512]{1,0:T(8,128)(2,1)}), bf16[384,512]{1,0:T(8,128)(2,1)}) %reduce-scatter.32.cloned.1.call-update) | async-done | bytes 393232 | tf_op jit(solution)/shard_map/reduce_scatter | solution.py:214
  1469.4 40.3 %all-reduce.6 = (f32[1536]{0:T(1024)S(1)}, f32[1536]{0:T(1024)S(1)}, f32[16,6,11]{2,0,1:T(8,128)S(1)}, f32[8,2,2]{0,2,1:T(2,128)}) all-reduce(f32[1536]{0:T(1024)S(1)} %get-tuple-element.622, f32[1536]{0:T(1024)S(1)} %copy-done.76, f32[16,6,11]{2,0,1:T(8,128)S(1)} %bitcast.760, ...), channel_id=12, replica_groups=mesh['row'=4,'seq'=8] {'row','seq'}, use_global_device_ids=true, to_apply=%region_88.89.clone | all-reduce | flops 4160 | bytes 33280
  1512.8 84.6 %reduce-scatter.28.cloned.1.call-done = f32[48,1536]{1,0:T(8,128)} async-done(((f32[1536,1536]{1,0:T(8,128)}), f32[48,1536]{1,0:T(8,128)}) %reduce-scatter.28.cloned.1.call-update) | async-done | bytes 294928 | tf_op jit(solution)/shard_map/reduce_scatter | solution.py:327
  1597.4 141.5 %reduce-scatter.22.cloned.1.call-done = f32[48,1536]{1,0:T(8,128)} async-done(((f32[1536,1536]{1,0:T(8,128)}), f32[48,1536]{1,0:T(8,128)}) %reduce-scatter.22.cloned.1.call-update) | async-done | bytes 294928 | tf_op jit(solution)/shard_map/reduce_scatter | solution.py:324
  1738.9 141.5 %reduce-scatter.26.cloned.1.call-done = f32[48,1536]{1,0:T(8,128)} async-done(((f32[1536,1536]{1,0:T(8,128)}), f32[48,1536]{1,0:T(8,128)}) %reduce-scatter.26.cloned.1.call-update) | async-done | bytes 294928 | tf_op jit(solution)/shard_map/reduce_scatter | solution.py:326
  1880.5 141.5 %reduce-scatter.24.cloned.1.call-done = f32[48,1536]{1,0:T(8,128)} async-done(((f32[1536,1536]{1,0:T(8,128)}), f32[48,1536]{1,0:T(8,128)}) %reduce-scatter.24.cloned.1.call-update) | async-done | bytes 294928 | tf_op jit(solution)/shard_map/reduce_scatter | solution.py:325
  (2435 shorter events, 910.1 us)
Async XLA Ops:
  7.2 48.8 %all-gather.22.cloned.1.call-start = ((), (), s32[]{:S(2)}) async-start(), calls=%async_computation.25 | async-start | bytes 3538944 | tf_op jit(solution)/shard_map/all_gather | solution.py:124
  14.9 80.7 %all-gather.20.cloned.1.call-start = ((), (), s32[]{:S(2)}) async-start(), calls=%async_computation.24 | async-start | bytes 3538944 | tf_op jit(solution)/shard_map/all_gather | solution.py:125
  18.8 303.4 %all-gather.12.cloned.1.call-start = ((), (), s32[]{:S(2)}) async-start(), calls=%async_computation.12 | async-start | bytes 1966080 | tf_op jit(solution)/shard_map/all_gather | solution.py:179
  19.6 305.3 %all-gather.14.cloned.1.call-start = ((), (), s32[]{:S(2)}) async-start(), calls=%async_computation.13 | async-start | bytes 1966080 | tf_op jit(solution)/shard_map/all_gather | solution.py:180
  25.2 332.4 %all-gather.10.cloned.1.call-start = ((), (), s32[]{:S(2)}) async-start(), calls=%async_computation.11 | async-start | bytes 3538944 | tf_op jit(solution)/shard_map/all_gather | solution.py:185
  320.3 68.6 %all-gather.16.cloned.1.call-start = ((), (), s32[]{:S(2)}) async-start(), calls=%async_computation.14 | async-start | bytes 1966080 | tf_op jit(solution)/shard_map/all_gather | solution.py:181
  320.9 108.5 %all-gather.18.cloned.1.call-start = ((), (), s32[]{:S(2)}) async-start(), calls=%async_computation.16 | async-start | bytes 3538944 | tf_op jit(solution)/shard_map/all_gather | solution.py:196
  321.8 160.6 %reduce-scatter.20.cloned.1.call-start = ((), (), s32[]{:S(2)}) async-start(), calls=%async_computation.17 | async-start | bytes 3538944 | tf_op jit(solution)/shard_map/reduce_scatter | solution.py:204
  442.9 81.5 %reduce-scatter.18.cloned.1.call-start = ((), (), s32[]{:S(2)}) async-start(), calls=%async_computation.15 | async-start | bytes 3538944 | tf_op jit(solution)/shard_map/reduce_scatter | solution.py:190
  448.3 863.1 %reduce-scatter.36.cloned.1.call-start = ((), (), s32[]{:S(2)}) async-start(), calls=%async_computation.27 | async-start | bytes 3538944
  591.2 25.4 %collective-permute-start = (bf16[1,2,5,1024]{3,2,1,0:T(8,128)(2,1)}, bf16[1,2,5,1024]{3,2,1,0:T(8,128)(2,1)S(1)}, u32[]{:S(2)}, u32[]{:S(2)}) collective-permute-start(bf16[1,2,5,1024]{3,2,1,0:T(8,128)(2,1)} %slice.4008), channel_id=1, source_target_pairs={{1,0},{2,1},{3,2},{4,3},{5,4},{6,5},{7,6},{9,8},{10,9},{11,10},{12... | collective-permute-start | bytes 61448 | tf_op jit(solution)/shard_map/while/body/eval_jaxpr/ppermute | solution.py:18
  677.4 25.4 %collective-permute-start = (bf16[1,2,5,1024]{3,2,1,0:T(8,128)(2,1)}, bf16[1,2,5,1024]{3,2,1,0:T(8,128)(2,1)S(1)}, u32[]{:S(2)}, u32[]{:S(2)}) collective-permute-start(bf16[1,2,5,1024]{3,2,1,0:T(8,128)(2,1)} %slice.4008), channel_id=1, source_target_pairs={{1,0},{2,1},{3,2},{4,3},{5,4},{6,5},{7,6},{9,8},{10,9},{11,10},{12... | collective-permute-start | bytes 61448 | tf_op jit(solution)/shard_map/while/body/eval_jaxpr/ppermute | solution.py:18
  849.9 25.4 %collective-permute-start = (bf16[1,2,5,1024]{3,2,1,0:T(8,128)(2,1)}, bf16[1,2,5,1024]{3,2,1,0:T(8,128)(2,1)S(1)}, u32[]{:S(2)}, u32[]{:S(2)}) collective-permute-start(bf16[1,2,5,1024]{3,2,1,0:T(8,128)(2,1)} %slice.4008), channel_id=1, source_target_pairs={{1,0},{2,1},{3,2},{4,3},{5,4},{6,5},{7,6},{9,8},{10,9},{11,10},{12... | collective-permute-start | bytes 61448 | tf_op jit(solution)/shard_map/while/body/eval_jaxpr/ppermute | solution.py:18
  936.1 25.4 %collective-permute-start = (bf16[1,2,5,1024]{3,2,1,0:T(8,128)(2,1)}, bf16[1,2,5,1024]{3,2,1,0:T(8,128)(2,1)S(1)}, u32[]{:S(2)}, u32[]{:S(2)}) collective-permute-start(bf16[1,2,5,1024]{3,2,1,0:T(8,128)(2,1)} %slice.4008), channel_id=1, source_target_pairs={{1,0},{2,1},{3,2},{4,3},{5,4},{6,5},{7,6},{9,8},{10,9},{11,10},{12... | collective-permute-start | bytes 61448 | tf_op jit(solution)/shard_map/while/body/eval_jaxpr/ppermute | solution.py:18
  1022.4 25.4 %collective-permute-start = (bf16[1,2,5,1024]{3,2,1,0:T(8,128)(2,1)}, bf16[1,2,5,1024]{3,2,1,0:T(8,128)(2,1)S(1)}, u32[]{:S(2)}, u32[]{:S(2)}) collective-permute-start(bf16[1,2,5,1024]{3,2,1,0:T(8,128)(2,1)} %slice.4008), channel_id=1, source_target_pairs={{1,0},{2,1},{3,2},{4,3},{5,4},{6,5},{7,6},{9,8},{10,9},{11,10},{12... | collective-permute-start | bytes 61448 | tf_op jit(solution)/shard_map/while/body/eval_jaxpr/ppermute | solution.py:18
  1108.6 25.4 %collective-permute-start = (bf16[1,2,5,1024]{3,2,1,0:T(8,128)(2,1)}, bf16[1,2,5,1024]{3,2,1,0:T(8,128)(2,1)S(1)}, u32[]{:S(2)}, u32[]{:S(2)}) collective-permute-start(bf16[1,2,5,1024]{3,2,1,0:T(8,128)(2,1)} %slice.4008), channel_id=1, source_target_pairs={{1,0},{2,1},{3,2},{4,3},{5,4},{6,5},{7,6},{9,8},{10,9},{11,10},{12... | collective-permute-start | bytes 61448 | tf_op jit(solution)/shard_map/while/body/eval_jaxpr/ppermute | solution.py:18
  1262.9 90.6 %reduce-scatter.34.cloned.1.call-start = ((), (), s32[]{:S(2)}) async-start(), calls=%async_computation.26 | async-start | bytes 3538944
  1281.8 104.8 %reduce-scatter.38.cloned.1.call-start = ((), (), s32[]{:S(2)}) async-start(), calls=%async_computation.28 | async-start | bytes 1966080
  1288.4 132.4 %reduce-scatter.30.cloned.1.call-start = ((), (), s32[]{:S(2)}) async-start(), calls=%async_computation.22 | async-start | bytes 1966080 | tf_op jit(solution)/shard_map/reduce_scatter | solution.py:211
  1296.1 158.7 %reduce-scatter.32.cloned.1.call-start = ((), (), s32[]{:S(2)}) async-start(), calls=%async_computation.23 | async-start | bytes 1966080 | tf_op jit(solution)/shard_map/reduce_scatter | solution.py:214
  1296.7 300.7 %reduce-scatter.28.cloned.1.call-start = ((), (), s32[]{:S(2)}) async-start(), calls=%async_computation.21 | async-start | bytes 9732096 | tf_op jit(solution)/shard_map/reduce_scatter | solution.py:327
  1302.4 436.6 %reduce-scatter.22.cloned.1.call-start = ((), (), s32[]{:S(2)}) async-start(), calls=%async_computation.18 | async-start | bytes 9732096 | tf_op jit(solution)/shard_map/reduce_scatter | solution.py:324
  1308.6 571.9 %reduce-scatter.26.cloned.1.call-start = ((), (), s32[]{:S(2)}) async-start(), calls=%async_computation.20 | async-start | bytes 9732096 | tf_op jit(solution)/shard_map/reduce_scatter | solution.py:326
  1318.7 703.3 %reduce-scatter.24.cloned.1.call-start = ((), (), s32[]{:S(2)}) async-start(), calls=%async_computation.19 | async-start | bytes 9732096 | tf_op jit(solution)/shard_map/reduce_scatter | solution.py:325
  (676 other events, 5246.8 us)
Sparse Core Ops, SparseCore 0:
  15.0 40.9 all-gather.21
  58.2 37.3 all-gather.19
  97.4 29.7 all-gather.11
  128.9 30.8 all-gather.13
  320.4 37.1 all-gather.9
  359.3 29.5 all-gather.15
  391.1 38.2 all-gather.17
  443.1 39.2 reduce-scatter.19
  484.7 39.7 reduce-scatter.17
  1263.0 48.3 reduce-scatter.35
  1313.6 39.7 reduce-scatter.33
  1356.3 30.3 reduce-scatter.37
  1389.6 31.1 reduce-scatter.29
  1423.6 31.1 reduce-scatter.31
  1461.1 136.2 reduce-scatter.27
  1603.7 135.1 reduce-scatter.21
  1745.3 135.1 reduce-scatter.25
  1886.8 135.1 reduce-scatter.23
where the time goes:
time: 2040 us; the launch traced here: 2030 us
  waiting for transfers between devices  871 us (43%)
  other arithmetic  634 us (31%)
  local copies, waits for them, and re-layouts  262 us (13%)
  matrix products  115 us (6%)
  loops' own time  78.4 us (4%)
  blocking collectives  40.3 us (2%)
    reduce_sum x8, other arithmetic, backward_group(): inner = jnp.sum(grad_probs * probs, axis=-1, keepdims=True)  160 us
    reduce_sum x32, other arithmetic, tap_grads(): entries.append(jnp.sum(grad_conv * piece, axis=(0, 2, 3)))  157 us
    convert_element_type x8, other arithmetic, backward_group(): jnp.where(own_mask[:, None], grad_masked, 0.0).astype(jnp.bfloat16)  147 us
    reduce_scatter x1, waiting for transfers between devices, shards(): lax.psum_scatter(grad_query_w, ('row', 'seq'), scatter_dimension=0, tiled...  142 us
    reduce_scatter x1, waiting for transfers between devices, shards(): lax.psum_scatter(grad_key_w, ('row', 'seq'), scatter_dimension=0, tiled=T...  142 us
    reduce_scatter x1, waiting for transfers between devices, shards(): lax.psum_scatter(grad_value_w, ('row', 'seq'), scatter_dimension=0, tiled...  142 us
    reduce_max x8, other arithmetic, forward_group(): highest = jnp.max(logits, axis=-1, keepdims=True)  140 us
    reduce_scatter x1, waiting for transfers between devices, shards(): lax.psum_scatter(grad_out_part, ('row', 'seq'), scatter_dimension=0, tile...  84.6 us
  transfers between devices with their start and end apart: 27, of which 17 were waited for; matrix products, arithmetic and copies ran while one was open for 24% of the time, Pallas kernels for 0%

commit v1 on v0

v1 whole, which is shorter than its diff:
```python
import jax
import jax.numpy as jnp
from jax import lax
from jax.sharding import PartitionSpec as P

HEADS = 16
HD = 96
QCONV = 6
KCONV = 11
PAD = 8

epsilon = 1e-06


def rms_scale(values):
    return lax.rsqrt(jnp.mean(values * values, axis=-1, keepdims=True) + epsilon)


def project(values, weight):
    return jnp.dot(values, weight, preferred_element_type=jnp.float32)


def contract_rows(left, right):
    return lax.dot_general(
        left, right, (((0,), (0,)), ((), ())), preferred_element_type=jnp.float32
    )


def contract_cols(left, right):
    return lax.dot_general(
        left, right, (((1,), (1,)), ((), ())), preferred_element_type=jnp.float32
    )


def mix_heads(probs, mixing):
    return mixing[:, 0][:, None, None] * probs[0:1] + mixing[:, 1][:, None, None] * probs[1:2]


def mix_back(grads, mixing):
    return mixing[0, :][:, None, None] * grads[0:1] + mixing[1, :][:, None, None] * grads[1:2]


def shards(
    inputs,
    doc_ids,
    w_query,
    w_key,
    w_value,
    w_out,
    gain_attn,
    gain_ffn,
    conv_taps,
    head_mix,
    w_gate,
    w_up,
    w_down,
    cotangent,
):
    row_dev, blk, width = inputs.shape
    assert row_dev == 1
    seq_count = lax.axis_size("seq")
    row_count = lax.axis_size("row")
    seq_index = lax.axis_index("seq")
    row_index = lax.axis_index("row")
    length = blk * seq_count
    groups = HEADS // 2
    assert seq_count % groups == 0
    splits = seq_count // groups
    span = length // splits
    pw = 2 * HD
    ext = span + 2 * PAD
    xrows = span + PAD
    score_scale = HD ** (-0.5)
    pair = seq_index // splits
    part = seq_index % splits
    q0 = part * span

    flat_in = inputs.reshape(blk, width)
    scale_one = rms_scale(flat_in)
    normed = (flat_in * scale_one * gain_attn).astype(jnp.bfloat16)
    normed_all = lax.all_gather(normed, "seq", axis=0, tiled=True)

    wq_g = lax.dynamic_slice_in_dim(w_query, pair * pw, pw, 1)
    wk_g = lax.dynamic_slice_in_dim(w_key, pair * pw, pw, 1)
    wv_g = lax.dynamic_slice_in_dim(w_value, pair * pw, pw, 1)
    wo_g = lax.dynamic_slice_in_dim(w_out, pair * pw, pw, 0)
    taps = lax.dynamic_slice_in_dim(conv_taps, pair * 2, 2, 0)
    mixing = lax.dynamic_index_in_dim(head_mix, pair, 0, keepdims=False)

    normed_pad = jnp.pad(normed_all, ((PAD, PAD), (0, 0)))
    q_ext = project(lax.dynamic_slice_in_dim(normed_pad, q0, ext, 0), wq_g).astype(jnp.bfloat16)
    k_all = project(normed_all, wk_g).astype(jnp.bfloat16)
    v_all = project(normed_all, wv_g).astype(jnp.bfloat16)
    q3 = q_ext.reshape(ext, 2, HD)
    k3 = k_all.reshape(length, 2, HD)
    v3 = v_all.reshape(length, 2, HD)

    docs = doc_ids[0]
    docs_pad = jnp.pad(docs, (PAD, PAD), constant_values=-1)
    ext_docs = lax.dynamic_slice_in_dim(docs_pad, q0, ext, 0)
    ext_pos = q0 - PAD + jnp.arange(ext, dtype=jnp.int32)
    key_pos = jnp.arange(length, dtype=jnp.int32)
    mask_e = (key_pos[None, :] <= ext_pos[:, None]) & (ext_docs[:, None] == docs[None, :])

    scores = jnp.einsum("ihd,jhd->hij", q3, k3, preferred_element_type=jnp.float32) * score_scale
    masked = jnp.where(mask_e[None], scores, 0.0)
    mp = jnp.pad(masked, ((0, 0), (0, 0), (KCONV - 1, 0)))
    conv_x = jnp.zeros((2, xrows, length), jnp.float32)
    for a in range(QCONV):
        for b in range(KCONV):
            weight = taps[:, a, b][:, None, None]
            conv_x = conv_x + weight * mp[:, PAD - a : PAD - a + xrows, KCONV - 1 - b : KCONV - 1 - b + length]
    mask_x = mask_e[PAD : PAD + xrows]
    logits = jnp.where(mask_x[None], conv_x, -jnp.inf)
    highest = jnp.max(logits, axis=-1, keepdims=True)
    highest = jnp.where(highest > -jnp.inf, highest, 0.0)
    expd = jnp.exp(logits - highest)
    denom = jnp.sum(expd, axis=-1, keepdims=True)
    probs_x = expd / jnp.where(denom > 0, denom, 1.0)
    mixed_own = mix_heads(probs_x[:, :span], mixing).astype(jnp.bfloat16)
    heads_own = (
        jnp.einsum("hij,jhd->ihd", mixed_own, v3, preferred_element_type=jnp.float32)
        .astype(jnp.bfloat16)
        .reshape(span, pw)
    )

    def to_tokens(values):
        cols = values.shape[1]
        if splits == 1:
            full = values
        else:
            full = lax.dynamic_update_slice_in_dim(
                jnp.zeros((length, cols), values.dtype), values, q0, 0
            )
        got = lax.all_to_all(full, "seq", 0, 0, tiled=True)
        got = got.reshape(groups, splits, blk, cols)
        if splits > 1:
            got = jnp.sum(got.astype(jnp.float32), axis=1).astype(values.dtype)
        else:
            got = got[:, 0]
        return got

    heads_tok = jnp.transpose(to_tokens(heads_own), (1, 0, 2)).reshape(blk, width)
    middle = flat_in + project(heads_tok, w_out)
    scale_two = rms_scale(middle)
    normed_ffn = (middle * scale_two * gain_ffn).astype(jnp.bfloat16)
    gate_full, up_full, down_full = (
        lax.all_gather(w_gate, "row", axis=0, tiled=True),
        lax.all_gather(w_up, "row", axis=0, tiled=True),
        lax.all_gather(w_down, "row", axis=1, tiled=True),
    )
    hid_width = gate_full.shape[1]
    joint = jnp.concatenate([gate_full, up_full], axis=1)
    ffn_rows = lax.all_gather(normed_ffn, "seq", axis=0, tiled=True)
    gate_up = project(ffn_rows, joint)
    gate_vals = gate_up[:, :hid_width]
    up_vals = gate_up[:, hid_width:]
    hidden = (jax.nn.silu(gate_vals) * up_vals).astype(jnp.bfloat16)
    ffn_out = lax.psum_scatter(
        project(hidden, down_full).astype(jnp.bfloat16), "seq", scatter_dimension=0, tiled=True
    ).astype(jnp.float32)
    outputs = middle + ffn_out
    cot_flat = cotangent.reshape(blk, width)
    cot_low = cot_flat.astype(jnp.bfloat16)
    cot_rows = lax.all_gather(cot_low, "seq", axis=0, tiled=True)
    grad_hidden = contract_cols(cot_rows, down_full)
    grad_down_part = contract_rows(hidden, cot_rows)
    sigmoid_gate = jax.nn.sigmoid(gate_vals)
    grad_gate_vals = grad_hidden * up_vals * sigmoid_gate * (1.0 + gate_vals * (1.0 - sigmoid_gate))
    grad_up_vals = grad_hidden * gate_vals * sigmoid_gate
    grad_joint = jnp.concatenate([grad_gate_vals, grad_up_vals], axis=1).astype(jnp.bfloat16)
    grad_joint_w = contract_rows(ffn_rows, grad_joint)
    grad_normed_ffn = lax.psum_scatter(
        contract_cols(grad_joint, joint).astype(jnp.bfloat16),
        "seq",
        scatter_dimension=0,
        tiled=True,
    ).astype(jnp.float32)
    grad_w_gate, grad_w_up, grad_w_down = (
        lax.psum_scatter(
            grad_joint_w[:, :hid_width].astype(jnp.bfloat16), "row", scatter_dimension=0, tiled=True
        ).astype(jnp.float32),
        lax.psum_scatter(
            grad_joint_w[:, hid_width:].astype(jnp.bfloat16), "row", scatter_dimension=0, tiled=True
        ).astype(jnp.float32),
        lax.psum_scatter(
            grad_down_part.astype(jnp.bfloat16), "row", scatter_dimension=1, tiled=True
        ).astype(jnp.float32),
    )
    gain_ffn_part = jnp.sum(grad_normed_ffn * middle * scale_two, axis=0)
    scaled_two = grad_normed_ffn * gain_ffn
    grad_middle = (
        cot_flat
        + scale_two * scaled_two
        - middle * scale_two**3 * jnp.mean(scaled_two * middle, axis=-1, keepdims=True)
    )
    grad_attn = grad_middle.astype(jnp.bfloat16)
    grad_attn_all = lax.all_gather(grad_attn, "seq", axis=0, tiled=True)
    grad_attn_pad = jnp.pad(grad_attn_all, ((0, PAD), (0, 0)))
    grad_heads_x = contract_cols(
        lax.dynamic_slice_in_dim(grad_attn_pad, q0, xrows, 0), wo_g
    ).astype(jnp.bfloat16)
    gh3 = grad_heads_x.reshape(xrows, 2, HD)
    grad_out_part = contract_rows(heads_own, lax.dynamic_slice_in_dim(grad_attn_all, q0, span, 0))

    grad_mixed = jnp.einsum("ihd,jhd->hij", gh3, v3, preferred_element_type=jnp.float32)
    grad_v_part = jnp.einsum(
        "hij,ihd->jhd", mixed_own, gh3[:span], preferred_element_type=jnp.float32
    ).reshape(length, pw)
    grad_mix_part = jnp.stack(
        [
            jnp.sum(grad_mixed[:, :span] * probs_x[0:1, :span], axis=(1, 2)),
            jnp.sum(grad_mixed[:, :span] * probs_x[1:2, :span], axis=(1, 2)),
        ],
        axis=1,
    )
    grad_probs = mix_back(grad_mixed, mixing)
    inner = jnp.sum(grad_probs * probs_x, axis=-1, keepdims=True)
    grad_conv = probs_x * (grad_probs - inner)
    tap_entries = []
    for a in range(QCONV):
        for b in range(KCONV):
            piece = mp[:, PAD - a : PAD - a + span, KCONV - 1 - b : KCONV - 1 - b + length]
            tap_entries.append(jnp.sum(grad_conv[:, :span] * piece, axis=(1, 2)))
    grad_taps_part = jnp.stack(tap_entries, axis=1).reshape(2, QCONV, KCONV)
    gc_pad = jnp.pad(grad_conv, ((0, 0), (0, 0), (0, KCONV - 1)))
    grad_masked = jnp.zeros((2, span, length), jnp.float32)
    for a in range(QCONV):
        for b in range(KCONV):
            weight = taps[:, a, b][:, None, None]
            grad_masked = grad_masked + weight * gc_pad[:, a : a + span, b : b + length]
    grad_scores = jnp.where(mask_e[None, PAD : PAD + span], grad_masked, 0.0).astype(jnp.bfloat16)
    grad_q_own = (
        jnp.einsum("hij,jhd->ihd", grad_scores, k3, preferred_element_type=jnp.float32) * score_scale
    ).astype(jnp.bfloat16).reshape(span, pw)
    grad_k_part = (
        jnp.einsum("hij,ihd->jhd", grad_scores, q3[PAD : PAD + span], preferred_element_type=jnp.float32)
        * score_scale
    ).reshape(length, pw)

    def split_sum(values):
        if splits == 1:
            return values
        total = values
        for step in range(1, splits):
            route = []
            for s in range(seq_count):
                base = (s // splits) * splits
                route.append((s, base + (s - base + step) % splits))
            total = total + lax.ppermute(values, "seq", route)
        return total

    grad_k_low = split_sum(grad_k_part).astype(jnp.bfloat16)
    grad_v_low = split_sum(grad_v_part).astype(jnp.bfloat16)
    grad_k_own = lax.dynamic_slice_in_dim(grad_k_low, q0, span, 0)
    grad_v_own = lax.dynamic_slice_in_dim(grad_v_low, q0, span, 0)

    normed_own = lax.dynamic_slice_in_dim(normed_all, q0, span, 0)
    rows_per_dev = width // (row_count * seq_count)

    def finish_in(partial):
        red = lax.psum_scatter(partial, "row", scatter_dimension=0, tiled=True)
        got = lax.all_to_all(red, "seq", 0, 0, tiled=True)
        got = got.reshape(groups, splits, rows_per_dev, pw).sum(axis=1)
        return jnp.transpose(got, (1, 0, 2)).reshape(rows_per_dev, width)

    grad_w_query = finish_in(contract_rows(normed_own, grad_q_own))
    grad_w_key = finish_in(contract_rows(normed_own, grad_k_own))
    grad_w_value = finish_in(contract_rows(normed_own, grad_v_own))

    red_out = lax.psum_scatter(grad_out_part, "row", scatter_dimension=0, tiled=True)
    red_out = red_out.reshape(splits, rows_per_dev, width)
    grad_w_out = jnp.zeros((rows_per_dev, width), jnp.float32)
    for src_part in range(splits):
        for j in range(splits):
            route = []
            for r in range(row_count):
                for g in range(groups):
                    src = r * seq_count + g * splits + src_part
                    dst = g * row_count * splits + r * splits + j
                    route.append((src, dst))
            grad_w_out = grad_w_out + lax.ppermute(red_out[j], ("row", "seq"), route)

    grad_tok = to_tokens(jnp.concatenate([grad_q_own, grad_k_own, grad_v_own], axis=1))
    grad_tok = grad_tok.reshape(groups, blk, 3, pw)
    gq_tok = jnp.transpose(grad_tok[:, :, 0], (1, 0, 2)).reshape(blk, width)
    gk_tok = jnp.transpose(grad_tok[:, :, 1], (1, 0, 2)).reshape(blk, width)
    gv_tok = jnp.transpose(grad_tok[:, :, 2], (1, 0, 2)).reshape(blk, width)
    grad_normed = (
        contract_cols(gq_tok, w_query) + contract_cols(gk_tok, w_key) + contract_cols(gv_tok, w_value)
    )
    gain_attn_part = jnp.sum(grad_normed * flat_in * scale_one, axis=0)
    scaled_one = grad_normed * gain_attn
    grad_inputs = (
        grad_middle
        + scale_one * scaled_one
        - flat_in * scale_one**3 * jnp.mean(scaled_one * flat_in, axis=-1, keepdims=True)
    )
    grad_gain_attn, grad_gain_ffn = (
        lax.psum_scatter(gain_attn_part, ("row", "seq"), scatter_dimension=0, tiled=True),
        lax.psum_scatter(gain_ffn_part, ("row", "seq"), scatter_dimension=0, tiled=True),
    )
    taps_full = lax.dynamic_update_slice_in_dim(
        jnp.zeros((HEADS, QCONV, KCONV), jnp.float32), grad_taps_part, pair * 2, 0
    )
    mix_full = lax.dynamic_update_slice_in_dim(
        jnp.zeros((groups, 2, 2), jnp.float32), grad_mix_part[None], pair, 0
    )
    grad_taps, grad_mix = lax.psum((taps_full, mix_full), ("row", "seq"))
    return (
        outputs.reshape(row_dev, blk, width),
        grad_inputs.reshape(row_dev, blk, width),
        grad_w_query,
        grad_w_key,
        grad_w_value,
        grad_w_out,
        grad_gain_attn,
        grad_gain_ffn,
        grad_taps,
        grad_mix,
        grad_w_gate,
        grad_w_up,
        grad_w_down,
    )


def solution(mesh):
    return jax.shard_map(
        shards,
        mesh=mesh,
        in_specs=(
            P("row", "seq", None),
            P("row", None),
            P(),
            P(),
            P(),
            P(),
            P(),
            P(),
            P(),
            P(),
            P("row", "seq"),
            P("row", "seq"),
            P("seq", "row"),
            P("row", "seq", None),
        ),
        out_specs=(
            P("row", "seq", None),
            P("row", "seq", None),
            P(("row", "seq"), None),
            P(("row", "seq"), None),
            P(("row", "seq"), None),
            P(("row", "seq"), None),
            P(("row", "seq")),
            P(("row", "seq")),
            P(),
            P(),
            P("row", "seq"),
            P("row", "seq"),
            P("seq", "row"),
        ),
        check_vma=False,
    )
```

time: 2040 us -> 1760 us (0.86)
  waiting for transfers between devices: 871 us -> 326 us
  other arithmetic: 634 us -> 1170 us
  local copies, waits for them, and re-layouts: 262 us -> 58.3 us
  loops' own time: 78.4 us -> 0 us
    reduce_scatter x4, waiting for transfers between devices: 509 us -> 0.04 us  [the longest x3 0.04 us: finish_in(): red = lax.psum_scatter(partial, 'row', scatter_dimension=0, tiled=True)]
    reduce_max x8 -> x1, other arithmetic: 140 us -> 411 us  [shards(): highest = jnp.max(logits, axis=-1, keepdims=True)]
    convert_element_type x16 -> x3, other arithmetic: 147 us -> 390 us  [the longest x1 386 us: shards(): jnp.where(mask_e[None, PAD:PAD + span], grad_masked, 0.0)]
    another operation x2 -> x0, loops' own time: 78.4 us -> none  [the longest x1 51.8 us: shards(): lax.scan(backward_group, start_bufs, jnp.arange(groups))]
    dynamic_slice x81 -> x1, local copies, waits for them, and re-layouts: 52.1 us -> 0.84 us  [shards(): mixing = lax.dynamic_index_in_dim(head_mix, pair, 0, keepdims=False)]
    unnamed x69 -> x236, local copies, waits for them, and re-layouts: 66.2 us -> 15 us
    another operation x564 -> x67, local copies, waits for them, and re-layouts: 58.9 us -> 10.8 us  [shards(): grad_taps_part = jnp.stack(tap_entries, axis=1).reshape(2, QCONV, KCONV)]
    unnamed x21 -> x17, waiting for transfers between devices: 65.4 us -> 31.3 us
  transfers between devices with their start and end apart: 27 -> 21, of which waited for: 17 -> 12; matrix products, arithmetic and copies ran while one was open for 24% -> 65% of each run, Pallas kernels for 0% -> 0%
where the time goes in v1:
time: 1760 us; the launch traced here: 1750 us
  other arithmetic  1170 us (66%)
  waiting for transfers between devices  326 us (19%)
  matrix products  95.8 us (5%)
  local copies, waits for them, and re-layouts  58.3 us (3%)
  blocking collectives  57.1 us (3%)
  starting transfers between devices  24.5 us (1%)
    reduce_max x1, other arithmetic, shards(): highest = jnp.max(logits, axis=-1, keepdims=True)  411 us
    convert_element_type x1, other arithmetic, shards(): jnp.where(mask_e[None, PAD:PAD + span], grad_masked, 0.0)  386 us
    reduce_sum x7, other arithmetic, shards(): tap_entries.append(jnp.sum(grad_conv[:, :span] * piece, axis=(1, 2)))  332 us
    unnamed x1, blocking collectives  41.8 us
    reduce_scatter x1, waiting for transfers between devices, shards(): lax.psum_scatter(project(hidden, down_full).astype(jnp.bfloat16), 'seq',...  40.7 us
    all_gather x1, waiting for transfers between devices, shards(): cot_rows = lax.all_gather(cot_low, 'seq', axis=0, tiled=True)  40.3 us
    all_gather x1, waiting for transfers between devices, shards(): grad_attn_all = lax.all_gather(grad_attn, 'seq', axis=0, tiled=True)  37.8 us
  transfers between devices with their start and end apart: 21, of which 12 were waited for; matrix products, arithmetic and copies ran while one was open for 65% of the time, Pallas kernels for 0%

profile of v1, /device:TPU:0, one launch (start us, length us, event | category | flops | bytes accessed | tf_op | source)
XLA Modules:
  0.0 1749.8 jit_solution(17493991479786910086)
XLA Ops:
  20.4 32.2 %all-gather.8.cloned.1.call-done = bf16[1024,1536]{1,0:T(8,128)(2,1)} async-done(((bf16[128,1536]{1,0:T(8,128)(2,1)}), bf16[1024,1536]{1,0:T(8,128)(2,1)}) %all-gather.8.cloned.1.call-update) | async-done | bytes 3145744 | tf_op jit(solution)/shard_map/all_gather | solution.py:81
  65.4 410.7 %fusion.247 = (f32[2,1032]{1,0:T(2,128)S(1)}, f32[2,1032,1024]{2,1,0:T(8,128)}) fusion(f32[2]{0:T(128)} %get-tuple-element.178, f32[2]{0:T(128)S(1)} %get-tuple-element.114, f32[2]{0:T(128)S(1)} %get-tuple-element.115, f32[2]{0:T(128)S(1)} %get-tuple-element.116, f32[2]{0:T(128)S(1)} %get-tuple-element.117, f32[2]{0:T(128)S(1)} %get-tuple-element.118, ...), kind=kLoop, calls=%fused_computation.475 | loop fusion | flops 281098240 | bytes 68778352 | tf_op jit(solution)/shard_map/reduce_max | solution.py:115
  492.8 15.3 all_to_all.42
  517.1 30.2 %all-gather.10.cloned.1.call-done = bf16[1024,1536]{1,0:T(8,128)(2,1)} async-done(((bf16[128,1536]{1,0:T(8,128)(2,1)}), bf16[1024,1536]{1,0:T(8,128)(2,1)}) %all-gather.10.cloned.1.call-update) | async-done | bytes 3145744 | tf_op jit(solution)/shard_map/all_gather | solution.py:154
  547.3 8.3 fusion.251
  555.5 23.0 %all-gather.16.cloned.1.call-done = bf16[512,1536]{1,0:T(8,128)(2,1)} async-done(((bf16[512,384]{1,0:T(8,128)(2,1)}), bf16[512,1536]{1,0:T(8,128)(2,1)}) %all-gather.16.cloned.1.call-update) | async-done | bytes 1572880 | tf_op jit(solution)/shard_map/all_gather | solution.py:150
  578.6 40.3 %all-gather.18.cloned.1.call-done = bf16[1024,1536]{1,0:T(8,128)(2,1)} async-done(((bf16[128,1536]{1,0:T(8,128)(2,1)}), bf16[1024,1536]{1,0:T(8,128)(2,1)}) %all-gather.18.cloned.1.call-update) | async-done | bytes 3145744 | tf_op jit(solution)/shard_map/all_gather | solution.py:165
  618.9 7.3 multiply_convert_fusion.1
  654.8 17.2 reduce-scatter.14.cloned.1.call-done
  673.3 40.7 %reduce-scatter.12.cloned.1.call-done = bf16[128,1536]{1,0:T(8,128)(2,1)} async-done(((bf16[1024,1536]{1,0:T(8,128)(2,1)}), bf16[128,1536]{1,0:T(8,128)(2,1)}) %reduce-scatter.12.cloned.1.call-update) | async-done | bytes 393232 | tf_op jit(solution)/shard_map/reduce_scatter | solution.py:159
  719.0 28.5 %reduce-scatter.28.cloned.1.call-done = bf16[384,512]{1,0:T(8,128)(2,1)} async-done(((bf16[1536,512]{1,0:T(8,128)(2,1)}), bf16[384,512]{1,0:T(8,128)(2,1)}) %reduce-scatter.28.cloned.1.call-update) | async-done | bytes 393232
  749.7 31.9 %reduce-scatter.24.cloned.1.call-done = bf16[384,512]{1,0:T(8,128)(2,1)} async-done(((bf16[1536,512]{1,0:T(8,128)(2,1)}), bf16[384,512]{1,0:T(8,128)(2,1)}) %reduce-scatter.24.cloned.1.call-update) | async-done | bytes 393232 | tf_op jit(solution)/shard_map/reduce_scatter | solution.py:180
  783.5 32.2 %reduce-scatter.26.cloned.1.call-done = bf16[384,512]{1,0:T(8,128)(2,1)} async-done(((bf16[1536,512]{1,0:T(8,128)(2,1)}), bf16[384,512]{1,0:T(8,128)(2,1)}) %reduce-scatter.26.cloned.1.call-update) | async-done | bytes 393232 | tf_op jit(solution)/shard_map/reduce_scatter | solution.py:183
  817.7 37.8 %all-gather.20.cloned.1.call-done = bf16[1024,1536]{1,0:T(8,128)(2,1)} async-done(((bf16[128,1536]{1,0:T(8,128)(2,1)}), bf16[1024,1536]{1,0:T(8,128)(2,1)}) %all-gather.20.cloned.1.call-update) | async-done | bytes 3145744 | tf_op jit(solution)/shard_map/all_gather | solution.py:198
  876.6 47.7 %multiply_reduce_fusion.7 = (f32[2]{0:T(128)}, f32[2]{0:T(128)}, f32[2]{0:T(128)}, f32[2]{0:T(128)}, f32[2]{0:T(128)}, /*index=5*/f32[2]{0:T(128)}, f32[2]{0:T(128)}, f32[2]{0:T(128)}, f32[2]{0:T(128)}) fusion(f32[2,1040,1024]{2,1,0:T(8,128)} %multiply_select_fusion, f32[2,1032,1024]{2,1,0:T(8,128)} %subtract_multiply_fusion), kind=kLoop, calls=%fused_computation.156 | loop fusion | flops 37748720 | bytes 16908360 | tf_op jit(solution)/shard_map/reduce_sum | solution.py:224
  924.4 38.5 %multiply_reduce_fusion.9 = (f32[2]{0:T(128)}, f32[2]{0:T(128)}, f32[2]{0:T(128)}, f32[2]{0:T(128)}, f32[2]{0:T(128)}, /*index=5*/f32[2]{0:T(128)}, f32[2]{0:T(128)}, f32[2]{0:T(128)}, f32[2]{0:T(128)}) fusion(f32[2,1040,1024]{2,1,0:T(8,128)} %multiply_select_fusion, f32[2,1032,1024]{2,1,0:T(8,128)} %subtract_multiply_fusion), kind=kLoop, calls=%fused_computation.158 | loop fusion | flops 37748720 | bytes 50462792 | tf_op jit(solution)/shard_map/reduce_sum | solution.py:224
  962.9 59.0 %multiply_reduce_fusion.8 = (f32[2]{0:T(128)}, f32[2]{0:T(128)}, f32[2]{0:T(128)}, f32[2]{0:T(128)}, f32[2]{0:T(128)}, /*index=5*/f32[2]{0:T(128)}, f32[2]{0:T(1...) fusion(f32[2,1040,1024]{2,1,0:T(8,128)} %multiply_select_fusion, ...), kind=kLoop, calls=%fused_computation.157 | loop fusion | flops 50331632 | bytes 33685600 | tf_op jit(solution)/shard_map/reduce_sum | solution.py:224
  1029.6 385.7 %fusion.170 = bf16[2,1024,1024]{2,1,0:T(8,128)(2,1)} fusion(f32[2,1032,1024]{2,1,0:T(8,128)} %subtract_multiply_fusion, f32[2]{0:T(128)} %get-tuple-element.178, f32[2]{0:T(128)S(1)} %copy-done.30, f32[2]{0:T(128)} %copy-done.31, f32[2]{0:T(128)} %copy-done.32, f32[2]{0:T(128)} %copy-done.33, f32[2]{0:T(128)} %copy-done.34, f32[2]{0:T(128)} %copy-done.35, ...), kind=kLoop, calls=%fused_computation.287 | loop fusion | flops 278921216 | bytes 64061456 | tf_op jit(solution)/shard_map/convert_element_type | solution.py:232
  1429.8 48.2 %multiply_reduce_fusion.6 = (f32[2]{0:T(128)}, f32[2]{0:T(128)}, f32[2]{0:T(128)}, f32[2]{0:T(128)}, f32[2]{0:T(128)}, /*index=5*/f32[2]{0:T(128)}, f32[2]{0:T(128)}, f32[2]{0:T(128)S(1)}, f32[2]{0:T(128)S(1)}) fusion(f32[2,1040,1024]{2,1,0:T(8,128)} %multiply_select_fusion, f32[2,1032,1024]{2,1,0:T(8,128)} %subtract_multiply_fusion), kind=kLoop, calls=%fused_computation.155 | loop fusion | flops 37748720 | bytes 16908360 | tf_op jit(solution)/shard_map/reduce_sum | solution.py:224
  1481.8 47.8 %multiply_reduce_fusion.5 = (f32[2]{0:T(128)}, f32[2]{0:T(128)}, f32[2]{0:T(128)}, f32[2]{0:T(128)}, f32[2]{0:T(128)}, /*index=5*/f32[2]{0:T(128)}, f32[2]{0:T(128)}, f32[2]{0:T(128)}, f32[2]{0:T(128)}) fusion(f32[2,1040,1024]{2,1,0:T(8,128)} %multiply_select_fusion, f32[2,1032,1024]{2,1,0:T(8,128)} %subtract_multiply_fusion), kind=kLoop, calls=%fused_computation.154 | loop fusion | flops 37748720 | bytes 16908360 | tf_op jit(solution)/shard_map/reduce_sum | solution.py:224
  1531.4 47.4 %multiply_reduce_fusion.4 = (f32[2]{0:T(128)S(1)}, f32[2]{0:T(128)S(1)}, f32[2]{0:T(128)S(1)}, f32[2]{0:T(128)S(1)}, f32[2]{0:T(128)S(1)}, /*index=5*/f32[2]{0:T...) fusion(f32[2,1040,1024]{2,1,0:T(8,128)} %multiply_select_fusion, f32[2,1032,1024]{2,1,0:T(8,128)} %subtract_multiply_fusion), kind=kLoop, calls=%fused_computation.153 | loop fusion | flops 37748720 | bytes 16908360 | tf_op jit(solution)/shard_map/reduce_sum | solution.py:224
  1578.8 43.5 %multiply_reduce_fusion.3 = (f32[2]{0:T(128)S(1)}, f32[2]{0:T(128)S(1)}, f32[2]{0:T(128)S(1)}, f32[2]{0:T(128)S(1)}, f32[2]{0:T(128)S(1)}, /*index=5*/f32[2]{0:T...) fusion(f32[2,1040,1024]{2,1,0:T(8,128)} %multiply_select_fusion, f32[2,1032,1024]{2,1,0:T(8,128)} %subtract_multiply_fusion), kind=kLoop, calls=%fused_computation.152 | loop fusion | flops 37748720 | bytes 16908360 | tf_op jit(solution)/shard_map/reduce_sum | solution.py:224
  1674.3 41.8 %all-reduce.7 = (f32[1536]{0:T(1024)S(1)}, f32[1536]{0:T(1024)S(1)}, f32[16,6,11]{0,1,2:T(8,128)}, f32[8,2,2]{0,2,1:T(2,128)}) all-reduce(f32[1536]{0:T(1024)} %get-tuple-element.81, f32[1536]{0:T(1024)S(1)} %get-tuple-element.83, f32[16,6,11]{0,1,2:T(8,128)} %copy-done.22, ...), channel_id=8, replica_groups=mesh['row'=4,'seq'=8] {'row','seq'}, use_global_device_ids=true, to_apply=%region_14.15.clone | all-reduce | flops 4160 | bytes 33280
  1721.4 7.1 all-to-all-start.2
  (433 shorter events, 211.6 us)
Async XLA Ops:
  7.2 45.5 %all-gather.8.cloned.1.call-start = ((), (), s32[]{:S(2)}) async-start(), calls=%async_computation.14 | async-start | bytes 3538944 | tf_op jit(solution)/shard_map/all_gather | solution.py:81
  11.6 500.0 %all-gather.12.cloned.1.call-start = ((), (), s32[]{:S(2)}) async-start(), calls=%async_computation.16 | async-start | bytes 1966080 | tf_op jit(solution)/shard_map/all_gather | solution.py:148
  12.3 501.9 %all-gather.14.cloned.1.call-start = ((), (), s32[]{:S(2)}) async-start(), calls=%async_computation.17 | async-start | bytes 1966080 | tf_op jit(solution)/shard_map/all_gather | solution.py:149
  13.1 534.2 %all-gather.10.cloned.1.call-start = ((), (), s32[]{:S(2)}) async-start(), calls=%async_computation.15 | async-start | bytes 3538944 | tf_op jit(solution)/shard_map/all_gather | solution.py:154
  510.0 68.6 %all-gather.16.cloned.1.call-start = ((), (), s32[]{:S(2)}) async-start(), calls=%async_computation.18 | async-start | bytes 1966080 | tf_op jit(solution)/shard_map/all_gather | solution.py:150
  510.6 108.3 %all-gather.18.cloned.1.call-start = ((), (), s32[]{:S(2)}) async-start(), calls=%async_computation.20 | async-start | bytes 3538944 | tf_op jit(solution)/shard_map/all_gather | solution.py:165
  511.5 160.5 %reduce-scatter.14.cloned.1.call-start = ((), (), s32[]{:S(2)}) async-start(), calls=%async_computation.21 | async-start | bytes 3538944 | tf_op jit(solution)/shard_map/reduce_scatter | solution.py:173
  632.6 81.4 %reduce-scatter.12.cloned.1.call-start = ((), (), s32[]{:S(2)}) async-start(), calls=%async_computation.19 | async-start | bytes 3538944 | tf_op jit(solution)/shard_map/reduce_scatter | solution.py:159
  637.9 109.6 %reduce-scatter.28.cloned.1.call-start = ((), (), s32[]{:S(2)}) async-start(), calls=%async_computation.29 | async-start | bytes 1966080
  645.8 135.7 %reduce-scatter.24.cloned.1.call-start = ((), (), s32[]{:S(2)}) async-start(), calls=%async_computation.27 | async-start | bytes 1966080 | tf_op jit(solution)/shard_map/reduce_scatter | solution.py:180
  654.0 161.7 %reduce-scatter.26.cloned.1.call-start = ((), (), s32[]{:S(2)}) async-start(), calls=%async_computation.28 | async-start | bytes 1966080 | tf_op jit(solution)/shard_map/reduce_scatter | solution.py:183
  654.8 200.7 %all-gather.20.cloned.1.call-start = ((), (), s32[]{:S(2)}) async-start(), calls=%async_computation.22 | async-start | bytes 3538944 | tf_op jit(solution)/shard_map/all_gather | solution.py:198
  716.7 142.1 %copy-start.17 = (bf16[1024,192]{0,1:T(8,128)(2,1)S(1)}, bf16[1024,192]{0,1:T(8,128)(2,1)}, u32[]{:S(2)}) copy-start(bf16[1024,192]{0,1:T(8,128)(2,1)} %copy-done.16) | copy-start | bytes 1179652
  716.7 927.6 %reduce-scatter.20.cloned.1.call-start = ((), (), s32[]{:S(2)}) async-start(), calls=%async_computation.25 | async-start | bytes 1474560 | tf_op jit(solution)/shard_map/reduce_scatter | solution.py:262
  1029.6 385.8 %copy-start.19 = (bf16[1024,192]{0,1:T(8,128)(2,1)S(1)}, bf16[1024,192]{0,1:T(8,128)(2,1)}, u32[]{:S(2)}) copy-start(bf16[1024,192]{0,1:T(8,128)(2,1)} %copy-done.18) | copy-start | bytes 1179652
  1423.7 218.6 %all-to-all-start.1 = ((bf16[8,128,576]{1,2,0:T(8,128)(2,1)}), bf16[8,128,576]{1,2,0:T(8,128)(2,1)}, u32[]{:S(2)}, u32[]{:S(2)}) async-start(bf16[8,128,576]{1,2,0:T(8,128)(2,1)} %pad_maximum_fusion.3), calls=%async_computation.3 | async-start | bytes 2359296 | tf_op jit(solution)/shard_map/all_to_all | solution.py:135
  1428.0 233.0 %reduce-scatter.18.cloned.1.call-start = ((), (), s32[]{:S(2)}) async-start(), calls=%async_computation.24 | async-start | bytes 1474560 | tf_op jit(solution)/shard_map/reduce_scatter | solution.py:262
  1478.0 240.0 %reduce-scatter.22.cloned.1.call-start = ((), (), s32[]{:S(2)}) async-start(), calls=%async_computation.26 | async-start | bytes 1474560 | tf_op jit(solution)/shard_map/reduce_scatter | solution.py:271
  1529.6 190.0 %reduce-scatter.16.cloned.1.call-start = ((), (), s32[]{:S(2)}) async-start(), calls=%async_computation.23 | async-start | bytes 1474560 | tf_op jit(solution)/shard_map/reduce_scatter | solution.py:262
  1646.3 19.2 %all-to-all-start.4 = ((f32[8,48,192]{2,1,0:T(8,128)}), f32[8,48,192]{2,1,0:T(8,128)}, u32[]{:S(2)}, u32[]{:S(2)}) async-start(f32[8,48,192]{2,1,0:T(8,128)} %bitcast.104), calls=%async_computation.9 | async-start | bytes 786432 | tf_op jit(solution)/shard_map/all_to_all | solution.py:263
  1656.8 71.7 %copy-start.15 = (f32[128,1536]{1,0:T(8,128)S(1)}, f32[128,1536]{1,0:T(8,128)}, u32[]{:S(2)}) copy-start(f32[128,1536]{1,0:T(8,128)} %get-tuple-element.94) | copy-start | bytes 2359300
  1665.5 56.0 %all-to-all-start.3 = ((f32[8,48,192]{2,1,0:T(8,128)}), f32[8,48,192]{2,1,0:T(8,128)}, u32[]{:S(2)}, u32[]{:S(2)}) async-start(f32[8,48,192]{2,1,0:T(8,128)} %bitcast.101), calls=%async_computation.7 | async-start | bytes 786432 | tf_op jit(solution)/shard_map/all_to_all | solution.py:263
  1718.0 12.4 collective-permute-start
  1721.4 19.8 %all-to-all-start.2 = ((f32[8,48,192]{2,1,0:T(8,128)}), f32[8,48,192]{2,1,0:T(8,128)S(1)}, u32[]{:S(2)}, u32[]{:S(2)}) async-start(f32[8,48,192]{2,1,0:T(8,128)} %bitcast.98), calls=%async_computation.5 | async-start | bytes 786432 | tf_op jit(solution)/shard_map/all_to_all | solution.py:263
  (110 other events, 2631.3 us)
Sparse Core Ops, SparseCore 0:
  11.7 40.9 all-gather.7
  54.5 29.7 all-gather.11
  86.1 30.8 all-gather.13
  510.1 37.0 all-gather.9
  548.9 29.5 all-gather.15
  580.6 38.2 all-gather.17
  632.7 39.2 reduce-scatter.13
  674.3 39.6 reduce-scatter.11
  717.0 30.4 reduce-scatter.27
  750.3 31.1 reduce-scatter.23
  784.5 31.1 reduce-scatter.25
  817.2 38.2 all-gather.19
  1029.7 27.6 reduce-scatter.19
  1478.1 29.9 reduce-scatter.17
  1529.7 29.9 reduce-scatter.21
  1578.9 29.9 reduce-scatter.15

commit v2 on v1

--- a/solution.py
+++ b/solution.py
@@ -2,12 +2,18 @@
 import jax.numpy as jnp
 from jax import lax
 from jax.sharding import PartitionSpec as P
+from jax.experimental import pallas as pl
+from jax.experimental.pallas import tpu as pltpu
 
 HEADS = 16
 HD = 96
 QCONV = 6
 KCONV = 11
 PAD = 8
+TQ = 128
+EXT = TQ + PAD
+SCALE = HD ** (-0.5)
+TAPS = QCONV * KCONV
 
 epsilon = 1e-06
 
@@ -32,12 +38,283 @@
     )
 
 
-def mix_heads(probs, mixing):
-    return mixing[:, 0][:, None, None] * probs[0:1] + mixing[:, 1][:, None, None] * probs[1:2]
-
-
-def mix_back(grads, mixing):
-    return mixing[0, :][:, None, None] * grads[0:1] + mixing[1, :][:, None, None] * grads[1:2]
+def normed_pad_tail(values, extra):
+    return jnp.pad(values, ((PAD, TQ * extra), (0, 0)))
+
+
+def window_start(block, nw, length):
+    return pl.multiple_of(jnp.clip((block - nw + 1) * TQ, 0, length - nw * TQ), TQ)
+
+
+def tap_accumulate(sh_ref, acc_ref, taps_ref, head, width):
+    ncols = width // 128
+
+    def body(idx, carry):
+        r0 = pl.multiple_of((idx // ncols) * 8, 8)
+        c0 = pl.multiple_of((idx % ncols) * 128, 128)
+        tiles = [sh_ref[b, pl.ds(r0, 8), pl.ds(c0, 128)] for b in range(KCONV)]
+        for a in range(QCONV):
+            base = head * TAPS + a * KCONV
+            total = taps_ref[base] * tiles[0]
+            for b in range(1, KCONV):
+                total = total + taps_ref[base + b] * tiles[b]
+            acc_ref[a, pl.ds(r0, 8), pl.ds(c0, 128)] = total
+        return carry
+
+    lax.fori_loop(0, (EXT // 8) * ncols, body, 0)
+
+
+def tap_products(sh_ref, g_ref, width):
+    ncols = width // 128
+    sums = []
+    for b in range(KCONV):
+
+        def body(idx, accs):
+            r0 = pl.multiple_of((idx // ncols) * 8, 8)
+            c0 = pl.multiple_of((idx % ncols) * 128, 128)
+            tile = sh_ref[b, pl.ds(r0, 8), pl.ds(c0, 128)]
+            return tuple(
+                accs[a] + g_ref[a, pl.ds(r0, 8), pl.ds(c0, 128)] * tile for a in range(QCONV)
+            )
+
+        start = tuple(jnp.zeros((8, 128), jnp.float32) for _ in range(QCONV))
+        sums.append(lax.fori_loop(0, (EXT // 8) * ncols, body, start))
+    return sums
+
+
+def masks(block, kstart, width, rdoc_ref, kdoc_ref):
+    keydoc = kdoc_ref[:, pl.ds(kstart, width)]
+    ext_pos = block * TQ - PAD + lax.broadcasted_iota(jnp.int32, (EXT, width), 0)
+    key_ext = kstart + lax.broadcasted_iota(jnp.int32, (EXT, width), 1)
+    allowed_ext = (key_ext <= ext_pos) & (rdoc_ref[0] == keydoc)
+    own_pos = block * TQ + lax.broadcasted_iota(jnp.int32, (TQ, width), 0)
+    key_own = kstart + lax.broadcasted_iota(jnp.int32, (TQ, width), 1)
+    allowed_own = (key_own <= own_pos) & (rdoc_ref[0, PAD:, :] == keydoc)
+    return allowed_ext, allowed_own
+
+
+def masked_shifts(q_ref, k_ref, head, kstart, width, allowed_ext, sh_ref):
+    keys = k_ref[head, pl.ds(kstart, width), :]
+    scores = lax.dot_general(
+        q_ref[0, head], keys, (((1,), (1,)), ((), ())), preferred_element_type=jnp.float32
+    ) * SCALE
+    masked = jnp.where(allowed_ext, scores, 0.0)
+    col = lax.broadcasted_iota(jnp.int32, (EXT, width), 1)
+    sh_ref[0] = masked
+    for b in range(1, KCONV):
+        sh_ref[b] = jnp.where(col >= b, pltpu.roll(masked, b, 1), 0.0)
+
+
+def fwd_kernel(toff_ref, taps_ref, mix_ref, q_ref, k_ref, v_ref, rdoc_ref, kdoc_ref,
+               heads_ref, probs_ref, sh_ref, acc_ref, *, nw, length):
+    width = nw * TQ
+    block = toff_ref[0] + pl.program_id(0)
+    kstart = window_start(block, nw, length)
+    allowed_ext, allowed_own = masks(block, kstart, width, rdoc_ref, kdoc_ref)
+    for head in range(2):
+        masked_shifts(q_ref, k_ref, head, kstart, width, allowed_ext, sh_ref)
+        tap_accumulate(sh_ref, acc_ref, taps_ref, head, width)
+        conv = acc_ref[0]
+        for a in range(1, QCONV):
+            conv = conv + pltpu.roll(acc_ref[a], a, 0)
+        logits = jnp.where(allowed_own, conv[PAD:], -jnp.inf)
+        highest = jnp.max(logits, axis=1, keepdims=True)
+        highest = jnp.where(highest > -jnp.inf, highest, 0.0)
+        expd = jnp.exp(logits - highest)
+        denom = jnp.sum(expd, axis=1, keepdims=True)
+        probs_ref[0, head] = expd / jnp.where(denom > 0.0, denom, 1.0)
+    p0 = probs_ref[0, 0]
+    p1 = probs_ref[0, 1]
+    for c in range(2):
+        mixed = (mix_ref[2 * c] * p0 + mix_ref[2 * c + 1] * p1).astype(jnp.bfloat16)
+        heads_ref[0, c] = jnp.dot(
+            mixed, v_ref[c, pl.ds(kstart, width), :], preferred_element_type=jnp.float32
+        ).astype(jnp.bfloat16)
+
+
+def attention_forward(toff, taps_flat, mix_flat, q_blocks, k_heads, v_heads, row_docs, key_docs, nw, length):
+    nb_all = q_blocks.shape[0]
+    width = nw * TQ
+    smem = pl.BlockSpec(memory_space=pltpu.SMEM)
+    flops = nb_all * 2 * (4 * EXT * width * HD + 2 * TAPS * EXT * width)
+    return pl.pallas_call(
+        lambda *refs: fwd_kernel(*refs, nw=nw, length=length),
+        grid=(nb_all,),
+        in_specs=[
+            smem,
+            smem,
+            smem,
+            pl.BlockSpec((1, 2, EXT, HD), lambda t: (t, 0, 0, 0)),
+            pl.BlockSpec((2, length, HD), lambda t: (0, 0, 0)),
+            pl.BlockSpec((2, length, HD), lambda t: (0, 0, 0)),
+            pl.BlockSpec((1, EXT, 1), lambda t: (t, 0, 0)),
+            pl.BlockSpec((1, length), lambda t: (0, 0)),
+        ],
+        out_specs=[
+            pl.BlockSpec((1, 2, TQ, HD), lambda t: (t, 0, 0, 0)),
+            pl.BlockSpec((1, 2, TQ, width), lambda t: (t, 0, 0, 0)),
+        ],
+        out_shape=[
+            jax.ShapeDtypeStruct((nb_all, 2, TQ, HD), jnp.bfloat16),
+            jax.ShapeDtypeStruct((nb_all, 2, TQ, width), jnp.float32),
+        ],
+        scratch_shapes=[
+            pltpu.VMEM((KCONV, EXT, width), jnp.float32),
+            pltpu.VMEM((QCONV, EXT, width), jnp.float32),
+        ],
+        compiler_params=pltpu.CompilerParams(
+            dimension_semantics=("arbitrary",), vmem_limit_bytes=56 * 1024 * 1024
+        ),
+        cost_estimate=pl.CostEstimate(
+            flops=flops, transcendentals=nb_all * 2 * TQ * width,
+            bytes_accessed=nb_all * 2 * TQ * width * 4 + 4 * length * HD * 2,
+        ),
+    )(toff, taps_flat, mix_flat, q_blocks, k_heads, v_heads, row_docs, key_docs)
+
+
+def bwd_kernel(toff_ref, taps_ref, mix_ref, q_ref, qo_ref, k_ref, v_ref, rdoc_ref, kdoc_ref,
+               probs_ref, gh_ref, gq_ref, gk_ref, gv_ref, tacc_ref, macc_ref,
+               carry_ref, sh_ref, acc_ref, g_ref, gx_ref, *, nw, length, nb, nb_all):
+    width = nw * TQ
+    step = pl.program_id(0)
+    local = nb_all - 1 - step
+    block = toff_ref[0] + local
+    kstart = window_start(block, nw, length)
+
+    @pl.when(step == 0)
+    def _init():
+        gk_ref[...] = jnp.zeros(gk_ref.shape, jnp.float32)
+        gv_ref[...] = jnp.zeros(gv_ref.shape, jnp.float32)
+        tacc_ref[...] = jnp.zeros(tacc_ref.shape, jnp.float32)
+        macc_ref[...] = jnp.zeros(macc_ref.shape, jnp.float32)
+        carry_ref[...] = jnp.zeros(carry_ref.shape, jnp.float32)
+
+    allowed_ext, allowed_own = masks(block, kstart, width, rdoc_ref, kdoc_ref)
+    gm = [
+        lax.dot_general(
+            gh_ref[0, c], v_ref[c, pl.ds(kstart, width), :], (((1,), (1,)), ((), ())),
+            preferred_element_type=jnp.float32,
+        )
+        for c in range(2)
+    ]
+    probs = [probs_ref[0, 0], probs_ref[0, 1]]
+    gc = []
+    for e in range(2):
+        gp = mix_ref[e] * gm[0] + mix_ref[2 + e] * gm[1]
+        inner = jnp.sum(gp * probs[e], axis=1, keepdims=True)
+        gc.append(probs[e] * (gp - inner))
+
+    def own_sums():
+        for c in range(2):
+            for e in range(2):
+                macc_ref[pl.ds(2 * c + e, 1), :] += jnp.sum(gm[c] * probs[e], axis=0, keepdims=True)
+            mixed = (mix_ref[2 * c] * probs[0] + mix_ref[2 * c + 1] * probs[1]).astype(jnp.bfloat16)
+            gv_ref[c, pl.ds(kstart, width), :] += lax.dot_general(
+                mixed, gh_ref[0, c], (((0,), (0,)), ((), ())), preferred_element_type=jnp.float32
+            )
+
+    def head_taps(e):
+        masked_shifts(q_ref, k_ref, e, kstart, width, allowed_ext, sh_ref)
+        gcp = jnp.concatenate([jnp.zeros((PAD, width), jnp.float32), gc[e]], axis=0)
+        g_ref[0] = gcp
+        for a in range(1, QCONV):
+            g_ref[a] = pltpu.roll(gcp, EXT - a, 0)
+        sums = tap_products(sh_ref, g_ref, width)
+        for b in range(KCONV):
+            for a in range(QCONV):
+                tacc_ref[e * TAPS + a * KCONV + b] += sums[b][a]
+
+    def head_keys(e, gs):
+        gk_ref[e, pl.ds(kstart, width), :] += lax.dot_general(
+            gs, qo_ref[0, e], (((0,), (0,)), ((), ())), preferred_element_type=jnp.float32
+        ) * SCALE
+
+    nxt = [carry_ref[e, :, pl.ds(kstart, width + TQ)] for e in range(2)]
+    if nb < nb_all:
+        pl.when(local < nb)(own_sums)
+    else:
+        own_sums()
+    for e in range(2):
+        if nb < nb_all:
+            pl.when(local < nb)(lambda: head_taps(e))
+        else:
+            head_taps(e)
+        gx_ref[pl.ds(0, TQ), pl.ds(0, width)] = gc[e]
+        gx_ref[pl.ds(0, TQ), pl.ds(width, TQ)] = jnp.zeros((TQ, TQ), jnp.float32)
+        gx_ref[pl.ds(TQ, PAD), :] = nxt[e]
+        gxv = gx_ref[...]
+        sh_ref[0] = gxv[:, :width]
+        for b in range(1, KCONV):
+            sh_ref[b] = pltpu.roll(gxv, width + TQ - b, 1)[:, :width]
+        tap_accumulate(sh_ref, acc_ref, taps_ref, e, width)
+        gmk = acc_ref[0]
+        for a in range(1, QCONV):
+            gmk = gmk + pltpu.roll(acc_ref[a], EXT - a, 0)
+        gs = jnp.where(allowed_own, gmk[:TQ], 0.0).astype(jnp.bfloat16)
+        gq_ref[0, e] = (
+            jnp.dot(gs, k_ref[e, pl.ds(kstart, width), :], preferred_element_type=jnp.float32) * SCALE
+        ).astype(jnp.bfloat16)
+        if nb < nb_all:
+            pl.when(local < nb)(lambda: head_keys(e, gs))
+        else:
+            head_keys(e, gs)
+    carry_ref[...] = jnp.zeros(carry_ref.shape, jnp.float32)
+    for e in range(2):
+        carry_ref[e, :, pl.ds(kstart, width)] = gc[e][:PAD]
+
+
+def attention_backward(toff, taps_flat, mix_flat, q_blocks, q_own, k_heads, v_heads, row_docs, key_docs,
+                       probs_blk, gh_blocks, nw, length, nb):
+    nb_all = q_blocks.shape[0]
+    width = nw * TQ
+    smem = pl.BlockSpec(memory_space=pltpu.SMEM)
+    rev = lambda s: nb_all - 1 - s
+    flops = nb_all * 2 * (8 * TQ * width * HD + 6 * TAPS * EXT * width)
+    return pl.pallas_call(
+        lambda *refs: bwd_kernel(*refs, nw=nw, length=length, nb=nb, nb_all=nb_all),
+        grid=(nb_all,),
+        in_specs=[
+            smem,
+            smem,
+            smem,
+            pl.BlockSpec((1, 2, EXT, HD), lambda s: (rev(s), 0, 0, 0)),
+            pl.BlockSpec((1, 2, TQ, HD), lambda s: (rev(s), 0, 0, 0)),
+            pl.BlockSpec((2, length, HD), lambda s: (0, 0, 0)),
+            pl.BlockSpec((2, length, HD), lambda s: (0, 0, 0)),
+            pl.BlockSpec((1, EXT, 1), lambda s: (rev(s), 0, 0)),
+            pl.BlockSpec((1, length), lambda s: (0, 0)),
+            pl.BlockSpec((1, 2, TQ, width), lambda s: (rev(s), 0, 0, 0)),
+            pl.BlockSpec((1, 2, TQ, HD), lambda s: (rev(s), 0, 0, 0)),
+        ],
+        out_specs=[
+            pl.BlockSpec((1, 2, TQ, HD), lambda s: (rev(s), 0, 0, 0)),
+            pl.BlockSpec((2, length, HD), lambda s: (0, 0, 0)),
+            pl.BlockSpec((2, length, HD), lambda s: (0, 0, 0)),
+            pl.BlockSpec((2 * TAPS, 8, 128), lambda s: (0, 0, 0)),
+            pl.BlockSpec((4, width), lambda s: (0, 0)),
+        ],
+        out_shape=[
+            jax.ShapeDtypeStruct((nb_all, 2, TQ, HD), jnp.bfloat16),
+            jax.ShapeDtypeStruct((2, length, HD), jnp.float32),
+            jax.ShapeDtypeStruct((2, length, HD), jnp.float32),
+            jax.ShapeDtypeStruct((2 * TAPS, 8, 128), jnp.float32),
+            jax.ShapeDtypeStruct((4, width), jnp.float32),
+        ],
+        scratch_shapes=[
+            pltpu.VMEM((2, PAD, length + TQ), jnp.float32),
+            pltpu.VMEM((KCONV, EXT, width), jnp.float32),
+            pltpu.VMEM((QCONV, EXT, width), jnp.float32),
+            pltpu.VMEM((QCONV, EXT, width), jnp.float32),
+            pltpu.VMEM((EXT, width + TQ), jnp.float32),
+        ],
+        compiler_params=pltpu.CompilerParams(
+            dimension_semantics=("arbitrary",), vmem_limit_bytes=60 * 1024 * 1024
+        ),
+        cost_estimate=pl.CostEstimate(
+            flops=flops, transcendentals=0,
+            bytes_accessed=nb_all * 2 * TQ * width * 4 + 8 * length * HD * 4,
+        ),
+    )(toff, taps_flat, mix_flat, q_blocks, q_own, k_heads, v_heads, row_docs, key_docs, probs_blk, gh_blocks)
 
 
 def shards(
@@ -68,9 +345,6 @@
     splits = seq_count // groups
     span = length // splits
     pw = 2 * HD
-    ext = span + 2 * PAD
-    xrows = span + PAD
-    score_scale = HD ** (-0.5)
     pair = seq_index // splits
     part = seq_index % splits
     q0 = part * span
@@ -87,42 +361,35 @@
     taps = lax.dynamic_slice_in_dim(conv_taps, pair * 2, 2, 0)
     mixing = lax.dynamic_index_in_dim(head_mix, pair, 0, keepdims=False)
 
-    normed_pad = jnp.pad(normed_all, ((PAD, PAD), (0, 0)))
-    q_ext = project(lax.dynamic_slice_in_dim(normed_pad, q0, ext, 0), wq_g).astype(jnp.bfloat16)
     k_all = project(normed_all, wk_g).astype(jnp.bfloat16)
     v_all = project(normed_all, wv_g).astype(jnp.bfloat16)
-    q3 = q_ext.reshape(ext, 2, HD)
     k3 = k_all.reshape(length, 2, HD)
     v3 = v_all.reshape(length, 2, HD)
 
     docs = doc_ids[0]
-    docs_pad = jnp.pad(docs, (PAD, PAD), constant_values=-1)
-    ext_docs = lax.dynamic_slice_in_dim(docs_pad, q0, ext, 0)
-    ext_pos = q0 - PAD + jnp.arange(ext, dtype=jnp.int32)
-    key_pos = jnp.arange(length, dtype=jnp.int32)
-    mask_e = (key_pos[None, :] <= ext_pos[:, None]) & (ext_docs[:, None] == docs[None, :])
-
-    scores = jnp.einsum("ihd,jhd->hij", q3, k3, preferred_element_type=jnp.float32) * score_scale
-    masked = jnp.where(mask_e[None], scores, 0.0)
-    mp = jnp.pad(masked, ((0, 0), (0, 0), (KCONV - 1, 0)))
-    conv_x = jnp.zeros((2, xrows, length), jnp.float32)
-    for a in range(QCONV):
-        for b in range(KCONV):
-            weight = taps[:, a, b][:, None, None]
-            conv_x = conv_x + weight * mp[:, PAD - a : PAD - a + xrows, KCONV - 1 - b : KCONV - 1 - b + length]
-    mask_x = mask_e[PAD : PAD + xrows]
-    logits = jnp.where(mask_x[None], conv_x, -jnp.inf)
-    highest = jnp.max(logits, axis=-1, keepdims=True)
-    highest = jnp.where(highest > -jnp.inf, highest, 0.0)
-    expd = jnp.exp(logits - highest)
-    denom = jnp.sum(expd, axis=-1, keepdims=True)
-    probs_x = expd / jnp.where(denom > 0, denom, 1.0)
-    mixed_own = mix_heads(probs_x[:, :span], mixing).astype(jnp.bfloat16)
-    heads_own = (
-        jnp.einsum("hij,jhd->ihd", mixed_own, v3, preferred_element_type=jnp.float32)
-        .astype(jnp.bfloat16)
-        .reshape(span, pw)
-    )
+    nb = span // TQ
+    extra = 1 if splits > 1 else 0
+    nb_all = nb + extra
+    doc_cap = length // 2
+    nw = min(length // TQ, (doc_cap + QCONV - 2 + TQ - 1) // TQ + 1)
+    q_tail = normed_pad_tail(normed_all, extra)
+    q_rows = project(lax.dynamic_slice_in_dim(q_tail, q0, nb_all * TQ + PAD, 0), wq_g).astype(jnp.bfloat16)
+    q_blocks = jnp.stack([q_rows[t * TQ : t * TQ + EXT] for t in range(nb_all)])
+    q_blocks = jnp.transpose(q_blocks.reshape(nb_all, EXT, 2, HD), (0, 2, 1, 3))
+    q_own = q_blocks[:, :, PAD:]
+    k_heads = jnp.transpose(k3, (1, 0, 2))
+    v_heads = jnp.transpose(v3, (1, 0, 2))
+    docs_tail = jnp.pad(docs, (PAD, TQ * extra), constant_values=-1)
+    doc_rows = lax.dynamic_slice_in_dim(docs_tail, q0, nb_all * TQ + PAD, 0)
+    row_docs = jnp.stack([doc_rows[t * TQ : t * TQ + EXT] for t in range(nb_all)])[:, :, None]
+    key_docs = docs[None, :]
+    toff = (q0 // TQ).astype(jnp.int32).reshape(1)
+    taps_flat = taps.reshape(2 * QCONV * KCONV)
+    mix_flat = mixing.reshape(4)
+    heads_blk, probs_blk = attention_forward(
+        toff, taps_flat, mix_flat, q_blocks, k_heads, v_heads, row_docs, key_docs, nw, length
+    )
+    heads_own = jnp.transpose(heads_blk[:nb], (0, 2, 1, 3)).reshape(span, pw)
 
     def to_tokens(values):
         cols = values.shape[1]
@@ -196,47 +463,21 @@
     )
     grad_attn = grad_middle.astype(jnp.bfloat16)
     grad_attn_all = lax.all_gather(grad_attn, "seq", axis=0, tiled=True)
-    grad_attn_pad = jnp.pad(grad_attn_all, ((0, PAD), (0, 0)))
+    grad_attn_tail = jnp.pad(grad_attn_all, ((0, TQ * extra), (0, 0)))
     grad_heads_x = contract_cols(
-        lax.dynamic_slice_in_dim(grad_attn_pad, q0, xrows, 0), wo_g
+        lax.dynamic_slice_in_dim(grad_attn_tail, q0, nb_all * TQ, 0), wo_g
     ).astype(jnp.bfloat16)
-    gh3 = grad_heads_x.reshape(xrows, 2, HD)
+    gh_blocks = jnp.transpose(grad_heads_x.reshape(nb_all, TQ, 2, HD), (0, 2, 1, 3))
     grad_out_part = contract_rows(heads_own, lax.dynamic_slice_in_dim(grad_attn_all, q0, span, 0))
-
-    grad_mixed = jnp.einsum("ihd,jhd->hij", gh3, v3, preferred_element_type=jnp.float32)
-    grad_v_part = jnp.einsum(
-        "hij,ihd->jhd", mixed_own, gh3[:span], preferred_element_type=jnp.float32
-    ).reshape(length, pw)
-    grad_mix_part = jnp.stack(
-        [
-            jnp.sum(grad_mixed[:, :span] * probs_x[0:1, :span], axis=(1, 2)),
-            jnp.sum(grad_mixed[:, :span] * probs_x[1:2, :span], axis=(1, 2)),
-        ],
-        axis=1,
-    )
-    grad_probs = mix_back(grad_mixed, mixing)
-    inner = jnp.sum(grad_probs * probs_x, axis=-1, keepdims=True)
-    grad_conv = probs_x * (grad_probs - inner)
-    tap_entries = []
-    for a in range(QCONV):
-        for b in range(KCONV):
-            piece = mp[:, PAD - a : PAD - a + span, KCONV - 1 - b : KCONV - 1 - b + length]
-            tap_entries.append(jnp.sum(grad_conv[:, :span] * piece, axis=(1, 2)))
-    grad_taps_part = jnp.stack(tap_entries, axis=1).reshape(2, QCONV, KCONV)
-    gc_pad = jnp.pad(grad_conv, ((0, 0), (0, 0), (0, KCONV - 1)))
-    grad_masked = jnp.zeros((2, span, length), jnp.float32)
-    for a in range(QCONV):
-        for b in range(KCONV):
-            weight = taps[:, a, b][:, None, None]
-            grad_masked = grad_masked + weight * gc_pad[:, a : a + span, b : b + length]
-    grad_scores = jnp.where(mask_e[None, PAD : PAD + span], grad_masked, 0.0).astype(jnp.bfloat16)
-    grad_q_own = (
-        jnp.einsum("hij,jhd->ihd", grad_scores, k3, preferred_element_type=jnp.float32) * score_scale
-    ).astype(jnp.bfloat16).reshape(span, pw)
-    grad_k_part = (
-        jnp.einsum("hij,ihd->jhd", grad_scores, q3[PAD : PAD + span], preferred_element_type=jnp.float32)
-        * score_scale
-    ).reshape(length, pw)
+    gq_blk, gk_heads, gv_heads, tap_acc, mix_acc = attention_backward(
+        toff, taps_flat, mix_flat, q_blocks, q_own, k_heads, v_heads, row_docs, key_docs,
+        probs_blk, gh_blocks, nw, length, nb,
+    )
+    grad_q_own = jnp.transpose(gq_blk[:nb], (0, 2, 1, 3)).reshape(span, pw)
+    grad_k_part = jnp.transpose(gk_heads, (1, 0, 2)).reshape(length, pw)
+    grad_v_part = jnp.transpose(gv_heads, (1, 0, 2)).reshape(length, pw)
+    grad_taps_part = jnp.sum(tap_acc, axis=(1, 2)).reshape(2, QCONV, KCONV)
+    grad_mix_part = jnp.sum(mix_acc, axis=1).reshape(2, 2)
 
     def split_sum(values):
         if splits == 1:

time: 1760 us -> 1110 us (0.63)
  other arithmetic: 1170 us -> 24 us
  Pallas kernels: 0 us -> 582 us
  waiting for transfers between devices: 326 us -> 244 us
  matrix products: 95.8 us -> 77.1 us
    pallas_call x0 -> x2, Pallas kernels: none -> 582 us  [the longest x1 480 us: attention_backward(): pl.pallas_call(lambda *refs: bwd_kernel(*refs, nw=nw, length=length, nb=n...]
    reduce_max x1 -> x0, other arithmetic: 411 us -> none  [shards(): highest = jnp.max(logits, axis=-1, keepdims=True)]
    convert_element_type x1, other arithmetic: 386 us -> 2.64 us  [shards(): grad_v_low = split_sum(grad_v_part).astype(jnp.bfloat16)]
    reduce_sum x10 -> x2, other arithmetic: 349 us -> 1.15 us  [the longest x1 1.03 us: shards(): grad_taps_part = jnp.sum(tap_acc, axis=(1, 2)).reshape(2, QCONV, KCONV)]
    reduce_scatter x1, waiting for transfers between devices: 32.2 us -> 0.01 us  [shards(): lax.psum_scatter(grad_joint_w[:, hid_width:].astype(jnp.bfloat16), 'row',...]
    reduce_scatter x1, waiting for transfers between devices: 31.9 us -> 0.01 us  [shards(): lax.psum_scatter(grad_joint_w[:, :hid_width].astype(jnp.bfloat16), 'row',...]
    unnamed x17, waiting for transfers between devices: 31.3 us -> 2.65 us
    all_gather x1, waiting for transfers between devices: 37.8 us -> 10.5 us  [shards(): grad_attn_all = lax.all_gather(grad_attn, 'seq', axis=0, tiled=True)]
  transfers between devices with their start and end apart: 21 -> 21, of which waited for: 12 -> 10; matrix products, arithmetic and copies ran while one was open for 65% -> 13% of each run, Pallas kernels for 0% -> 53%
where the time goes in v2:
time: 1110 us; the launch traced here: 1100 us
  Pallas kernels  582 us (52%)
  waiting for transfers between devices  244 us (22%)
  matrix products  77.1 us (7%)
  local copies, waits for them, and re-layouts  66.9 us (6%)
  blocking collectives  57 us (5%)
  starting transfers between devices  30.5 us (3%)
  other arithmetic  24 us (2%)
  between operations  14.5 us (1%)
    pallas_call x1, Pallas kernels, attention_backward(): pl.pallas_call(lambda *refs: bwd_kernel(*refs, nw=nw, length=length, nb=n...  480 us
    pallas_call x1, Pallas kernels, attention_forward(): pl.pallas_call(lambda *refs: fwd_kernel(*refs, nw=nw, length=length), gri...  102 us
    unnamed x1, blocking collectives  41.9 us
    reduce_scatter x1, waiting for transfers between devices, shards(): lax.psum_scatter(project(hidden, down_full).astype(jnp.bfloat16), 'seq',...  40.5 us
    all_gather x1, waiting for transfers between devices, shards(): cot_rows = lax.all_gather(cot_low, 'seq', axis=0, tiled=True)  40.3 us
    all_gather x1, waiting for transfers between devices, shards(): normed_all = lax.all_gather(normed, 'seq', axis=0, tiled=True)  36.7 us
    reduce_scatter x1, waiting for transfers between devices, shards(): lax.psum_scatter(contract_cols(grad_joint, joint).astype(jnp.bfloat16), '...  34.1 us
    dot_general x6, matrix products, contract_cols(): lax.dot_general(left, right, (((1,), (1,)), ((), ())), preferred_element_...  28.7 us
  transfers between devices with their start and end apart: 21, of which 10 were waited for; matrix products, arithmetic and copies ran while one was open for 13% of the time, Pallas kernels for 53%

profile of v2, /device:TPU:0, one launch (start us, length us, event | category | flops | bytes accessed | tf_op | source)
XLA Modules:
  0.0 1096.4 jit_solution(1238416370682446434)
XLA Ops:
  15.0 36.7 %all-gather.8.cloned.1.call-done = bf16[1024,1536]{1,0:T(8,128)(2,1)} async-done(((bf16[128,1536]{1,0:T(8,128)(2,1)}), bf16[1024,1536]{1,0:T(8,128)(2,1)}) %all-gather.8.cloned.1.call-update) | async-done | bytes 3145744 | tf_op jit(solution)/shard_map/all_gather | solution.py:355
  83.2 102.2 %shard_map.237 = (bf16[8,2,128,96]{3,2,1,0:T(8,128)(2,1)}, f32[8,2,128,768]{3,2,1,0:T(8,128)}) custom-call(s32[1]{0:T(128)} %constant.62.clone.1.refs_0_, f32[132]{0:T(256)} %reshape.192.refs_1_, f32[4]{0:T(128)} %reshape.193.refs_2_, bf16[8,2,136,96]{3,2,1,0:T(8,128)(2,1)} %bitcast.9.refs_3_, bf16[2,1024,96]{2,1,0:T(8,128)(2,1)} %bitcast.149, ...), custom_call_target="tpu_custom_call" | custom-call | flops 862322688 | bytes 7077888 | tf_op jit(solution)/shard_map/pallas_call | solution.py:140
  186.6 15.0 %all_to_all.42 = bf16[8,128,192]{1,2,0:T(8,128)(2,1)S(1)} all-to-all(bf16[8,128,192]{1,2,0:T(8,128)(2,1)S(1)} %bitcast.169), channel_id=1, replica_groups=mesh['row'=4,'seq'=8] {'seq'}, dimensions={0} | all-to-all | bytes 786432 | tf_op jit(solution)/shard_map/all_to_all | solution.py:402
  215.5 28.7 %all-gather.10.cloned.1.call-done = bf16[1024,1536]{1,0:T(8,128)(2,1)} async-done(((bf16[128,1536]{1,0:T(8,128)(2,1)}), bf16[1024,1536]{1,0:T(8,128)(2,1)}) %all-gather.10.cloned.1.call-update) | async-done | bytes 3145744 | tf_op jit(solution)/shard_map/all_gather | solution.py:421
  244.2 8.4 fusion.45
  252.5 22.9 %all-gather.16.cloned.1.call-done = bf16[512,1536]{1,0:T(8,128)(2,1)} async-done(((bf16[512,384]{1,0:T(8,128)(2,1)}), bf16[512,1536]{1,0:T(8,128)(2,1)}) %all-gather.16.cloned.1.call-update) | async-done | bytes 1572880 | tf_op jit(solution)/shard_map/all_gather | solution.py:417
  275.5 40.3 %all-gather.18.cloned.1.call-done = bf16[1024,1536]{1,0:T(8,128)(2,1)} async-done(((bf16[128,1536]{1,0:T(8,128)(2,1)}), bf16[1024,1536]{1,0:T(8,128)(2,1)}) %all-gather.18.cloned.1.call-update) | async-done | bytes 3145744 | tf_op jit(solution)/shard_map/all_gather | solution.py:432
  315.8 7.3 multiply_convert_fusion.1
  324.5 5.0 convolution_convert_fusion.2
  329.5 5.2 convolution_convert_fusion
  334.8 34.1 %reduce-scatter.14.cloned.1.call-done = bf16[128,1536]{1,0:T(8,128)(2,1)} async-done(((bf16[1024,1536]{1,0:T(8,128)(2,1)}), bf16[128,1536]{1,0:T(8,128)(2,1)}) %reduce-scatter.14.cloned.1.call-update) | async-done | bytes 393232 | tf_op jit(solution)/shard_map/reduce_scatter | solution.py:440
  370.4 40.5 %reduce-scatter.12.cloned.1.call-done = bf16[128,1536]{1,0:T(8,128)(2,1)} async-done(((bf16[1024,1536]{1,0:T(8,128)(2,1)}), bf16[128,1536]{1,0:T(8,128)(2,1)}) %reduce-scatter.12.cloned.1.call-update) | async-done | bytes 393232 | tf_op jit(solution)/shard_map/reduce_scatter | solution.py:426
  414.2 5.2 convolution_convert_fusion.3
  422.1 6.0 convolution_convert_fusion.1
  430.6 8.7 reduce-scatter.18.cloned.1.call-start
  441.1 10.5 all-gather.20.cloned.1.call-done
  456.0 480.1 %shard_map.238 = (bf16[8,2,128,96]{3,2,1,0:T(8,128)(2,1)}, f32[2,1024,96]{2,1,0:T(8,128)}, f32[2,1024,96]{2,1,0:T(8,128)}, f32[132,8,128]{2,1,0:T(8,128)}, f32[4,768]{1,0:T(4,128)}) custom-call(s32[1]{0:T(128)} %constant.62.clone.1.refs_0_, f32[132]{0:T(256)} %reshape.192.refs_1_, f32[4]{0:T(128)} %reshape.193.refs_2_, ...), custom_call_target="tpu_custom_call" | custom-call | flops 1869742080 | bytes 9437184 | tf_op jit(solution)/shard_map/pallas_call | solution.py:273
  959.0 4.2 all-to-all-start.1
  974.7 18.0 %all-to-all-done.1 = bf16[8,128,576]{1,2,0:T(8,128)(2,1)} async-done(((bf16[8,128,576]{1,2,0:T(8,128)(2,1)}), bf16[8,128,576]{1,2,0:T(8,128)(2,1)}, u32[]{:S(2)}, u32[]{:S(2)}) %all-to-all-start.1) | async-done | bytes 1179680 | tf_op jit(solution)/shard_map/all_to_all | solution.py:402
  995.9 4.1 all-to-all-start.3
  1016.1 5.1 fusion.21
  1021.2 41.9 %all-reduce.4 = (f32[1536]{0:T(1024)S(1)}, f32[1536]{0:T(1024)S(1)}, f32[16,6,11]{0,1,2:T(8,128)}, f32[8,2,2]{0,2,1:T(2,128)}) all-reduce(f32[1536]{0:T(1024)S(1)} %get-tuple-element.27, f32[1536]{0:T(1024)S(1)} %get-tuple-element.29, ...), channel_id=8, replica_groups=mesh['row'=4,'seq'=8] {'row','seq'}, use_global_device_ids=true, to_apply=%region_11.12.clone | all-reduce | flops 4160 | bytes 33280
  1067.8 7.3 all-to-all-start.2
  1080.6 7.2 all-to-all-done.2
  (172 shorter events, 137.3 us)
Async XLA Ops:
  7.2 44.5 %all-gather.8.cloned.1.call-start = ((), (), s32[]{:S(2)}) async-start(), calls=%async_computation.14 | async-start | bytes 3538944 | tf_op jit(solution)/shard_map/all_gather | solution.py:355
  10.6 199.3 %all-gather.12.cloned.1.call-start = ((), (), s32[]{:S(2)}) async-start(), calls=%async_computation.16 | async-start | bytes 1966080 | tf_op jit(solution)/shard_map/all_gather | solution.py:415
  11.3 201.3 %all-gather.14.cloned.1.call-start = ((), (), s32[]{:S(2)}) async-start(), calls=%async_computation.17 | async-start | bytes 1966080 | tf_op jit(solution)/shard_map/all_gather | solution.py:416
  12.1 232.1 %all-gather.10.cloned.1.call-start = ((), (), s32[]{:S(2)}) async-start(), calls=%async_computation.15 | async-start | bytes 3538944 | tf_op jit(solution)/shard_map/all_gather | solution.py:421
  206.9 68.5 %all-gather.16.cloned.1.call-start = ((), (), s32[]{:S(2)}) async-start(), calls=%async_computation.18 | async-start | bytes 1966080 | tf_op jit(solution)/shard_map/all_gather | solution.py:417
  207.5 108.3 %all-gather.18.cloned.1.call-start = ((), (), s32[]{:S(2)}) async-start(), calls=%async_computation.20 | async-start | bytes 3538944 | tf_op jit(solution)/shard_map/all_gather | solution.py:432
  209.5 159.4 %reduce-scatter.14.cloned.1.call-start = ((), (), s32[]{:S(2)}) async-start(), calls=%async_computation.21 | async-start | bytes 3538944 | tf_op jit(solution)/shard_map/reduce_scatter | solution.py:440
  329.5 81.5 %reduce-scatter.12.cloned.1.call-start = ((), (), s32[]{:S(2)}) async-start(), calls=%async_computation.19 | async-start | bytes 3538944 | tf_op jit(solution)/shard_map/reduce_scatter | solution.py:426
  334.7 116.9 %all-gather.20.cloned.1.call-start = ((), (), s32[]{:S(2)}) async-start(), calls=%async_computation.22 | async-start | bytes 3538944 | tf_op jit(solution)/shard_map/all_gather | solution.py:465
  414.1 552.6 %reduce-scatter.28.cloned.1.call-start = ((), (), s32[]{:S(2)}) async-start(), calls=%async_computation.29 | async-start | bytes 1966080
  422.0 546.9 %reduce-scatter.24.cloned.1.call-start = ((), (), s32[]{:S(2)}) async-start(), calls=%async_computation.27 | async-start | bytes 1966080 | tf_op jit(solution)/shard_map/reduce_scatter | solution.py:447
  430.0 540.9 %reduce-scatter.26.cloned.1.call-start = ((), (), s32[]{:S(2)}) async-start(), calls=%async_computation.28 | async-start | bytes 1966080 | tf_op jit(solution)/shard_map/reduce_scatter | solution.py:450
  430.6 563.4 %reduce-scatter.18.cloned.1.call-start = ((), (), s32[]{:S(2)}) async-start(), calls=%async_computation.24 | async-start | bytes 1474560 | tf_op jit(solution)/shard_map/reduce_scatter | solution.py:503
  941.8 66.4 %reduce-scatter.20.cloned.1.call-start = ((), (), s32[]{:S(2)}) async-start(), calls=%async_computation.25 | async-start | bytes 1474560 | tf_op jit(solution)/shard_map/reduce_scatter | solution.py:503
  946.7 117.6 %reduce-scatter.22.cloned.1.call-start = ((), (), s32[]{:S(2)}) async-start(), calls=%async_computation.26 | async-start | bytes 1474560 | tf_op jit(solution)/shard_map/reduce_scatter | solution.py:512
  959.0 33.6 %all-to-all-start.1 = ((bf16[8,128,576]{1,2,0:T(8,128)(2,1)}), bf16[8,128,576]{1,2,0:T(8,128)(2,1)}, u32[]{:S(2)}, u32[]{:S(2)}) async-start(bf16[8,128,576]{1,2,0:T(8,128)(2,1)} %pad_maximum_fusion.3), calls=%async_computation.3 | async-start | bytes 2359296 | tf_op jit(solution)/shard_map/all_to_all | solution.py:402
  963.3 102.6 %reduce-scatter.16.cloned.1.call-start = ((), (), s32[]{:S(2)}) async-start(), calls=%async_computation.23 | async-start | bytes 1474560 | tf_op jit(solution)/shard_map/reduce_scatter | solution.py:503
  995.9 16.6 %all-to-all-start.3 = ((f32[8,48,192]{2,1,0:T(8,128)}), f32[8,48,192]{2,1,0:T(8,128)}, u32[]{:S(2)}, u32[]{:S(2)}) async-start(f32[8,48,192]{2,1,0:T(8,128)} %bitcast.42), calls=%async_computation.7 | async-start | bytes 786432 | tf_op jit(solution)/shard_map/all_to_all | solution.py:504
  1004.1 11.9 %copy-start.3 = (f32[1,128,1536]{2,1,0:T(8,128)S(1)}, f32[1,128,1536]{2,1,0:T(8,128)}, u32[]{:S(2)}) copy-start(f32[1,128,1536]{2,1,0:T(8,128)} %param.14) | copy-start | bytes 2359300
  1012.6 55.3 %all-to-all-start.4 = ((f32[8,48,192]{2,1,0:T(8,128)}), f32[8,48,192]{2,1,0:T(8,128)S(1)}, u32[]{:S(2)}, u32[]{:S(2)}) async-start(f32[8,48,192]{2,1,0:T(8,128)} %bitcast.45), calls=%async_computation.9 | async-start | bytes 786432 | tf_op jit(solution)/shard_map/all_to_all | solution.py:504
  1016.0 59.1 %copy-start.5 = (f32[128,1536]{1,0:T(8,128)S(1)}, f32[128,1536]{1,0:T(8,128)}, u32[]{:S(2)}) copy-start(f32[128,1536]{1,0:T(8,128)} %get-tuple-element.36) | copy-start | bytes 2359300
  1064.3 13.1 %collective-permute-start = (f32[48,1536]{1,0:T(8,128)}, f32[48,1536]{1,0:T(8,128)S(1)}, u32[]{:S(2)}, u32[]{:S(2)}) collective-permute-start(f32[48,1536]{1,0:T(8,128)} %reduce-scatter.22.cloned.1.call-done), channel_id=1, source_target_pairs={{0,0},{1,4},{2,8},{3,12},{4,16},{5,20},{6,24},{7,28},{8,1},{9,5},{... | collective-permute-start | bytes 884744 | tf_op jit(solution)/shard_map/ppermute | solution.py:523
  1067.8 20.0 %all-to-all-start.2 = ((f32[8,48,192]{2,1,0:T(8,128)}), f32[8,48,192]{2,1,0:T(8,128)S(1)}, u32[]{:S(2)}, u32[]{:S(2)}) async-start(f32[8,48,192]{2,1,0:T(8,128)} %bitcast.39), calls=%async_computation.5 | async-start | bytes 786432 | tf_op jit(solution)/shard_map/all_to_all | solution.py:504
  1075.2 14.5 %copy-start.1 = (f32[16,6,11]{0,1,2:T(8,128)S(1)}, f32[16,6,11]{0,1,2:T(8,128)}, u32[]{:S(2)}) copy-start(f32[16,6,11]{0,1,2:T(8,128)} %param.22) | copy-start | bytes 12676
  (13 other events, 71.9 us)
Sparse Core Ops, SparseCore 0:
  10.7 40.9 all-gather.7
  53.5 29.7 all-gather.11
  85.2 30.8 all-gather.13
  207.0 37.0 all-gather.9
  245.8 29.5 all-gather.15
  277.5 38.2 all-gather.17
  329.6 39.2 reduce-scatter.13
  371.2 39.6 reduce-scatter.11
  414.2 37.3 all-gather.19
  454.5 30.0 reduce-scatter.27
  487.6 31.1 reduce-scatter.23
  521.6 31.1 reduce-scatter.25
  942.0 27.6 reduce-scatter.17
  972.4 28.6 reduce-scatter.19
  1003.9 29.2 reduce-scatter.21
  1035.9 28.7 reduce-scatter.15

commit v3 on v2

--- a/solution.py
+++ b/solution.py
@@ -47,18 +47,19 @@
 
 
 def tap_accumulate(sh_ref, acc_ref, taps_ref, head, width):
-    ncols = width // 128
+    cw = 256 if (width // 128) % 2 == 0 else 128
+    ncols = width // cw
 
     def body(idx, carry):
         r0 = pl.multiple_of((idx // ncols) * 8, 8)
-        c0 = pl.multiple_of((idx % ncols) * 128, 128)
-        tiles = [sh_ref[b, pl.ds(r0, 8), pl.ds(c0, 128)] for b in range(KCONV)]
+        c0 = pl.multiple_of((idx % ncols) * cw, cw)
+        tiles = [sh_ref[b, pl.ds(r0, 8), pl.ds(c0, cw)] for b in range(KCONV)]
         for a in range(QCONV):
             base = head * TAPS + a * KCONV
             total = taps_ref[base] * tiles[0]
             for b in range(1, KCONV):
                 total = total + taps_ref[base + b] * tiles[b]
-            acc_ref[a, pl.ds(r0, 8), pl.ds(c0, 128)] = total
+            acc_ref[a, pl.ds(r0, 8), pl.ds(c0, cw)] = total
         return carry
 
     lax.fori_loop(0, (EXT // 8) * ncols, body, 0)
@@ -66,19 +67,25 @@
 
 def tap_products(sh_ref, g_ref, width):
     ncols = width // 128
-    sums = []
-    for b in range(KCONV):
+    sums = {}
+    for a0 in range(0, QCONV, 2):
 
         def body(idx, accs):
             r0 = pl.multiple_of((idx // ncols) * 8, 8)
             c0 = pl.multiple_of((idx % ncols) * 128, 128)
-            tile = sh_ref[b, pl.ds(r0, 8), pl.ds(c0, 128)]
-            return tuple(
-                accs[a] + g_ref[a, pl.ds(r0, 8), pl.ds(c0, 128)] * tile for a in range(QCONV)
-            )
-
-        start = tuple(jnp.zeros((8, 128), jnp.float32) for _ in range(QCONV))
-        sums.append(lax.fori_loop(0, (EXT // 8) * ncols, body, start))
+            ga = [g_ref[a0 + k, pl.ds(r0, 8), pl.ds(c0, 128)] for k in range(2)]
+            out = list(accs)
+            for b in range(KCONV):
+                tile = sh_ref[b, pl.ds(r0, 8), pl.ds(c0, 128)]
+                for k in range(2):
+                    out[k * KCONV + b] = out[k * KCONV + b] + ga[k] * tile
+            return tuple(out)
+
+        start = tuple(jnp.zeros((8, 128), jnp.float32) for _ in range(2 * KCONV))
+        res = lax.fori_loop(0, (EXT // 8) * ncols, body, start)
+        for k in range(2):
+            for b in range(KCONV):
+                sums[(a0 + k, b)] = res[k * KCONV + b]
     return sums
 
 
@@ -173,7 +180,7 @@
 
 
 def bwd_kernel(toff_ref, taps_ref, mix_ref, q_ref, qo_ref, k_ref, v_ref, rdoc_ref, kdoc_ref,
-               probs_ref, gh_ref, gq_ref, gk_ref, gv_ref, tacc_ref, macc_ref,
+               probs_ref, gh_ref, ght_ref, gq_ref, gk_ref, gv_ref, tacc_ref, macc_ref,
                carry_ref, sh_ref, acc_ref, g_ref, gx_ref, *, nw, length, nb, nb_all):
     width = nw * TQ
     step = pl.program_id(0)
@@ -209,8 +216,8 @@
             for e in range(2):
                 macc_ref[pl.ds(2 * c + e, 1), :] += jnp.sum(gm[c] * probs[e], axis=0, keepdims=True)
             mixed = (mix_ref[2 * c] * probs[0] + mix_ref[2 * c + 1] * probs[1]).astype(jnp.bfloat16)
-            gv_ref[c, pl.ds(kstart, width), :] += lax.dot_general(
-                mixed, gh_ref[0, c], (((0,), (0,)), ((), ())), preferred_element_type=jnp.float32
+            gv_ref[c, :, pl.ds(kstart, width)] += jnp.dot(
+                ght_ref[0, c], mixed, preferred_element_type=jnp.float32
             )
 
     def head_taps(e):
@@ -222,11 +229,11 @@
         sums = tap_products(sh_ref, g_ref, width)
         for b in range(KCONV):
             for a in range(QCONV):
-                tacc_ref[e * TAPS + a * KCONV + b] += sums[b][a]
+                tacc_ref[e * TAPS + a * KCONV + b] += sums[(a, b)]
 
     def head_keys(e, gs):
-        gk_ref[e, pl.ds(kstart, width), :] += lax.dot_general(
-            gs, qo_ref[0, e], (((0,), (0,)), ((), ())), preferred_element_type=jnp.float32
+        gk_ref[e, :, pl.ds(kstart, width)] += jnp.dot(
+            qo_ref[0, e], gs, preferred_element_type=jnp.float32
         ) * SCALE
 
     nxt = [carry_ref[e, :, pl.ds(kstart, width + TQ)] for e in range(2)]
@@ -265,6 +272,8 @@
 
 def attention_backward(toff, taps_flat, mix_flat, q_blocks, q_own, k_heads, v_heads, row_docs, key_docs,
                        probs_blk, gh_blocks, nw, length, nb):
+    q_own = jnp.swapaxes(q_own, 2, 3)
+    gh_t = jnp.swapaxes(gh_blocks, 2, 3)
     nb_all = q_blocks.shape[0]
     width = nw * TQ
     smem = pl.BlockSpec(memory_space=pltpu.SMEM)
@@ -278,25 +287,26 @@
             smem,
             smem,
             pl.BlockSpec((1, 2, EXT, HD), lambda s: (rev(s), 0, 0, 0)),
-            pl.BlockSpec((1, 2, TQ, HD), lambda s: (rev(s), 0, 0, 0)),
+            pl.BlockSpec((1, 2, HD, TQ), lambda s: (rev(s), 0, 0, 0)),
             pl.BlockSpec((2, length, HD), lambda s: (0, 0, 0)),
             pl.BlockSpec((2, length, HD), lambda s: (0, 0, 0)),
             pl.BlockSpec((1, EXT, 1), lambda s: (rev(s), 0, 0)),
             pl.BlockSpec((1, length), lambda s: (0, 0)),
             pl.BlockSpec((1, 2, TQ, width), lambda s: (rev(s), 0, 0, 0)),
             pl.BlockSpec((1, 2, TQ, HD), lambda s: (rev(s), 0, 0, 0)),
+            pl.BlockSpec((1, 2, HD, TQ), lambda s: (rev(s), 0, 0, 0)),
         ],
         out_specs=[
             pl.BlockSpec((1, 2, TQ, HD), lambda s: (rev(s), 0, 0, 0)),
-            pl.BlockSpec((2, length, HD), lambda s: (0, 0, 0)),
-            pl.BlockSpec((2, length, HD), lambda s: (0, 0, 0)),
+            pl.BlockSpec((2, HD, length), lambda s: (0, 0, 0)),
+            pl.BlockSpec((2, HD, length), lambda s: (0, 0, 0)),
             pl.BlockSpec((2 * TAPS, 8, 128), lambda s: (0, 0, 0)),
             pl.BlockSpec((4, width), lambda s: (0, 0)),
         ],
         out_shape=[
             jax.ShapeDtypeStruct((nb_all, 2, TQ, HD), jnp.bfloat16),
-            jax.ShapeDtypeStruct((2, length, HD), jnp.float32),
-            jax.ShapeDtypeStruct((2, length, HD), jnp.float32),
+            jax.ShapeDtypeStruct((2, HD, length), jnp.float32),
+            jax.ShapeDtypeStruct((2, HD, length), jnp.float32),
             jax.ShapeDtypeStruct((2 * TAPS, 8, 128), jnp.float32),
             jax.ShapeDtypeStruct((4, width), jnp.float32),
         ],
@@ -314,7 +324,7 @@
             flops=flops, transcendentals=0,
             bytes_accessed=nb_all * 2 * TQ * width * 4 + 8 * length * HD * 4,
         ),
-    )(toff, taps_flat, mix_flat, q_blocks, q_own, k_heads, v_heads, row_docs, key_docs, probs_blk, gh_blocks)
+    )(toff, taps_flat, mix_flat, q_blocks, q_own, k_heads, v_heads, row_docs, key_docs, probs_blk, gh_blocks, gh_t)
 
 
 def shards(
@@ -474,8 +484,8 @@
         probs_blk, gh_blocks, nw, length, nb,
     )
     grad_q_own = jnp.transpose(gq_blk[:nb], (0, 2, 1, 3)).reshape(span, pw)
-    grad_k_part = jnp.transpose(gk_heads, (1, 0, 2)).reshape(length, pw)
-    grad_v_part = jnp.transpose(gv_heads, (1, 0, 2)).reshape(length, pw)
+    grad_k_part = jnp.transpose(gk_heads, (2, 0, 1)).reshape(length, pw)
+    grad_v_part = jnp.transpose(gv_heads, (2, 0, 1)).reshape(length, pw)
     grad_taps_part = jnp.sum(tap_acc, axis=(1, 2)).reshape(2, QCONV, KCONV)
     grad_mix_part = jnp.sum(mix_acc, axis=1).reshape(2, 2)
 

time: 1110 us -> 840 us (0.76)
  Pallas kernels: 582 us -> 323 us
    pallas_call x1, Pallas kernels: 480 us -> 243 us  [attention_backward(): pl.pallas_call(lambda *refs: bwd_kernel(*refs, nw=nw, length=length, nb=n...]
    pallas_call x1, Pallas kernels: 102 us -> 80.4 us  [attention_forward(): pl.pallas_call(lambda *refs: fwd_kernel(*refs, nw=nw, length=length), gri...]
  transfers between devices with their start and end apart: 21 -> 21, of which waited for: 10 -> 11; matrix products, arithmetic and copies ran while one was open for 13% -> 16% of each run, Pallas kernels for 53% -> 39%
where the time goes in v3:
time: 840 us; the launch traced here: 831 us
  Pallas kernels  323 us (38%)
  waiting for transfers between devices  246 us (29%)
  matrix products  78.3 us (9%)
  local copies, waits for them, and re-layouts  60.1 us (7%)
  blocking collectives  57.5 us (7%)
  starting transfers between devices  30.1 us (4%)
  other arithmetic  21.5 us (3%)
  between operations  14.6 us (2%)
    pallas_call x1, Pallas kernels, attention_backward(): pl.pallas_call(lambda *refs: bwd_kernel(*refs, nw=nw, length=length, nb=n...  243 us
    pallas_call x1, Pallas kernels, attention_forward(): pl.pallas_call(lambda *refs: fwd_kernel(*refs, nw=nw, length=length), gri...  80.4 us
    unnamed x1, blocking collectives  41.6 us
    reduce_scatter x1, waiting for transfers between devices, shards(): lax.psum_scatter(project(hidden, down_full).astype(jnp.bfloat16), 'seq',...  40.6 us
    all_gather x1, waiting for transfers between devices, shards(): cot_rows = lax.all_gather(cot_low, 'seq', axis=0, tiled=True)  40.3 us
    all_gather x1, waiting for transfers between devices, shards(): normed_all = lax.all_gather(normed, 'seq', axis=0, tiled=True)  36.7 us
    reduce_scatter x1, waiting for transfers between devices, shards(): lax.psum_scatter(contract_cols(grad_joint, joint).astype(jnp.bfloat16), '...  34.1 us
    all_gather x1, waiting for transfers between devices, shards(): ffn_rows = lax.all_gather(normed_ffn, 'seq', axis=0, tiled=True)  28.7 us
  transfers between devices with their start and end apart: 21, of which 11 were waited for; matrix products, arithmetic and copies ran while one was open for 16% of the time, Pallas kernels for 39%

profile of v3, /device:TPU:0, one launch (start us, length us, event | category | flops | bytes accessed | tf_op | source)
XLA Modules:
  0.0 830.9 jit_solution(7234066572751501183)
XLA Ops:
  15.0 36.7 %all-gather.8.cloned.1.call-done = bf16[1024,1536]{1,0:T(8,128)(2,1)} async-done(((bf16[128,1536]{1,0:T(8,128)(2,1)}), bf16[1024,1536]{1,0:T(8,128)(2,1)}) %all-gather.8.cloned.1.call-update) | async-done | bytes 3145744 | tf_op jit(solution)/shard_map/all_gather | solution.py:365
  75.5 80.4 %shard_map.237 = (bf16[8,2,128,96]{3,2,1,0:T(8,128)(2,1)}, f32[8,2,128,768]{3,2,1,0:T(8,128)}) custom-call(s32[1]{0:T(128)} %constant.62.clone.1.refs_0_, f32[132]{0:T(256)} %reshape.192.refs_1_, f32[4]{0:T(128)} %reshape.193.refs_2_, bf16[8,2,136,96]{3,2,1,0:T(8,128)(2,1)} %copy.86.refs_3_, bf16[2,1024,96]{2,1,0:T(8,128)(2,1)} %bitcast.164, ...), custom_call_target="tpu_custom_call" | custom-call | flops 862322688 | bytes 7077888 | tf_op jit(solution)/shard_map/pallas_call | solution.py:147
  157.9 15.9 %all_to_all.42 = bf16[8,128,192]{1,2,0:T(8,128)(2,1)S(1)} all-to-all(bf16[8,128,192]{1,2,0:T(8,128)(2,1)} %bitcast.181), channel_id=1, replica_groups=mesh['row'=4,'seq'=8] {'seq'}, dimensions={0} | all-to-all | bytes 786432 | tf_op jit(solution)/shard_map/all_to_all | solution.py:412
  187.5 28.7 %all-gather.10.cloned.1.call-done = bf16[1024,1536]{1,0:T(8,128)(2,1)} async-done(((bf16[128,1536]{1,0:T(8,128)(2,1)}), bf16[1024,1536]{1,0:T(8,128)(2,1)}) %all-gather.10.cloned.1.call-update) | async-done | bytes 3145744 | tf_op jit(solution)/shard_map/all_gather | solution.py:431
  216.2 8.4 %fusion.45 = f32[1024,1024]{0,1:T(8,128)} fusion(bf16[1024,1536]{1,0:T(8,128)(2,1)} %all-gather.10.cloned.1.call-done, bf16[1536,1024]{1,0:T(8,128)(2,1)} %constant_dynamic-update-slice_fusion.8), kind=kOutput, calls=%fused_computation.90 | convolution fusion | flops 3221225472 | bytes 10485760 | tf_op jit(solution)/shard_map/dot_general | solution.py:26
  224.6 22.9 %all-gather.16.cloned.1.call-done = bf16[512,1536]{1,0:T(8,128)(2,1)} async-done(((bf16[512,384]{1,0:T(8,128)(2,1)}), bf16[512,1536]{1,0:T(8,128)(2,1)}) %all-gather.16.cloned.1.call-update) | async-done | bytes 1572880 | tf_op jit(solution)/shard_map/all_gather | solution.py:427
  247.5 40.3 %all-gather.18.cloned.1.call-done = bf16[1024,1536]{1,0:T(8,128)(2,1)} async-done(((bf16[128,1536]{1,0:T(8,128)(2,1)}), bf16[1024,1536]{1,0:T(8,128)(2,1)}) %all-gather.18.cloned.1.call-update) | async-done | bytes 3145744 | tf_op jit(solution)/shard_map/all_gather | solution.py:442
  287.8 7.3 multiply_convert_fusion.1
  296.5 5.0 convolution_convert_fusion.2
  301.6 5.2 convolution_convert_fusion
  306.8 34.1 %reduce-scatter.14.cloned.1.call-done = bf16[128,1536]{1,0:T(8,128)(2,1)} async-done(((bf16[1024,1536]{1,0:T(8,128)(2,1)}), bf16[128,1536]{1,0:T(8,128)(2,1)}) %reduce-scatter.14.cloned.1.call-update) | async-done | bytes 393232 | tf_op jit(solution)/shard_map/reduce_scatter | solution.py:450
  342.4 40.6 %reduce-scatter.12.cloned.1.call-done = bf16[128,1536]{1,0:T(8,128)(2,1)} async-done(((bf16[1024,1536]{1,0:T(8,128)(2,1)}), bf16[128,1536]{1,0:T(8,128)(2,1)}) %reduce-scatter.12.cloned.1.call-update) | async-done | bytes 393232 | tf_op jit(solution)/shard_map/reduce_scatter | solution.py:436
  386.3 5.2 convolution_convert_fusion.3
  394.2 6.0 convolution_convert_fusion.1
  402.7 8.4 %reduce-scatter.16.cloned.1.call-start = ((), (), s32[]{:S(2)}) async-start(), calls=%async_computation.23 | async-start | bytes 1474560 | tf_op jit(solution)/shard_map/reduce_scatter | solution.py:513
  413.2 10.7 %all-gather.20.cloned.1.call-done = bf16[1024,1536]{1,0:T(8,128)(2,1)} async-done(((bf16[128,1536]{1,0:T(8,128)(2,1)}), bf16[1024,1536]{1,0:T(8,128)(2,1)}) %all-gather.20.cloned.1.call-update) | async-done | bytes 3145744 | tf_op jit(solution)/shard_map/all_gather | solution.py:475
  430.8 242.7 %shard_map.238 = (bf16[8,2,128,96]{3,2,1,0:T(8,128)(2,1)}, f32[2,96,1024]{2,1,0:T(8,128)}, f32[2,96,1024]{2,1,0:T(8,128)}, f32[132,8,128]{2,1,0:T(8,128)}, f32[4,768]{1,0:T(4,128)}) custom-call(s32[1]{0:T(128)} %constant.62.clone.1.refs_0_, f32[132]{0:T(256)} %reshape.192.refs_1_, f32[4]{0:T(128)} %reshape.193.refs_2_, ...), custom_call_target="tpu_custom_call" | custom-call | flops 1869742080 | bytes 9437184 | tf_op jit(solution)/shard_map/pallas_call | solution.py:282
  693.9 4.2 all-to-all-start.1
  709.3 18.3 %all-to-all-done.1 = bf16[8,128,576]{1,2,0:T(8,128)(2,1)} async-done(((bf16[8,128,576]{1,2,0:T(8,128)(2,1)}), bf16[8,128,576]{1,2,0:T(8,128)(2,1)}, u32[]{:S(2)}, u32[]{:S(2)}) %all-to-all-start.1) | async-done | bytes 1179680 | tf_op jit(solution)/shard_map/all_to_all | solution.py:412
  739.1 4.1 convolution_add_fusion.1
  751.5 4.5 fusion.21
  756.1 41.6 %all-reduce.4 = (f32[1536]{0:T(1024)S(1)}, f32[1536]{0:T(1024)S(1)}, f32[16,6,11]{0,1,2:T(8,128)}, f32[8,2,2]{0,2,1:T(2,128)}) all-reduce(f32[1536]{0:T(1024)S(1)} %get-tuple-element.27, f32[1536]{0:T(1024)S(1)} %get-tuple-element.29, ...), channel_id=8, replica_groups=mesh['row'=4,'seq'=8] {'row','seq'}, use_global_device_ids=true, to_apply=%region_11.12.clone | all-reduce | flops 4160 | bytes 33280
  802.5 7.1 all-to-all-start.3
  814.0 8.3 %all-to-all-done.3 = f32[8,48,192]{2,1,0:T(8,128)S(1)} async-done(((f32[8,48,192]{2,1,0:T(8,128)}), f32[8,48,192]{2,1,0:T(8,128)S(1)}, u32[]{:S(2)}, u32[]{:S(2)}) %all-to-all-start.3) | async-done | bytes 294944 | tf_op jit(solution)/shard_map/all_to_all | solution.py:514
  (175 shorter events, 129.6 us)
Async XLA Ops:
  7.2 44.5 %all-gather.8.cloned.1.call-start = ((), (), s32[]{:S(2)}) async-start(), calls=%async_computation.14 | async-start | bytes 3538944 | tf_op jit(solution)/shard_map/all_gather | solution.py:365
  10.6 171.3 %all-gather.12.cloned.1.call-start = ((), (), s32[]{:S(2)}) async-start(), calls=%async_computation.16 | async-start | bytes 1966080 | tf_op jit(solution)/shard_map/all_gather | solution.py:425
  11.3 173.3 %all-gather.14.cloned.1.call-start = ((), (), s32[]{:S(2)}) async-start(), calls=%async_computation.17 | async-start | bytes 1966080 | tf_op jit(solution)/shard_map/all_gather | solution.py:426
  12.1 204.1 %all-gather.10.cloned.1.call-start = ((), (), s32[]{:S(2)}) async-start(), calls=%async_computation.15 | async-start | bytes 3538944 | tf_op jit(solution)/shard_map/all_gather | solution.py:431
  179.0 68.5 %all-gather.16.cloned.1.call-start = ((), (), s32[]{:S(2)}) async-start(), calls=%async_computation.18 | async-start | bytes 1966080 | tf_op jit(solution)/shard_map/all_gather | solution.py:427
  179.6 108.2 %all-gather.18.cloned.1.call-start = ((), (), s32[]{:S(2)}) async-start(), calls=%async_computation.20 | async-start | bytes 3538944 | tf_op jit(solution)/shard_map/all_gather | solution.py:442
  181.6 159.4 %reduce-scatter.14.cloned.1.call-start = ((), (), s32[]{:S(2)}) async-start(), calls=%async_computation.21 | async-start | bytes 3538944 | tf_op jit(solution)/shard_map/reduce_scatter | solution.py:450
  301.5 81.6 %reduce-scatter.12.cloned.1.call-start = ((), (), s32[]{:S(2)}) async-start(), calls=%async_computation.19 | async-start | bytes 3538944 | tf_op jit(solution)/shard_map/reduce_scatter | solution.py:436
  306.8 117.1 %all-gather.20.cloned.1.call-start = ((), (), s32[]{:S(2)}) async-start(), calls=%async_computation.22 | async-start | bytes 3538944 | tf_op jit(solution)/shard_map/all_gather | solution.py:475
  386.3 315.0 %reduce-scatter.28.cloned.1.call-start = ((), (), s32[]{:S(2)}) async-start(), calls=%async_computation.29 | async-start | bytes 1966080
  394.2 309.3 %reduce-scatter.24.cloned.1.call-start = ((), (), s32[]{:S(2)}) async-start(), calls=%async_computation.27 | async-start | bytes 1966080 | tf_op jit(solution)/shard_map/reduce_scatter | solution.py:457
  402.1 303.3 %reduce-scatter.26.cloned.1.call-start = ((), (), s32[]{:S(2)}) async-start(), calls=%async_computation.28 | async-start | bytes 1966080 | tf_op jit(solution)/shard_map/reduce_scatter | solution.py:460
  402.7 326.9 %reduce-scatter.16.cloned.1.call-start = ((), (), s32[]{:S(2)}) async-start(), calls=%async_computation.23 | async-start | bytes 1474560 | tf_op jit(solution)/shard_map/reduce_scatter | solution.py:513
  678.3 64.9 %reduce-scatter.20.cloned.1.call-start = ((), (), s32[]{:S(2)}) async-start(), calls=%async_computation.25 | async-start | bytes 1474560 | tf_op jit(solution)/shard_map/reduce_scatter | solution.py:513
  682.1 116.7 %reduce-scatter.22.cloned.1.call-start = ((), (), s32[]{:S(2)}) async-start(), calls=%async_computation.26 | async-start | bytes 1474560 | tf_op jit(solution)/shard_map/reduce_scatter | solution.py:522
  693.9 33.6 %all-to-all-start.1 = ((bf16[8,128,576]{1,2,0:T(8,128)(2,1)}), bf16[8,128,576]{1,2,0:T(8,128)(2,1)}, u32[]{:S(2)}, u32[]{:S(2)}) async-start(bf16[8,128,576]{1,2,0:T(8,128)(2,1)} %pad_maximum_fusion.3), calls=%async_computation.3 | async-start | bytes 2359296 | tf_op jit(solution)/shard_map/all_to_all | solution.py:412
  698.1 102.5 %reduce-scatter.18.cloned.1.call-start = ((), (), s32[]{:S(2)}) async-start(), calls=%async_computation.24 | async-start | bytes 1474560 | tf_op jit(solution)/shard_map/reduce_scatter | solution.py:513
  731.5 15.9 %all-to-all-start.2 = ((f32[8,48,192]{2,1,0:T(8,128)}), f32[8,48,192]{2,1,0:T(8,128)S(1)}, u32[]{:S(2)}, u32[]{:S(2)}) async-start(f32[8,48,192]{2,1,0:T(8,128)} %bitcast.41), calls=%async_computation.5 | async-start | bytes 786432 | tf_op jit(solution)/shard_map/all_to_all | solution.py:514
  747.4 55.1 %all-to-all-start.4 = ((f32[8,48,192]{2,1,0:T(8,128)}), f32[8,48,192]{2,1,0:T(8,128)}, u32[]{:S(2)}, u32[]{:S(2)}) async-start(f32[8,48,192]{2,1,0:T(8,128)} %bitcast.47), calls=%async_computation.9 | async-start | bytes 786432 | tf_op jit(solution)/shard_map/all_to_all | solution.py:514
  751.5 58.1 %copy-start.8 = (f32[128,1536]{1,0:T(8,128)S(1)}, f32[128,1536]{1,0:T(8,128)}, u32[]{:S(2)}) copy-start(f32[128,1536]{1,0:T(8,128)} %get-tuple-element.36) | copy-start | bytes 2359300
  756.1 54.7 %copy-start.11 = (f32[8,48,192]{2,1,0:T(8,128)S(1)}, f32[8,48,192]{2,1,0:T(8,128)}, u32[]{:S(2)}) copy-start(f32[8,48,192]{2,1,0:T(8,128)} %copy-done.10) | copy-start | bytes 884740
  798.9 11.9 %collective-permute-start = (f32[48,1536]{1,0:T(8,128)}, f32[48,1536]{1,0:T(8,128)S(1)}, u32[]{:S(2)}, u32[]{:S(2)}) collective-permute-start(f32[48,1536]{1,0:T(8,128)} %reduce-scatter.22.cloned.1.call-done), channel_id=1, source_target_pairs={{0,0},{1,4},{2,8},{3,12},{4,16},{5,20},{6,24},{7,28},{8,1},{9,5},{... | collective-permute-start | bytes 884744 | tf_op jit(solution)/shard_map/ppermute | solution.py:533
  802.5 19.8 %all-to-all-start.3 = ((f32[8,48,192]{2,1,0:T(8,128)}), f32[8,48,192]{2,1,0:T(8,128)S(1)}, u32[]{:S(2)}, u32[]{:S(2)}) async-start(f32[8,48,192]{2,1,0:T(8,128)} %bitcast.183), calls=%async_computation.7 | async-start | bytes 786432 | tf_op jit(solution)/shard_map/all_to_all | solution.py:514
  809.6 14.5 %copy-start.1 = (f32[16,6,11]{0,1,2:T(8,128)S(1)}, f32[16,6,11]{0,1,2:T(8,128)}, u32[]{:S(2)}) copy-start(f32[16,6,11]{0,1,2:T(8,128)} %param.22) | copy-start | bytes 12676
  (18 other events, 86.3 us)
Sparse Core Ops, SparseCore 0:
  10.7 40.9 all-gather.7
  53.5 29.7 all-gather.11
  85.1 30.8 all-gather.13
  179.1 37.0 all-gather.9
  217.9 29.5 all-gather.15
  249.6 38.2 all-gather.17
  301.6 39.2 reduce-scatter.13
  343.2 39.7 reduce-scatter.11
  386.4 37.4 all-gather.19
  426.7 30.0 reduce-scatter.27
  459.8 31.1 reduce-scatter.23
  493.8 31.1 reduce-scatter.25
  678.4 27.3 reduce-scatter.15
  708.6 28.7 reduce-scatter.19
  740.1 29.0 reduce-scatter.21
  772.0 28.5 reduce-scatter.17

commit v4 on v3

--- a/solution.py
+++ b/solution.py
@@ -327,7 +327,7 @@
     )(toff, taps_flat, mix_flat, q_blocks, q_own, k_heads, v_heads, row_docs, key_docs, probs_blk, gh_blocks, gh_t)
 
 
-def shards(
+def shards_body(
     inputs,
     doc_ids,
     w_query,
@@ -421,11 +421,9 @@
     middle = flat_in + project(heads_tok, w_out)
     scale_two = rms_scale(middle)
     normed_ffn = (middle * scale_two * gain_ffn).astype(jnp.bfloat16)
-    gate_full, up_full, down_full = (
-        lax.all_gather(w_gate, "row", axis=0, tiled=True),
-        lax.all_gather(w_up, "row", axis=0, tiled=True),
-        lax.all_gather(w_down, "row", axis=1, tiled=True),
-    )
+    gate_full = lax.all_gather(w_gate, "row", axis=0, tiled=True)
+    up_full = lax.all_gather(w_up, "row", axis=0, tiled=True)
+    down_full = lax.all_gather(w_down, "row", axis=1, tiled=True)
     hid_width = gate_full.shape[1]
     joint = jnp.concatenate([gate_full, up_full], axis=1)
     ffn_rows = lax.all_gather(normed_ffn, "seq", axis=0, tiled=True)
@@ -433,10 +431,7 @@
     gate_vals = gate_up[:, :hid_width]
     up_vals = gate_up[:, hid_width:]
     hidden = (jax.nn.silu(gate_vals) * up_vals).astype(jnp.bfloat16)
-    ffn_out = lax.psum_scatter(
-        project(hidden, down_full).astype(jnp.bfloat16), "seq", scatter_dimension=0, tiled=True
-    ).astype(jnp.float32)
-    outputs = middle + ffn_out
+    ffn_part = project(hidden, down_full).astype(jnp.bfloat16)
     cot_flat = cotangent.reshape(blk, width)
     cot_low = cot_flat.astype(jnp.bfloat16)
     cot_rows = lax.all_gather(cot_low, "seq", axis=0, tiled=True)
@@ -473,6 +468,9 @@
     )
     grad_attn = grad_middle.astype(jnp.bfloat16)
     grad_attn_all = lax.all_gather(grad_attn, "seq", axis=0, tiled=True)
+    ffn_part, grad_attn_all = lax.optimization_barrier((ffn_part, grad_attn_all))
+    ffn_out = lax.psum_scatter(ffn_part, "seq", scatter_dimension=0, tiled=True).astype(jnp.float32)
+    outputs = middle + ffn_out
     grad_attn_tail = jnp.pad(grad_attn_all, ((0, TQ * extra), (0, 0)))
     grad_heads_x = contract_cols(
         lax.dynamic_slice_in_dim(grad_attn_tail, q0, nb_all * TQ, 0), wo_g
@@ -547,17 +545,22 @@
         + scale_one * scaled_one
         - flat_in * scale_one**3 * jnp.mean(scaled_one * flat_in, axis=-1, keepdims=True)
     )
-    grad_gain_attn, grad_gain_ffn = (
-        lax.psum_scatter(gain_attn_part, ("row", "seq"), scatter_dimension=0, tiled=True),
-        lax.psum_scatter(gain_ffn_part, ("row", "seq"), scatter_dimension=0, tiled=True),
-    )
     taps_full = lax.dynamic_update_slice_in_dim(
         jnp.zeros((HEADS, QCONV, KCONV), jnp.float32), grad_taps_part, pair * 2, 0
     )
     mix_full = lax.dynamic_update_slice_in_dim(
         jnp.zeros((groups, 2, 2), jnp.float32), grad_mix_part[None], pair, 0
     )
-    grad_taps, grad_mix = lax.psum((taps_full, mix_full), ("row", "seq"))
+    small = jnp.concatenate(
+        [gain_attn_part, gain_ffn_part, taps_full.reshape(-1), mix_full.reshape(-1)]
+    )
+    small = lax.psum(lax.psum(small, "seq"), "row")
+    gain_rows = width // (row_count * seq_count)
+    gain_at = (row_index * seq_count + seq_index) * gain_rows
+    grad_gain_attn = lax.dynamic_slice_in_dim(small, gain_at, gain_rows, 0)
+    grad_gain_ffn = lax.dynamic_slice_in_dim(small, width + gain_at, gain_rows, 0)
+    grad_taps = small[2 * width : 2 * width + HEADS * TAPS].reshape(HEADS, QCONV, KCONV)
+    grad_mix = small[2 * width + HEADS * TAPS :].reshape(groups, 2, 2)
     return (
         outputs.reshape(row_dev, blk, width),
         grad_inputs.reshape(row_dev, blk, width),
@@ -577,7 +580,7 @@
 
 def solution(mesh):
     return jax.shard_map(
-        shards,
+        shards_body,
         mesh=mesh,
         in_specs=(
             P("row", "seq", None),

time: 840 us -> 847 us (level)
  starting transfers between devices: 30.1 us -> 19 us
  blocking collectives: 57.5 us -> 67.5 us
  waiting for transfers between devices: 246 us -> 255 us
    psum x0 -> x2, blocking collectives: none -> 51.6 us  [shards_body(): small = lax.psum(lax.psum(small, 'seq'), 'row')]
    unnamed x1 -> x0, blocking collectives: 41.6 us -> none
    reduce_scatter x3, waiting for transfers between devices: 0.14 us -> 32.7 us  [finish_in(): red = lax.psum_scatter(partial, 'row', scatter_dimension=0, tiled=True)]
    reduce_scatter x5, waiting for transfers between devices: 74.7 us -> 53.1 us  [the longest x1 39.4 us: shards_body(): lax.psum_scatter(contract_cols(grad_joint, joint).astype(jnp.bfloat16), '...]
    unnamed x58 -> x64, local copies, waits for them, and re-layouts: 19.1 us -> 19.3 us
  transfers between devices with their start and end apart: 21 -> 21, of which waited for: 11 -> 10; matrix products, arithmetic and copies ran while one was open for 16% -> 16% of each run, Pallas kernels for 39% -> 39%
where the time goes in v4:
time: 847 us; the launch traced here: 838 us
  Pallas kernels  323 us (38%)
  waiting for transfers between devices  255 us (30%)
  matrix products  77.2 us (9%)
  blocking collectives  67.5 us (8%)
  local copies, waits for them, and re-layouts  58 us (7%)
  other arithmetic  23.1 us (3%)
  starting transfers between devices  19 us (2%)
  between operations  14.6 us (2%)
    pallas_call x1, Pallas kernels, attention_backward(): pl.pallas_call(lambda *refs: bwd_kernel(*refs, nw=nw, length=length, nb=n...  243 us
    pallas_call x1, Pallas kernels, attention_forward(): pl.pallas_call(lambda *refs: fwd_kernel(*refs, nw=nw, length=length), gri...  80.4 us
    psum x2, blocking collectives, shards_body(): small = lax.psum(lax.psum(small, 'seq'), 'row')  51.6 us
    all_gather x1, waiting for transfers between devices, shards_body(): cot_rows = lax.all_gather(cot_low, 'seq', axis=0, tiled=True)  40.3 us
    reduce_scatter x1, waiting for transfers between devices, shards_body(): lax.psum_scatter(contract_cols(grad_joint, joint).astype(jnp.bfloat16), '...  39.4 us
    all_gather x1, waiting for transfers between devices, shards_body(): normed_all = lax.all_gather(normed, 'seq', axis=0, tiled=True)  36.6 us
    reduce_scatter x3, waiting for transfers between devices, finish_in(): red = lax.psum_scatter(partial, 'row', scatter_dimension=0, tiled=True)  32.7 us
    all_gather x1, waiting for transfers between devices, shards_body(): ffn_rows = lax.all_gather(normed_ffn, 'seq', axis=0, tiled=True)  28.6 us
  transfers between devices with their start and end apart: 21, of which 10 were waited for; matrix products, arithmetic and copies ran while one was open for 16% of the time, Pallas kernels for 39%

profile of v4, /device:TPU:0, one launch (start us, length us, event | category | flops | bytes accessed | tf_op | source)
XLA Modules:
  0.0 837.6 jit_solution(367746447364713966)
XLA Ops:
  15.0 36.6 %all-gather.8.cloned.1.call-done = bf16[1024,1536]{1,0:T(8,128)(2,1)} async-done(((bf16[128,1536]{1,0:T(8,128)(2,1)}), bf16[1024,1536]{1,0:T(8,128)(2,1)}) %all-gather.8.cloned.1.call-update) | async-done | bytes 3145744 | tf_op jit(solution)/shard_map/all_gather | solution.py:365
  75.4 80.4 %shard_map.237 = (bf16[8,2,128,96]{3,2,1,0:T(8,128)(2,1)}, f32[8,2,128,768]{3,2,1,0:T(8,128)}) custom-call(s32[1]{0:T(128)} %constant.68.clone.1.refs_0_, f32[132]{0:T(256)} %reshape.212.refs_1_, f32[4]{0:T(128)} %reshape.213.refs_2_, bf16[8,2,136,96]{3,2,1,0:T(8,128)(2,1)} %copy.86.refs_3_, bf16[2,1024,96]{2,1,0:T(8,128)(2,1)} %bitcast.165, ...), custom_call_target="tpu_custom_call" | custom-call | flops 862322688 | bytes 7077888 | tf_op jit(solution)/shard_map/pallas_call | solution.py:147
  157.8 15.9 %all_to_all.42 = bf16[8,128,192]{1,2,0:T(8,128)(2,1)S(1)} all-to-all(bf16[8,128,192]{1,2,0:T(8,128)(2,1)} %bitcast.183), channel_id=1, replica_groups=mesh['row'=4,'seq'=8] {'seq'}, dimensions={0} | all-to-all | bytes 786432 | tf_op jit(solution)/shard_map/all_to_all | solution.py:412
  187.6 28.6 %all-gather.10.cloned.1.call-done = bf16[1024,1536]{1,0:T(8,128)(2,1)} async-done(((bf16[128,1536]{1,0:T(8,128)(2,1)}), bf16[1024,1536]{1,0:T(8,128)(2,1)}) %all-gather.10.cloned.1.call-update) | async-done | bytes 3145744 | tf_op jit(solution)/shard_map/all_gather | solution.py:429
  216.1 8.3 fusion.46
  224.4 23.0 %all-gather.16.cloned.1.call-done = bf16[512,1536]{1,0:T(8,128)(2,1)} async-done(((bf16[512,384]{1,0:T(8,128)(2,1)}), bf16[512,1536]{1,0:T(8,128)(2,1)}) %all-gather.16.cloned.1.call-update) | async-done | bytes 1572880 | tf_op jit(solution)/shard_map/all_gather | solution.py:426
  247.4 40.3 %all-gather.18.cloned.1.call-done = bf16[1024,1536]{1,0:T(8,128)(2,1)} async-done(((bf16[128,1536]{1,0:T(8,128)(2,1)}), bf16[1024,1536]{1,0:T(8,128)(2,1)}) %all-gather.18.cloned.1.call-update) | async-done | bytes 3145744 | tf_op jit(solution)/shard_map/all_gather | solution.py:437
  287.7 7.3 multiply_convert_fusion.1
  296.3 4.9 convolution_convert_fusion.2
  301.3 39.4 %reduce-scatter.12.cloned.1.call-done = bf16[128,1536]{1,0:T(8,128)(2,1)} async-done(((bf16[1024,1536]{1,0:T(8,128)(2,1)}), bf16[128,1536]{1,0:T(8,128)(2,1)}) %reduce-scatter.12.cloned.1.call-update) | async-done | bytes 393232 | tf_op jit(solution)/shard_map/reduce_scatter | solution.py:445
  345.0 5.2 convolution_convert_fusion.3
  353.0 6.0 convolution_convert_fusion.1
  363.9 5.2 convolution_convert_fusion
  369.1 13.6 %all-gather.20.cloned.1.call-done = bf16[1024,1536]{1,0:T(8,128)(2,1)} async-done(((bf16[128,1536]{1,0:T(8,128)(2,1)}), bf16[1024,1536]{1,0:T(8,128)(2,1)}) %all-gather.20.cloned.1.call-update) | async-done | bytes 3145744 | tf_op jit(solution)/shard_map/all_gather | solution.py:470
  389.6 242.6 %shard_map.238 = (bf16[8,2,128,96]{3,2,1,0:T(8,128)(2,1)}, f32[2,96,1024]{2,1,0:T(8,128)}, f32[2,96,1024]{2,1,0:T(8,128)}, f32[132,8,128]{2,1,0:T(8,128)}, f32[4,768]{1,0:T(4,128)}) custom-call(s32[1]{0:T(128)} %constant.68.clone.1.refs_0_, f32[132]{0:T(256)} %reshape.212.refs_1_, f32[4]{0:T(128)} %reshape.213.refs_2_, ...), custom_call_target="tpu_custom_call" | custom-call | flops 1869742080 | bytes 9437184 | tf_op jit(solution)/shard_map/pallas_call | solution.py:282
  665.2 21.5 %all-to-all-done.1 = bf16[8,128,576]{1,2,0:T(8,128)(2,1)S(1)} async-done(((bf16[8,128,576]{1,2,0:T(8,128)(2,1)}), bf16[8,128,576]{1,2,0:T(8,128)(2,1)S(1)}, u32[]{:S(2)}, u32[]{:S(2)}) %all-to-all-start.1) | async-done | bytes 1179680 | tf_op jit(solution)/shard_map/all_to_all | solution.py:412
  697.0 4.1 convolution_add_fusion.1
  705.4 4.1 all-to-all-start.4
  709.5 4.5 fusion.21
  714.1 13.7 %reduce-scatter.22.cloned.1.call-done = f32[48,1536]{1,0:T(8,128)} async-done(((f32[192,1536]{1,0:T(8,128)}), f32[48,1536]{1,0:T(8,128)}) %reduce-scatter.22.cloned.1.call-update) | async-done | bytes 294928 | tf_op jit(solution)/shard_map/reduce_scatter | solution.py:520
  729.4 32.7 %reduce-scatter.18.cloned.1.call-done = f32[384,192]{0,1:T(8,128)} async-done(((f32[1536,192]{0,1:T(8,128)}), f32[384,192]{0,1:T(8,128)}) %reduce-scatter.18.cloned.1.call-update) | async-done | bytes 294928 | tf_op jit(solution)/shard_map/reduce_scatter | solution.py:511
  764.0 4.6 all-to-all-start.3
  769.9 36.4 %psum.14 = f32[4160]{0:T(1024)S(1)} all-reduce(f32[4160]{0:T(1024)S(1)} %concatenate.21), channel_id=1, replica_groups=mesh['row'=4,'seq'=8] {'seq'}, use_global_device_ids=true, to_apply=%region_14.15 | all-reduce | flops 4160 | bytes 33280 | tf_op jit(solution)/shard_map/psum | solution.py:557
  806.2 15.3 %psum.15 = f32[4160]{0:T(1024)S(1)} all-reduce(f32[4160]{0:T(1024)S(1)} %psum.14), channel_id=1, replica_groups=mesh['row'=4,'seq'=8] {'row'}, use_global_device_ids=true, to_apply=%region_15.16 | all-reduce | flops 4160 | bytes 33280 | tf_op jit(solution)/shard_map/psum | solution.py:557
  (190 shorter events, 128.8 us)
Async XLA Ops:
  7.2 44.5 %all-gather.8.cloned.1.call-start = ((), (), s32[]{:S(2)}) async-start(), calls=%async_computation.14 | async-start | bytes 3538944 | tf_op jit(solution)/shard_map/all_gather | solution.py:365
  10.6 171.4 %all-gather.12.cloned.1.call-start = ((), (), s32[]{:S(2)}) async-start(), calls=%async_computation.16 | async-start | bytes 1966080 | tf_op jit(solution)/shard_map/all_gather | solution.py:424
  11.3 173.4 %all-gather.14.cloned.1.call-start = ((), (), s32[]{:S(2)}) async-start(), calls=%async_computation.17 | async-start | bytes 1966080 | tf_op jit(solution)/shard_map/all_gather | solution.py:425
  12.1 204.0 %all-gather.10.cloned.1.call-start = ((), (), s32[]{:S(2)}) async-start(), calls=%async_computation.15 | async-start | bytes 3538944 | tf_op jit(solution)/shard_map/all_gather | solution.py:429
  178.9 68.5 %all-gather.16.cloned.1.call-start = ((), (), s32[]{:S(2)}) async-start(), calls=%async_computation.18 | async-start | bytes 1966080 | tf_op jit(solution)/shard_map/all_gather | solution.py:426
  179.5 108.3 %all-gather.18.cloned.1.call-start = ((), (), s32[]{:S(2)}) async-start(), calls=%async_computation.19 | async-start | bytes 3538944 | tf_op jit(solution)/shard_map/all_gather | solution.py:437
  181.5 159.2 %reduce-scatter.12.cloned.1.call-start = ((), (), s32[]{:S(2)}) async-start(), calls=%async_computation.20 | async-start | bytes 3538944 | tf_op jit(solution)/shard_map/reduce_scatter | solution.py:445
  301.3 81.5 %all-gather.20.cloned.1.call-start = ((), (), s32[]{:S(2)}) async-start(), calls=%async_computation.21 | async-start | bytes 3538944 | tf_op jit(solution)/shard_map/all_gather | solution.py:470
  345.0 312.5 %reduce-scatter.28.cloned.1.call-start = ((), (), s32[]{:S(2)}) async-start(), calls=%async_computation.29 | async-start | bytes 1966080
  352.9 306.7 %reduce-scatter.24.cloned.1.call-start = ((), (), s32[]{:S(2)}) async-start(), calls=%async_computation.27 | async-start | bytes 1966080 | tf_op jit(solution)/shard_map/reduce_scatter | solution.py:452
  360.9 300.8 %reduce-scatter.26.cloned.1.call-start = ((), (), s32[]{:S(2)}) async-start(), calls=%async_computation.28 | async-start | bytes 1966080 | tf_op jit(solution)/shard_map/reduce_scatter | solution.py:455
  361.6 326.0 %reduce-scatter.16.cloned.1.call-start = ((), (), s32[]{:S(2)}) async-start(), calls=%async_computation.23 | async-start | bytes 1474560 | tf_op jit(solution)/shard_map/reduce_scatter | solution.py:511
  637.1 64.1 %reduce-scatter.20.cloned.1.call-start = ((), (), s32[]{:S(2)}) async-start(), calls=%async_computation.25 | async-start | bytes 1474560 | tf_op jit(solution)/shard_map/reduce_scatter | solution.py:511
  640.9 86.9 %reduce-scatter.22.cloned.1.call-start = ((), (), s32[]{:S(2)}) async-start(), calls=%async_computation.26 | async-start | bytes 1474560 | tf_op jit(solution)/shard_map/reduce_scatter | solution.py:520
  647.1 115.0 %reduce-scatter.18.cloned.1.call-start = ((), (), s32[]{:S(2)}) async-start(), calls=%async_computation.24 | async-start | bytes 1474560 | tf_op jit(solution)/shard_map/reduce_scatter | solution.py:511
  651.0 177.2 %reduce-scatter.14.cloned.1.call-start = ((), (), s32[]{:S(2)}) async-start(), calls=%async_computation.22 | async-start | bytes 3538944 | tf_op jit(solution)/shard_map/reduce_scatter | solution.py:472
  653.7 33.0 %all-to-all-start.1 = ((bf16[8,128,576]{1,2,0:T(8,128)(2,1)}), bf16[8,128,576]{1,2,0:T(8,128)(2,1)S(1)}, u32[]{:S(2)}, u32[]{:S(2)}) async-start(bf16[8,128,576]{1,2,0:T(8,128)(2,1)} %pad_maximum_fusion.3), calls=%async_computation.3 | async-start | bytes 2359296 | tf_op jit(solution)/shard_map/all_to_all | solution.py:412
  689.5 15.9 %all-to-all-start.2 = ((f32[8,48,192]{2,1,0:T(8,128)}), f32[8,48,192]{2,1,0:T(8,128)S(1)}, u32[]{:S(2)}, u32[]{:S(2)}) async-start(f32[8,48,192]{2,1,0:T(8,128)} %bitcast.41), calls=%async_computation.5 | async-start | bytes 786432 | tf_op jit(solution)/shard_map/all_to_all | solution.py:512
  705.4 58.6 %all-to-all-start.4 = ((f32[8,48,192]{2,1,0:T(8,128)}), f32[8,48,192]{2,1,0:T(8,128)}, u32[]{:S(2)}, u32[]{:S(2)}) async-start(f32[8,48,192]{2,1,0:T(8,128)} %bitcast.47), calls=%async_computation.9 | async-start | bytes 786432 | tf_op jit(solution)/shard_map/all_to_all | solution.py:512
  709.5 59.1 %copy-start.11 = (f32[128,1536]{1,0:T(8,128)S(1)}, f32[128,1536]{1,0:T(8,128)}, u32[]{:S(2)}) copy-start(f32[128,1536]{1,0:T(8,128)} %get-tuple-element.88) | copy-start | bytes 2359300
  714.1 109.8 %copy-start.14 = (f32[8,48,192]{2,1,0:T(8,128)S(1)}, f32[8,48,192]{2,1,0:T(8,128)}, u32[]{:S(2)}) copy-start(f32[8,48,192]{2,1,0:T(8,128)} %copy-done.13) | copy-start | bytes 884740
  727.8 96.0 %collective-permute-start = (f32[48,1536]{1,0:T(8,128)}, f32[48,1536]{1,0:T(8,128)S(1)}, u32[]{:S(2)}, u32[]{:S(2)}) collective-permute-start(f32[48,1536]{1,0:T(8,128)} %reduce-scatter.22.cloned.1.call-done), channel_id=1, source_target_pairs={{0,0},{1,4},{2,8},{3,12},{4,16},{5,20},{6,24},{7,28},{8,1},{9,5},{... | collective-permute-start | bytes 884744 | tf_op jit(solution)/shard_map/ppermute | solution.py:531
  764.0 63.0 %all-to-all-start.3 = ((f32[8,48,192]{2,1,0:T(8,128)}), f32[8,48,192]{2,1,0:T(8,128)S(1)}, u32[]{:S(2)}, u32[]{:S(2)}) async-start(f32[8,48,192]{2,1,0:T(8,128)} %bitcast.184), calls=%async_computation.7 | async-start | bytes 786432 | tf_op jit(solution)/shard_map/all_to_all | solution.py:512
  769.8 58.4 %copy-start.4 = (f32[128,1536]{1,0:T(8,128)S(1)}, f32[128,1536]{1,0:T(8,128)}, u32[]{:S(2)}) copy-start(f32[128,1536]{1,0:T(8,128)} %copy-done.3) | copy-start | bytes 2359300
  (21 other events, 101.1 us)
Sparse Core Ops, SparseCore 0:
  10.7 40.9 all-gather.7
  53.5 29.7 all-gather.11
  85.1 30.8 all-gather.13
  179.0 37.0 all-gather.9
  217.8 29.5 all-gather.15
  249.5 38.2 all-gather.17
  301.4 39.2 reduce-scatter.11
  345.1 37.5 all-gather.19
  385.7 30.0 reduce-scatter.27
  418.6 31.1 reduce-scatter.23
  452.8 31.1 reduce-scatter.25
  637.2 27.3 reduce-scatter.15
  667.6 28.6 reduce-scatter.19
  699.1 28.6 reduce-scatter.21
  730.6 31.4 reduce-scatter.17
  764.3 46.8 reduce-scatter.13

commit v5 on v4

--- a/solution.py
+++ b/solution.py
@@ -507,15 +507,18 @@
     normed_own = lax.dynamic_slice_in_dim(normed_all, q0, span, 0)
     rows_per_dev = width // (row_count * seq_count)
 
-    def finish_in(partial):
-        red = lax.psum_scatter(partial, "row", scatter_dimension=0, tiled=True)
-        got = lax.all_to_all(red, "seq", 0, 0, tiled=True)
-        got = got.reshape(groups, splits, rows_per_dev, pw).sum(axis=1)
-        return jnp.transpose(got, (1, 0, 2)).reshape(rows_per_dev, width)
-
-    grad_w_query = finish_in(contract_rows(normed_own, grad_q_own))
-    grad_w_key = finish_in(contract_rows(normed_own, grad_k_own))
-    grad_w_value = finish_in(contract_rows(normed_own, grad_v_own))
+    partials = jnp.stack(
+        [
+            contract_rows(normed_own, grad_q_own),
+            contract_rows(normed_own, grad_k_own),
+            contract_rows(normed_own, grad_v_own),
+        ]
+    )
+    red = lax.psum_scatter(partials, "row", scatter_dimension=1, tiled=True)
+    got = lax.all_to_all(red, "seq", 1, 1, tiled=True)
+    got = got.reshape(3, groups, splits, rows_per_dev, pw).sum(axis=2)
+    got = jnp.transpose(got, (0, 2, 1, 3)).reshape(3, rows_per_dev, width)
+    grad_w_query, grad_w_key, grad_w_value = got[0], got[1], got[2]
 
     red_out = lax.psum_scatter(grad_out_part, "row", scatter_dimension=0, tiled=True)
     red_out = red_out.reshape(splits, rows_per_dev, width)
@@ -551,16 +554,14 @@
     mix_full = lax.dynamic_update_slice_in_dim(
         jnp.zeros((groups, 2, 2), jnp.float32), grad_mix_part[None], pair, 0
     )
-    small = jnp.concatenate(
-        [gain_attn_part, gain_ffn_part, taps_full.reshape(-1), mix_full.reshape(-1)]
-    )
-    small = lax.psum(lax.psum(small, "seq"), "row")
+    small = jnp.concatenate([taps_full.reshape(-1), mix_full.reshape(-1), gain_ffn_part])
+    small = jnp.sum(lax.all_gather(small, ("row", "seq"), axis=0, tiled=False), axis=0)
     gain_rows = width // (row_count * seq_count)
     gain_at = (row_index * seq_count + seq_index) * gain_rows
-    grad_gain_attn = lax.dynamic_slice_in_dim(small, gain_at, gain_rows, 0)
-    grad_gain_ffn = lax.dynamic_slice_in_dim(small, width + gain_at, gain_rows, 0)
-    grad_taps = small[2 * width : 2 * width + HEADS * TAPS].reshape(HEADS, QCONV, KCONV)
-    grad_mix = small[2 * width + HEADS * TAPS :].reshape(groups, 2, 2)
+    grad_taps = small[: HEADS * TAPS].reshape(HEADS, QCONV, KCONV)
+    grad_mix = small[HEADS * TAPS : HEADS * TAPS + groups * 4].reshape(groups, 2, 2)
+    grad_gain_ffn = lax.dynamic_slice_in_dim(small, HEADS * TAPS + groups * 4 + gain_at, gain_rows, 0)
+    grad_gain_attn = lax.psum_scatter(gain_attn_part, ("row", "seq"), scatter_dimension=0, tiled=True)
     return (
         outputs.reshape(row_dev, blk, width),
         grad_inputs.reshape(row_dev, blk, width),

time: 847 us -> 936 us (1.11)
  the two profiles are of different devices: /device:TPU:0 before, /device:TPU:2 now
where the time goes in v5:
time: 936 us; the launch traced here: 927 us
  waiting for transfers between devices  345 us (37%)
  Pallas kernels  323 us (35%)
  blocking collectives  75 us (8%)
  matrix products  72.9 us (8%)
  local copies, waits for them, and re-layouts  55.6 us (6%)
  other arithmetic  29.8 us (3%)
  between operations  14.6 us (2%)
  starting transfers between devices  11.5 us (1%)
    pallas_call x1, Pallas kernels, attention_backward(): pl.pallas_call(lambda *refs: bwd_kernel(*refs, nw=nw, length=length, nb=n...  242 us
    unnamed x17, waiting for transfers between devices  112 us
    pallas_call x1, Pallas kernels, attention_forward(): pl.pallas_call(lambda *refs: fwd_kernel(*refs, nw=nw, length=length), gri...  80.3 us
    unnamed x1, blocking collectives  59.1 us
    reduce_scatter x1, waiting for transfers between devices, shards_body(): red = lax.psum_scatter(partials, 'row', scatter_dimension=1, tiled=True)  40.6 us
    all_gather x1, waiting for transfers between devices, shards_body(): cot_rows = lax.all_gather(cot_low, 'seq', axis=0, tiled=True)  40.3 us
    reduce_scatter x1, waiting for transfers between devices, shards_body(): lax.psum_scatter(contract_cols(grad_joint, joint).astype(jnp.bfloat16), '...  39.4 us
    all_gather x1, waiting for transfers between devices, shards_body(): normed_all = lax.all_gather(normed, 'seq', axis=0, tiled=True)  35.2 us
  transfers between devices with their start and end apart: 18, of which 9 were waited for; matrix products, arithmetic and copies ran while one was open for 14% of the time, Pallas kernels for 35%

profile of v5, /device:TPU:2, one launch (start us, length us, event | category | flops | bytes accessed | tf_op | source)
XLA Modules:
  0.0 926.8 jit_solution(1014354061510277009)
XLA Ops:
  15.0 35.2 %all-gather.9.cloned.1.call-done = bf16[1024,1536]{1,0:T(8,128)(2,1)} async-done(((bf16[128,1536]{1,0:T(8,128)(2,1)}), bf16[1024,1536]{1,0:T(8,128)(2,1)}) %all-gather.9.cloned.1.call-update) | async-done | bytes 3145744 | tf_op jit(solution)/shard_map/all_gather | solution.py:365
  50.2 3.8 fusion.2
  73.9 80.3 %shard_map.237 = (bf16[8,2,128,96]{3,2,1,0:T(8,128)(2,1)}, f32[8,2,128,768]{3,2,1,0:T(8,128)}) custom-call(s32[1]{0:T(128)} %constant.69.clone.1.refs_0_, f32[132]{0:T(256)} %reshape.195.refs_1_, f32[4]{0:T(128)} %reshape.196.refs_2_, bf16[8,2,136,96]{3,2,1,0:T(8,128)(2,1)} %copy.107.refs_3_, bf16[2,1024,96]{2,1,0:T(8,128)(2,1)} %bitcast.177, ...), custom_call_target="tpu_custom_call" | custom-call | flops 862322688 | bytes 7077888 | tf_op jit(solution)/shard_map/pallas_call | solution.py:147
  156.2 15.9 %all_to_all.20 = bf16[8,128,192]{1,2,0:T(8,128)(2,1)S(1)} all-to-all(bf16[8,128,192]{1,2,0:T(8,128)(2,1)} %bitcast.193), channel_id=1, replica_groups=mesh['row'=4,'seq'=8] {'seq'}, dimensions={0} | all-to-all | bytes 786432 | tf_op jit(solution)/shard_map/all_to_all | solution.py:412
  186.0 28.6 %all-gather.11.cloned.1.call-done = bf16[1024,1536]{1,0:T(8,128)(2,1)} async-done(((bf16[128,1536]{1,0:T(8,128)(2,1)}), bf16[1024,1536]{1,0:T(8,128)(2,1)}) %all-gather.11.cloned.1.call-update) | async-done | bytes 3145744 | tf_op jit(solution)/shard_map/all_gather | solution.py:429
  214.6 8.3 fusion.45
  222.9 23.0 %all-gather.17.cloned.1.call-done = bf16[512,1536]{1,0:T(8,128)(2,1)} async-done(((bf16[512,384]{1,0:T(8,128)(2,1)}), bf16[512,1536]{1,0:T(8,128)(2,1)}) %all-gather.17.cloned.1.call-update) | async-done | bytes 1572880 | tf_op jit(solution)/shard_map/all_gather | solution.py:426
  245.9 40.3 %all-gather.19.cloned.1.call-done = bf16[1024,1536]{1,0:T(8,128)(2,1)} async-done(((bf16[128,1536]{1,0:T(8,128)(2,1)}), bf16[1024,1536]{1,0:T(8,128)(2,1)}) %all-gather.19.cloned.1.call-update) | async-done | bytes 3145744 | tf_op jit(solution)/shard_map/all_gather | solution.py:437
  286.2 7.3 multiply_convert_fusion.1
  294.8 5.1 convolution_convert_fusion.2
  299.9 39.4 %reduce-scatter.10.cloned.1.call-done = bf16[128,1536]{1,0:T(8,128)(2,1)} async-done(((bf16[1024,1536]{1,0:T(8,128)(2,1)}), bf16[128,1536]{1,0:T(8,128)(2,1)}) %reduce-scatter.10.cloned.1.call-update) | async-done | bytes 393232 | tf_op jit(solution)/shard_map/reduce_scatter | solution.py:445
  343.7 5.2 convolution_convert_fusion.3
  351.6 6.0 convolution_convert_fusion.1
  362.5 5.3 convolution_convert_fusion
  367.8 13.4 %all-gather.21.cloned.1.call-done = bf16[1024,1536]{1,0:T(8,128)(2,1)} async-done(((bf16[128,1536]{1,0:T(8,128)(2,1)}), bf16[1024,1536]{1,0:T(8,128)(2,1)}) %all-gather.21.cloned.1.call-update) | async-done | bytes 3145744 | tf_op jit(solution)/shard_map/all_gather | solution.py:470
  388.2 242.4 %shard_map.238 = (bf16[8,2,128,96]{3,2,1,0:T(8,128)(2,1)}, f32[2,96,1024]{2,1,0:T(8,128)}, f32[2,96,1024]{2,1,0:T(8,128)}, f32[132,8,128]{2,1,0:T(8,128)}, f32[4,768]{1,0:T(4,128)}) custom-call(s32[1]{0:T(128)} %constant.69.clone.1.refs_0_, f32[132]{0:T(256)} %reshape.195.refs_1_, f32[4]{0:T(128)} %reshape.196.refs_2_, ...), custom_call_target="tpu_custom_call" | custom-call | flops 1869742080 | bytes 9437184 | tf_op jit(solution)/shard_map/pallas_call | solution.py:282
  655.6 3.6 all-to-all-start.1
  665.3 108.6 %all-reduce.6.cloned.1.call-done = f32[83968]{0:T(1024)} async-done(((f32[83968]{0:T(1024)}), f32[83968]{0:T(1024)}) %all-reduce.6.cloned.1.call-update) | async-done | bytes 335888
  778.3 4.6 fusion.46
  784.6 40.6 %reduce-scatter.14.cloned.1.call-done = f32[3,384,192]{1,2,0:T(8,128)} async-done(((f32[3,1536,192]{1,2,0:T(8,128)}), f32[3,384,192]{1,2,0:T(8,128)}) %reduce-scatter.14.cloned.1.call-update) | async-done | bytes 884752 | tf_op jit(solution)/shard_map/reduce_scatter | solution.py:517
  827.7 4.6 all-to-all-start.2
  832.3 5.1 fusion.21
  837.5 59.1 %all-reduce.3 = f32[1536]{0:T(1024)S(1)} all-reduce(f32[1536]{0:T(1024)S(1)} %get-tuple-element.96), channel_id=7, replica_groups=mesh['row'=4,'seq'=8] {'row','seq'}, use_global_device_ids=true, to_apply=%region_9.10.clone | all-reduce | flops 1536 | bytes 12288
  901.6 12.2 %collective-permute-done = f32[48,1536]{1,0:T(8,128)S(1)} collective-permute-done((f32[48,1536]{1,0:T(8,128)}, f32[48,1536]{1,0:T(8,128)S(1)}, u32[]{:S(2)}, u32[]{:S(2)}) %collective-permute-start) | collective-permute-done | bytes 294944 | tf_op jit(solution)/shard_map/ppermute | solution.py:534
  (185 shorter events, 114.6 us)
Async XLA Ops:
  7.2 43.0 %all-gather.9.cloned.1.call-start = ((), (), s32[]{:S(2)}) async-start(), calls=%async_computation.10 | async-start | bytes 3538944 | tf_op jit(solution)/shard_map/all_gather | solution.py:365
  10.6 169.9 %all-gather.13.cloned.1.call-start = ((), (), s32[]{:S(2)}) async-start(), calls=%async_computation.12 | async-start | bytes 1966080 | tf_op jit(solution)/shard_map/all_gather | solution.py:424
  11.3 171.8 %all-gather.15.cloned.1.call-start = ((), (), s32[]{:S(2)}) async-start(), calls=%async_computation.13 | async-start | bytes 1966080 | tf_op jit(solution)/shard_map/all_gather | solution.py:425
  12.1 202.5 %all-gather.11.cloned.1.call-start = ((), (), s32[]{:S(2)}) async-start(), calls=%async_computation.11 | async-start | bytes 3538944 | tf_op jit(solution)/shard_map/all_gather | solution.py:429
  50.2 6.4 copy-start.2
  177.4 68.5 %all-gather.17.cloned.1.call-start = ((), (), s32[]{:S(2)}) async-start(), calls=%async_computation.14 | async-start | bytes 1966080 | tf_op jit(solution)/shard_map/all_gather | solution.py:426
  178.0 108.3 %all-gather.19.cloned.1.call-start = ((), (), s32[]{:S(2)}) async-start(), calls=%async_computation.15 | async-start | bytes 3538944 | tf_op jit(solution)/shard_map/all_gather | solution.py:437
  179.9 159.4 %reduce-scatter.10.cloned.1.call-start = ((), (), s32[]{:S(2)}) async-start(), calls=%async_computation.16 | async-start | bytes 3538944 | tf_op jit(solution)/shard_map/reduce_scatter | solution.py:445
  286.2 8.6 copy-start.13
  299.9 81.4 %all-gather.21.cloned.1.call-start = ((), (), s32[]{:S(2)}) async-start(), calls=%async_computation.17 | async-start | bytes 3538944 | tf_op jit(solution)/shard_map/all_gather | solution.py:470
  343.6 315.5 %reduce-scatter.22.cloned.1.call-start = ((), (), s32[]{:S(2)}) async-start(), calls=%async_computation.24 | async-start | bytes 1966080
  351.5 309.8 %reduce-scatter.18.cloned.1.call-start = ((), (), s32[]{:S(2)}) async-start(), calls=%async_computation.21 | async-start | bytes 1966080 | tf_op jit(solution)/shard_map/reduce_scatter | solution.py:452
  359.5 303.9 %reduce-scatter.20.cloned.1.call-start = ((), (), s32[]{:S(2)}) async-start(), calls=%async_computation.22 | async-start | bytes 1966080 | tf_op jit(solution)/shard_map/reduce_scatter | solution.py:455
  360.2 413.8 %all-reduce.6.cloned.1.call-start = ((), (), s32[]{:S(2)}) async-start(), calls=%async_computation.23 | async-start | bytes 671744
  641.0 184.2 %reduce-scatter.14.cloned.1.call-start = ((), (), s32[]{:S(2)}) async-start(), calls=%async_computation.19 | async-start | bytes 4423680 | tf_op jit(solution)/shard_map/reduce_scatter | solution.py:517
  647.8 249.3 %reduce-scatter.16.cloned.1.call-start = ((), (), s32[]{:S(2)}) async-start(), calls=%async_computation.20 | async-start | bytes 1474560 | tf_op jit(solution)/shard_map/reduce_scatter | solution.py:523
  652.9 260.9 %reduce-scatter.12.cloned.1.call-start = ((), (), s32[]{:S(2)}) async-start(), calls=%async_computation.18 | async-start | bytes 3538944 | tf_op jit(solution)/shard_map/reduce_scatter | solution.py:472
  655.6 121.9 %all-to-all-start.1 = ((bf16[8,128,576]{1,2,0:T(8,128)(2,1)}), bf16[8,128,576]{1,2,0:T(8,128)(2,1)S(1)}, u32[]{:S(2)}, u32[]{:S(2)}) async-start(bf16[8,128,576]{1,2,0:T(8,128)(2,1)} %pad_maximum_fusion.4), calls=%async_computation.3 | async-start | bytes 2359296 | tf_op jit(solution)/shard_map/all_to_all | solution.py:412
  661.3 121.6 %slice-start = ((s8[4718592]{0:T(1024)(128)(4,1)}), s8[524288]{0:T(1024)(128)(4,1)S(1)}, s32[]{:S(2)}) async-start(s8[4718592]{0:T(1024)(128)(4,1)} %bitcast.165), calls=%async_computation.25 | async-start | bytes 1048576
  784.6 47.7 %copy-start.5 = (f32[1,128,1536]{2,1,0:T(8,128)S(1)}, f32[1,128,1536]{2,1,0:T(8,128)}, u32[]{:S(2)}) copy-start(f32[1,128,1536]{2,1,0:T(8,128)} %param.14) | copy-start | bytes 2359300
  784.6 47.7 %copy-start.15 = (f32[1536]{0:T(1024)S(1)}, f32[1536]{0:T(1024)}, u32[]{:S(2)}) copy-start(f32[1536]{0:T(1024)} %param.20) | copy-start | bytes 18436
  827.7 88.0 %all-to-all-start.2 = ((f32[3,384,192]{2,0,1:T(4,128)}), f32[3,384,192]{2,0,1:T(4,128)S(1)}, u32[]{:S(2)}, u32[]{:S(2)}) async-start(f32[3,384,192]{2,0,1:T(4,128)} %copy.121), calls=%async_computation.5 | async-start | bytes 3145728 | tf_op jit(solution)/shard_map/all_to_all | solution.py:518
  837.5 76.3 %copy-start.4 = (f32[128,1536]{1,0:T(8,128)S(1)}, f32[128,1536]{1,0:T(8,128)}, u32[]{:S(2)}) copy-start(f32[128,1536]{1,0:T(8,128)} %copy-done.3) | copy-start | bytes 2359300
  897.1 16.6 %collective-permute-start = (f32[48,1536]{1,0:T(8,128)}, f32[48,1536]{1,0:T(8,128)S(1)}, u32[]{:S(2)}, u32[]{:S(2)}) collective-permute-start(f32[48,1536]{1,0:T(8,128)} %reduce-scatter.16.cloned.1.call-done), channel_id=1, source_target_pairs={{0,0},{1,4},{2,8},{3,12},{4,16},{5,20},{6,24},{7,28},{8,1},{9,5},{... | collective-permute-start | bytes 884744 | tf_op jit(solution)/shard_map/ppermute | solution.py:534
  (16 other events, 43.1 us)
Sparse Core Ops, SparseCore 0:
  10.7 39.4 all-gather.8
  52.0 29.7 all-gather.12
  83.6 30.8 all-gather.14
  177.5 37.0 all-gather.10
  216.3 29.5 all-gather.16
  248.0 38.2 all-gather.18
  300.0 39.2 reduce-scatter.9
  343.7 37.4 all-gather.20
  384.2 30.0 reduce-scatter.21
  417.2 31.1 reduce-scatter.17
  451.3 31.1 reduce-scatter.19
  641.2 132.7 all-reduce.5
  777.1 48.1 reduce-scatter.13
  828.0 28.7 reduce-scatter.15
  859.0 42.4 reduce-scatter.11

commit v6 on v5

--- a/solution.py
+++ b/solution.py
@@ -48,41 +48,39 @@
 
 def tap_accumulate(sh_ref, acc_ref, taps_ref, head, width):
     cw = 256 if (width // 128) % 2 == 0 else 128
-    ncols = width // cw
-
-    def body(idx, carry):
-        r0 = pl.multiple_of((idx // ncols) * 8, 8)
-        c0 = pl.multiple_of((idx % ncols) * cw, cw)
-        tiles = [sh_ref[b, pl.ds(r0, 8), pl.ds(c0, cw)] for b in range(KCONV)]
-        for a in range(QCONV):
-            base = head * TAPS + a * KCONV
-            total = taps_ref[base] * tiles[0]
-            for b in range(1, KCONV):
-                total = total + taps_ref[base + b] * tiles[b]
-            acc_ref[a, pl.ds(r0, 8), pl.ds(c0, cw)] = total
+
+    def body(chunk, carry):
+        r0 = pl.multiple_of(chunk * 8, 8)
+        for c0 in range(0, width, cw):
+            tiles = [sh_ref[b, pl.ds(r0, 8), pl.ds(c0, cw)] for b in range(KCONV)]
+            for a in range(QCONV):
+                base = head * TAPS + a * KCONV
+                total = taps_ref[base] * tiles[0]
+                for b in range(1, KCONV):
+                    total = total + taps_ref[base + b] * tiles[b]
+                acc_ref[a, pl.ds(r0, 8), pl.ds(c0, cw)] = total
         return carry
 
-    lax.fori_loop(0, (EXT // 8) * ncols, body, 0)
+    lax.fori_loop(0, EXT // 8, body, 0)
 
 
 def tap_products(sh_ref, g_ref, width):
-    ncols = width // 128
     sums = {}
     for a0 in range(0, QCONV, 2):
 
-        def body(idx, accs):
-            r0 = pl.multiple_of((idx // ncols) * 8, 8)
-            c0 = pl.multiple_of((idx % ncols) * 128, 128)
-            ga = [g_ref[a0 + k, pl.ds(r0, 8), pl.ds(c0, 128)] for k in range(2)]
+        def body(chunk, accs):
+            r0 = pl.multiple_of(chunk * 8, 8)
             out = list(accs)
-            for b in range(KCONV):
-                tile = sh_ref[b, pl.ds(r0, 8), pl.ds(c0, 128)]
-                for k in range(2):
-                    out[k * KCONV + b] = out[k * KCONV + b] + ga[k] * tile
+            for c0 in range(0, width, 128):
+                ga = [g_ref[a0 + k, pl.ds(r0, 8), pl.ds(c0, 128)] for k in range(2)]
+                for b in range(KCONV):
+                    tile = sh_ref[b, pl.ds(r0, 8), pl.ds(c0, 128)]
+                    for k in range(2):
+                        out[k * KCONV + b] = out[k * KCONV + b] + ga[k] * tile
             return tuple(out)
 
         start = tuple(jnp.zeros((8, 128), jnp.float32) for _ in range(2 * KCONV))
-        res = lax.fori_loop(0, (EXT // 8) * ncols, body, start)
+        res = lax.fori_loop(0, EXT // 8, body, start)
         for k in range(2):
             for b in range(KCONV):
                 sums[(a0 + k, b)] = res[k * KCONV + b]
@@ -554,14 +552,16 @@
     mix_full = lax.dynamic_update_slice_in_dim(
         jnp.zeros((groups, 2, 2), jnp.float32), grad_mix_part[None], pair, 0
     )
-    small = jnp.concatenate([taps_full.reshape(-1), mix_full.reshape(-1), gain_ffn_part])
-    small = jnp.sum(lax.all_gather(small, ("row", "seq"), axis=0, tiled=False), axis=0)
+    small = jnp.concatenate(
+        [gain_attn_part, gain_ffn_part, taps_full.reshape(-1), mix_full.reshape(-1)]
+    )
+    small = lax.psum(small, ("row", "seq"))
     gain_rows = width // (row_count * seq_count)
     gain_at = (row_index * seq_count + seq_index) * gain_rows
-    grad_taps = small[: HEADS * TAPS].reshape(HEADS, QCONV, KCONV)
-    grad_mix = small[HEADS * TAPS : HEADS * TAPS + groups * 4].reshape(groups, 2, 2)
-    grad_gain_ffn = lax.dynamic_slice_in_dim(small, HEADS * TAPS + groups * 4 + gain_at, gain_rows, 0)
-    grad_gain_attn = lax.psum_scatter(gain_attn_part, ("row", "seq"), scatter_dimension=0, tiled=True)
+    grad_gain_attn = lax.dynamic_slice_in_dim(small, gain_at, gain_rows, 0)
+    grad_gain_ffn = lax.dynamic_slice_in_dim(small, width + gain_at, gain_rows, 0)
+    grad_taps = small[2 * width : 2 * width + HEADS * TAPS].reshape(HEADS, QCONV, KCONV)
+    grad_mix = small[2 * width + HEADS * TAPS :].reshape(groups, 2, 2)
     return (
         outputs.reshape(row_dev, blk, width),
         grad_inputs.reshape(row_dev, blk, width),

time: 936 us -> 674 us (0.72)
  the two profiles are of different devices: /device:TPU:2 before, /device:TPU:0 now
where the time goes in v6:
time: 674 us; the launch traced here: 665 us
  waiting for transfers between devices  224 us (33%)
  Pallas kernels  196 us (29%)
  matrix products  72.2 us (11%)
  blocking collectives  67.1 us (10%)
  local copies, waits for them, and re-layouts  53.3 us (8%)
  other arithmetic  27.9 us (4%)
  between operations  14.8 us (2%)
  starting transfers between devices  9.87 us (1%)
    pallas_call x1, Pallas kernels, attention_backward(): pl.pallas_call(lambda *refs: bwd_kernel(*refs, nw=nw, length=length, nb=n...  130 us
    pallas_call x1, Pallas kernels, attention_forward(): pl.pallas_call(lambda *refs: fwd_kernel(*refs, nw=nw, length=length), gri...  65.5 us
    psum x1, blocking collectives, shards_body(): small = lax.psum(small, ('row', 'seq'))  51.2 us
    all_gather x1, waiting for transfers between devices, shards_body(): cot_rows = lax.all_gather(cot_low, 'seq', axis=0, tiled=True)  40.3 us
    reduce_scatter x1, waiting for transfers between devices, shards_body(): lax.psum_scatter(contract_cols(grad_joint, joint).astype(jnp.bfloat16), '...  39.4 us
    all_gather x1, waiting for transfers between devices, shards_body(): normed_all = lax.all_gather(normed, 'seq', axis=0, tiled=True)  36.6 us
    all_gather x1, waiting for transfers between devices, shards_body(): ffn_rows = lax.all_gather(normed_ffn, 'seq', axis=0, tiled=True)  28.8 us
    dot_general x6, matrix products, project(): return jnp.dot(values, weight, preferred_element_type=jnp.float32)  27.8 us
  transfers between devices with their start and end apart: 17, of which 8 were waited for; matrix products, arithmetic and copies ran while one was open for 19% of the time, Pallas kernels for 29%

profile of v6, /device:TPU:0, one launch (start us, length us, event | category | flops | bytes accessed | tf_op | source)
XLA Modules:
  0.0 665.0 jit_solution(14300048776990925576)
XLA Ops:
  15.1 36.6 %all-gather.8.cloned.1.call-done = bf16[1024,1536]{1,0:T(8,128)(2,1)} async-done(((bf16[128,1536]{1,0:T(8,128)(2,1)}), bf16[1024,1536]{1,0:T(8,128)(2,1)}) %all-gather.8.cloned.1.call-update) | async-done | bytes 3145744 | tf_op jit(solution)/shard_map/all_gather | solution.py:363
  51.7 3.8 fusion.2
  58.1 3.5 convolution_convert_fusion.5
  75.4 65.5 %shard_map.237 = (bf16[8,2,128,96]{3,2,1,0:T(8,128)(2,1)}, f32[8,2,128,768]{3,2,1,0:T(8,128)}) custom-call(s32[1]{0:T(128)} %constant.68.clone.1.refs_0_, f32[132]{0:T(256)} %reshape.195.refs_1_, f32[4]{0:T(128)} %reshape.196.refs_2_, bf16[8,2,136,96]{3,2,1,0:T(8,128)(2,1)} %copy.82.refs_3_, bf16[2,1024,96]{2,1,0:T(8,128)(2,1)} %bitcast.177, ...), custom_call_target="tpu_custom_call" | custom-call | flops 862322688 | bytes 7077888 | tf_op jit(solution)/shard_map/pallas_call | solution.py:145
  142.9 15.9 %all_to_all.20 = bf16[8,128,192]{1,2,0:T(8,128)(2,1)S(1)} all-to-all(bf16[8,128,192]{1,2,0:T(8,128)(2,1)} %bitcast.193), channel_id=1, replica_groups=mesh['row'=4,'seq'=8] {'seq'}, dimensions={0} | all-to-all | bytes 786432 | tf_op jit(solution)/shard_map/all_to_all | solution.py:410
  172.4 28.8 %all-gather.10.cloned.1.call-done = bf16[1024,1536]{1,0:T(8,128)(2,1)} async-done(((bf16[128,1536]{1,0:T(8,128)(2,1)}), bf16[1024,1536]{1,0:T(8,128)(2,1)}) %all-gather.10.cloned.1.call-update) | async-done | bytes 3145744 | tf_op jit(solution)/shard_map/all_gather | solution.py:427
  201.3 8.4 %fusion.46 = f32[1024,1024]{0,1:T(8,128)} fusion(bf16[1024,1536]{1,0:T(8,128)(2,1)} %all-gather.10.cloned.1.call-done, bf16[1536,1024]{1,0:T(8,128)(2,1)} %constant_dynamic-update-slice_fusion.8), kind=kOutput, calls=%fused_computation.97 | convolution fusion | flops 3221225472 | bytes 10485760 | tf_op jit(solution)/shard_map/dot_general | solution.py:26
  209.6 22.9 %all-gather.16.cloned.1.call-done = bf16[512,1536]{1,0:T(8,128)(2,1)} async-done(((bf16[512,384]{1,0:T(8,128)(2,1)}), bf16[512,1536]{1,0:T(8,128)(2,1)}) %all-gather.16.cloned.1.call-update) | async-done | bytes 1572880 | tf_op jit(solution)/shard_map/all_gather | solution.py:424
  232.6 40.3 %all-gather.18.cloned.1.call-done = bf16[1024,1536]{1,0:T(8,128)(2,1)} async-done(((bf16[128,1536]{1,0:T(8,128)(2,1)}), bf16[1024,1536]{1,0:T(8,128)(2,1)}) %all-gather.18.cloned.1.call-update) | async-done | bytes 3145744 | tf_op jit(solution)/shard_map/all_gather | solution.py:435
  272.9 7.3 %multiply_convert_fusion.1 = (bf16[1024,512]{0,1:T(8,128)(2,1)S(1)}, bf16[1024,512]{0,1:T(8,128)(2,1)S(1)}, bf16[1024,512]{0,1:T(8,128)(2,1)}) fusion(f32[1024,1024]{0,1:T(8,128)} %fusion.46, bf16[1024,1536]{1,0:T(8,128)(2,1)} %all-gather.18.cloned.1.call-done, bf16[512,1536]{1,0:T(8,128)(2,1)} %all-gather.16.cloned.1.call-done), kind=kOutput, calls=%fused_computation.16 | convolution fusion | flops 1619001344 | bytes 12058624 | tf_op jit(solution)/shard_map/dot_general | solution.py:36
  281.5 5.0 convolution_convert_fusion.2
  286.6 39.4 %reduce-scatter.10.cloned.1.call-done = bf16[128,1536]{1,0:T(8,128)(2,1)} async-done(((bf16[1024,1536]{1,0:T(8,128)(2,1)}), bf16[128,1536]{1,0:T(8,128)(2,1)}) %reduce-scatter.10.cloned.1.call-update) | async-done | bytes 393232 | tf_op jit(solution)/shard_map/reduce_scatter | solution.py:443
  330.3 5.2 convolution_convert_fusion.3
  338.2 6.0 convolution_convert_fusion.1
  348.9 5.3 convolution_convert_fusion
  354.2 13.6 %all-gather.20.cloned.1.call-done = bf16[1024,1536]{1,0:T(8,128)(2,1)} async-done(((bf16[128,1536]{1,0:T(8,128)(2,1)}), bf16[1024,1536]{1,0:T(8,128)(2,1)}) %all-gather.20.cloned.1.call-update) | async-done | bytes 3145744 | tf_op jit(solution)/shard_map/all_gather | solution.py:468
  374.7 130.1 %shard_map.238 = (bf16[8,2,128,96]{3,2,1,0:T(8,128)(2,1)}, f32[2,96,1024]{2,1,0:T(8,128)}, f32[2,96,1024]{2,1,0:T(8,128)}, f32[132,8,128]{2,1,0:T(8,128)}, f32[4,768]{1,0:T(4,128)}) custom-call(s32[1]{0:T(128)} %constant.68.clone.1.refs_0_, f32[132]{0:T(256)} %reshape.195.refs_1_, f32[4]{0:T(128)} %reshape.196.refs_2_, ...), custom_call_target="tpu_custom_call" | custom-call | flops 1869742080 | bytes 9437184 | tf_op jit(solution)/shard_map/pallas_call | solution.py:280
  524.2 3.9 all-to-all-start.1
  536.0 21.5 %all-to-all-done.1 = bf16[8,128,576]{1,2,0:T(8,128)(2,1)S(1)} async-done(((bf16[8,128,576]{1,2,0:T(8,128)(2,1)}), bf16[8,128,576]{1,2,0:T(8,128)(2,1)S(1)}, u32[]{:S(2)}, u32[]{:S(2)}) %all-to-all-start.1) | async-done | bytes 1179680 | tf_op jit(solution)/shard_map/all_to_all | solution.py:410
  558.3 4.7 fusion.47
  567.3 3.6 all-to-all-start.2
  570.9 5.3 fusion.21
  576.2 17.7 %reduce-scatter.16.cloned.1.call-done = f32[48,1536]{1,0:T(8,128)} async-done(((f32[192,1536]{1,0:T(8,128)}), f32[48,1536]{1,0:T(8,128)}) %reduce-scatter.16.cloned.1.call-update) | async-done | bytes 294928 | tf_op jit(solution)/shard_map/reduce_scatter | solution.py:521
  598.2 51.2 %psum.7 = f32[4160]{0:T(1024)S(1)} all-reduce(f32[4160]{0:T(1024)S(1)} %concatenate.21), channel_id=1, replica_groups=mesh['row'=4,'seq'=8] {'row','seq'}, use_global_device_ids=true, to_apply=%region_12.13 | all-reduce | flops 4160 | bytes 33280 | tf_op jit(solution)/shard_map/psum | solution.py:558
  (181 shorter events, 104.8 us)
Async XLA Ops:
  7.2 44.5 %all-gather.8.cloned.1.call-start = ((), (), s32[]{:S(2)}) async-start(), calls=%async_computation.10 | async-start | bytes 3538944 | tf_op jit(solution)/shard_map/all_gather | solution.py:363
  10.6 156.3 %all-gather.12.cloned.1.call-start = ((), (), s32[]{:S(2)}) async-start(), calls=%async_computation.12 | async-start | bytes 1966080 | tf_op jit(solution)/shard_map/all_gather | solution.py:422
  11.3 158.3 %all-gather.14.cloned.1.call-start = ((), (), s32[]{:S(2)}) async-start(), calls=%async_computation.13 | async-start | bytes 1966080 | tf_op jit(solution)/shard_map/all_gather | solution.py:423
  12.1 189.2 %all-gather.10.cloned.1.call-start = ((), (), s32[]{:S(2)}) async-start(), calls=%async_computation.11 | async-start | bytes 3538944 | tf_op jit(solution)/shard_map/all_gather | solution.py:427
  51.7 6.4 copy-start.2
  164.1 68.5 %all-gather.16.cloned.1.call-start = ((), (), s32[]{:S(2)}) async-start(), calls=%async_computation.14 | async-start | bytes 1966080 | tf_op jit(solution)/shard_map/all_gather | solution.py:424
  164.6 108.2 %all-gather.18.cloned.1.call-start = ((), (), s32[]{:S(2)}) async-start(), calls=%async_computation.15 | async-start | bytes 3538944 | tf_op jit(solution)/shard_map/all_gather | solution.py:435
  166.6 159.3 %reduce-scatter.10.cloned.1.call-start = ((), (), s32[]{:S(2)}) async-start(), calls=%async_computation.16 | async-start | bytes 3538944 | tf_op jit(solution)/shard_map/reduce_scatter | solution.py:443
  272.9 8.6 %copy-start.13 = (bf16[1536,1024]{1,0:T(8,128)(2,1)S(1)}, bf16[1536,1024]{1,0:T(8,128)(2,1)}, u32[]{:S(2)}) copy-start(bf16[1536,1024]{1,0:T(8,128)(2,1)} %constant_dynamic-update-slice_fusion.8) | copy-start | bytes 9437188
  286.5 81.3 %all-gather.20.cloned.1.call-start = ((), (), s32[]{:S(2)}) async-start(), calls=%async_computation.17 | async-start | bytes 3538944 | tf_op jit(solution)/shard_map/all_gather | solution.py:468
  330.3 197.9 %reduce-scatter.22.cloned.1.call-start = ((), (), s32[]{:S(2)}) async-start(), calls=%async_computation.23 | async-start | bytes 1966080
  338.1 192.2 %reduce-scatter.18.cloned.1.call-start = ((), (), s32[]{:S(2)}) async-start(), calls=%async_computation.21 | async-start | bytes 1966080 | tf_op jit(solution)/shard_map/reduce_scatter | solution.py:450
  346.0 186.3 %reduce-scatter.20.cloned.1.call-start = ((), (), s32[]{:S(2)}) async-start(), calls=%async_computation.22 | async-start | bytes 1966080 | tf_op jit(solution)/shard_map/reduce_scatter | solution.py:453
  346.8 217.9 %reduce-scatter.14.cloned.1.call-start = ((), (), s32[]{:S(2)}) async-start(), calls=%async_computation.19 | async-start | bytes 4423680 | tf_op jit(solution)/shard_map/reduce_scatter | solution.py:515
  516.3 77.6 %reduce-scatter.16.cloned.1.call-start = ((), (), s32[]{:S(2)}) async-start(), calls=%async_computation.20 | async-start | bytes 1474560 | tf_op jit(solution)/shard_map/reduce_scatter | solution.py:521
  521.4 130.3 %reduce-scatter.12.cloned.1.call-start = ((), (), s32[]{:S(2)}) async-start(), calls=%async_computation.18 | async-start | bytes 3538944 | tf_op jit(solution)/shard_map/reduce_scatter | solution.py:470
  524.2 10.1 %copy-start.18 = (f32[4,768]{1,0:T(4,128)S(1)}, f32[4,768]{1,0:T(4,128)}, u32[]{:S(2)}) copy-start(f32[4,768]{1,0:T(4,128)} %get-tuple-element.30) | copy-start | bytes 36868
  524.2 10.3 %copy-start.14 = (f32[132,8,128]{2,1,0:T(8,128)S(1)}, f32[132,8,128]{2,1,0:T(8,128)}, u32[]{:S(2)}) copy-start(f32[132,8,128]{2,1,0:T(8,128)} %get-tuple-element.29) | copy-start | bytes 1622020
  524.2 38.8 %slice-start = ((s8[4718592]{0:T(1024)(128)(4,1)}), s8[524288]{0:T(1024)(128)(4,1)S(1)}, s32[]{:S(2)}) async-start(s8[4718592]{0:T(1024)(128)(4,1)} %bitcast.165), calls=%async_computation.24 | async-start | bytes 1048576
  524.2 33.2 %all-to-all-start.1 = ((bf16[8,128,576]{1,2,0:T(8,128)(2,1)}), bf16[8,128,576]{1,2,0:T(8,128)(2,1)S(1)}, u32[]{:S(2)}, u32[]{:S(2)}) async-start(bf16[8,128,576]{1,2,0:T(8,128)(2,1)} %pad_maximum_fusion.4), calls=%async_computation.3 | async-start | bytes 2359296 | tf_op jit(solution)/shard_map/all_to_all | solution.py:410
  564.6 6.3 copy-start.5
  567.3 86.4 %all-to-all-start.2 = ((f32[3,384,192]{2,0,1:T(4,128)}), f32[3,384,192]{2,0,1:T(4,128)S(1)}, u32[]{:S(2)}, u32[]{:S(2)}) async-start(f32[3,384,192]{2,0,1:T(4,128)} %copy.96), calls=%async_computation.5 | async-start | bytes 3145728 | tf_op jit(solution)/shard_map/all_to_all | solution.py:516
  576.2 75.5 %copy-start.4 = (f32[128,1536]{1,0:T(8,128)S(1)}, f32[128,1536]{1,0:T(8,128)}, u32[]{:S(2)}) copy-start(f32[128,1536]{1,0:T(8,128)} %copy-done.3) | copy-start | bytes 2359300
  594.0 57.8 %collective-permute-start = (f32[48,1536]{1,0:T(8,128)}, f32[48,1536]{1,0:T(8,128)S(1)}, u32[]{:S(2)}, u32[]{:S(2)}) collective-permute-start(f32[48,1536]{1,0:T(8,128)} %reduce-scatter.16.cloned.1.call-done), channel_id=1, source_target_pairs={{0,0},{1,4},{2,8},{3,12},{4,16},{5,20},{6,24},{7,28},{8,1},{9,5},{... | collective-permute-start | bytes 884744 | tf_op jit(solution)/shard_map/ppermute | solution.py:532
  (17 other events, 49.9 us)
Sparse Core Ops, SparseCore 0:
  10.7 40.9 all-gather.7
  53.5 29.7 all-gather.11
  85.1 30.8 all-gather.13
  164.2 37.0 all-gather.9
  202.9 29.5 all-gather.15
  234.6 38.2 all-gather.17
  286.7 39.2 reduce-scatter.9
  330.4 37.4 all-gather.19
  370.9 30.0 reduce-scatter.21
  403.8 31.1 reduce-scatter.17
  437.9 31.1 reduce-scatter.19
  516.4 45.7 reduce-scatter.13
  565.2 28.7 reduce-scatter.15
  596.1 50.5 reduce-scatter.11

commit v7 on v6

--- a/solution.py
+++ b/solution.py
@@ -419,11 +419,17 @@
     middle = flat_in + project(heads_tok, w_out)
     scale_two = rms_scale(middle)
     normed_ffn = (middle * scale_two * gain_ffn).astype(jnp.bfloat16)
-    gate_full = lax.all_gather(w_gate, "row", axis=0, tiled=True)
-    up_full = lax.all_gather(w_up, "row", axis=0, tiled=True)
-    down_full = lax.all_gather(w_down, "row", axis=1, tiled=True)
-    hid_width = gate_full.shape[1]
-    joint = jnp.concatenate([gate_full, up_full], axis=1)
+    hid_width = w_gate.shape[1]
+    packed = jnp.concatenate([w_gate, w_up, jnp.transpose(w_down)], axis=1)
+    pieces = [packed]
+    for k in range(1, row_count):
+        route = [(i, (i + k) % row_count) for i in range(row_count)]
+        pieces.append(lax.ppermute(packed, "row", route))
+    rev = jnp.stack(pieces[::-1] + pieces[::-1])
+    full_w = lax.dynamic_slice_in_dim(rev, row_count - 1 - row_index, row_count, 0)
+    full_w = full_w.reshape(row_count * packed.shape[0], packed.shape[1])
+    joint = full_w[:, : 2 * hid_width]
+    down_full = jnp.transpose(full_w[:, 2 * hid_width :])
     ffn_rows = lax.all_gather(normed_ffn, "seq", axis=0, tiled=True)
     gate_up = project(ffn_rows, joint)
     gate_vals = gate_up[:, :hid_width]
@@ -446,17 +452,17 @@
         scatter_dimension=0,
         tiled=True,
     ).astype(jnp.float32)
-    grad_w_gate, grad_w_up, grad_w_down = (
-        lax.psum_scatter(
-            grad_joint_w[:, :hid_width].astype(jnp.bfloat16), "row", scatter_dimension=0, tiled=True
-        ).astype(jnp.float32),
-        lax.psum_scatter(
-            grad_joint_w[:, hid_width:].astype(jnp.bfloat16), "row", scatter_dimension=0, tiled=True
-        ).astype(jnp.float32),
-        lax.psum_scatter(
-            grad_down_part.astype(jnp.bfloat16), "row", scatter_dimension=1, tiled=True
-        ).astype(jnp.float32),
-    )
+    grad_pack = jnp.concatenate([grad_joint_w, jnp.transpose(grad_down_part)], axis=1)
+    band = grad_pack.shape[0] // row_count
+    grad_blocks = grad_pack.reshape(row_count, band, grad_pack.shape[1]).astype(jnp.bfloat16)
+    ffn_grad = lax.dynamic_index_in_dim(grad_blocks, row_index, 0, keepdims=False).astype(jnp.float32)
+    for k in range(1, row_count):
+        route = [(i, (i + k) % row_count) for i in range(row_count)]
+        sent = lax.dynamic_index_in_dim(grad_blocks, (row_index + k) % row_count, 0, keepdims=False)
+        ffn_grad = ffn_grad + lax.ppermute(sent, "row", route).astype(jnp.float32)
+    grad_w_gate = ffn_grad[:, :hid_width]
+    grad_w_up = ffn_grad[:, hid_width : 2 * hid_width]
+    grad_w_down = jnp.transpose(ffn_grad[:, 2 * hid_width :])
     gain_ffn_part = jnp.sum(grad_normed_ffn * middle * scale_two, axis=0)
     scaled_two = grad_normed_ffn * gain_ffn
     grad_middle = (

time: 674 us -> 718 us (1.065)
  blocking collectives: 67.1 us -> 96.5 us
  local copies, waits for them, and re-layouts: 53.3 us -> 69.6 us
  waiting for transfers between devices: 224 us -> 214 us
  starting transfers between devices: 9.87 us -> 17.6 us
    ppermute x0 -> x6, waiting for transfers between devices: none -> 108 us  [the longest x3 60.1 us: shards_body(): ffn_grad = ffn_grad + lax.ppermute(sent, 'row', route).astype(jnp.float32)]
    all_gather x1, waiting for transfers between devices: 40.3 us -> 0.01 us  [shards_body(): cot_rows = lax.all_gather(cot_low, 'seq', axis=0, tiled=True)]
    psum x1, blocking collectives: 51.2 us -> 80.6 us  [shards_body(): small = lax.psum(small, ('row', 'seq'))]
    all_gather x1, waiting for transfers between devices: 28.8 us -> 0.01 us  [shards_body(): ffn_rows = lax.all_gather(normed_ffn, 'seq', axis=0, tiled=True)]
    all_gather x3 -> x0, waiting for transfers between devices: 22.9 us -> none  [the longest x1 22.9 us: shards_body(): down_full = lax.all_gather(w_down, 'row', axis=1, tiled=True)]
    all_to_all x1, waiting for transfers between devices: 21.5 us -> 0.01 us  [to_tokens(): got = lax.all_to_all(full, 'seq', 0, 0, tiled=True)]
    reduce_scatter x1, waiting for transfers between devices: 17.7 us -> 0.01 us  [shards_body(): lax.psum_scatter(grad_out_part, 'row', scatter_dimension=0, tiled=True)]
    all_gather x1, waiting for transfers between devices: 13.6 us -> 30.3 us  [shards_body(): grad_attn_all = lax.all_gather(grad_attn, 'seq', axis=0, tiled=True)]
  transfers between devices with their start and end apart: 17 -> 17, of which waited for: 8 -> 8; matrix products, arithmetic and copies ran while one was open for 19% -> 13% of each run, Pallas kernels for 29% -> 0%
where the time goes in v7:
time: 718 us; the launch traced here: 709 us
  waiting for transfers between devices  214 us (30%)
  Pallas kernels  195 us (27%)
  blocking collectives  96.5 us (13%)
  matrix products  69.8 us (10%)
  local copies, waits for them, and re-layouts  69.6 us (10%)
  other arithmetic  30.7 us (4%)
  starting transfers between devices  17.6 us (2%)
  between operations  15.2 us (2%)
    pallas_call x1, Pallas kernels, attention_backward(): pl.pallas_call(lambda *refs: bwd_kernel(*refs, nw=nw, length=length, nb=n...  130 us
    psum x1, blocking collectives, shards_body(): small = lax.psum(small, ('row', 'seq'))  80.6 us
    pallas_call x1, Pallas kernels, attention_forward(): pl.pallas_call(lambda *refs: fwd_kernel(*refs, nw=nw, length=length), gri...  65.5 us
    ppermute x3, waiting for transfers between devices, shards_body(): ffn_grad = ffn_grad + lax.ppermute(sent, 'row', route).astype(jnp.float32)  60.1 us
    ppermute x3, waiting for transfers between devices, shards_body(): pieces.append(lax.ppermute(packed, 'row', route))  48.1 us
    reduce_scatter x1, waiting for transfers between devices, shards_body(): lax.psum_scatter(contract_cols(grad_joint, joint).astype(jnp.bfloat16), '...  38 us
    all_gather x1, waiting for transfers between devices, shards_body(): normed_all = lax.all_gather(normed, 'seq', axis=0, tiled=True)  36.7 us
    all_gather x1, waiting for transfers between devices, shards_body(): grad_attn_all = lax.all_gather(grad_attn, 'seq', axis=0, tiled=True)  30.3 us
  transfers between devices with their start and end apart: 17, of which 8 were waited for; matrix products, arithmetic and copies ran while one was open for 13% of the time, Pallas kernels for 0%

profile of v7, /device:TPU:0, one launch (start us, length us, event | category | flops | bytes accessed | tf_op | source)
XLA Modules:
  0.0 708.6 jit_solution(10729192673287064537)
XLA Ops:
  15.0 36.7 %all-gather.5.cloned.1.call-done = bf16[1024,1536]{1,0:T(8,128)(2,1)} async-done(((bf16[128,1536]{1,0:T(8,128)(2,1)}), bf16[1024,1536]{1,0:T(8,128)(2,1)}) %all-gather.5.cloned.1.call-update) | async-done | bytes 3145744 | tf_op jit(solution)/shard_map/all_gather | solution.py:363
  51.7 3.6 fusion.6
  73.7 65.5 %shard_map.237 = (bf16[8,2,128,96]{3,2,1,0:T(8,128)(2,1)}, f32[8,2,128,768]{3,2,1,0:T(8,128)}) custom-call(s32[1]{0:T(128)} %constant.96.clone.1.refs_0_, f32[132]{0:T(256)} %reshape.202.refs_1_, f32[4]{0:T(128)} %reshape.203.refs_2_, bf16[8,2,136,96]{3,2,1,0:T(8,128)(2,1)} %copy.99.refs_3_, bf16[2,1024,96]{2,1,0:T(8,128)(2,1)} %bitcast.218, ...), custom_call_target="tpu_custom_call" | custom-call | flops 862322688 | bytes 7077888 | tf_op jit(solution)/shard_map/pallas_call | solution.py:145
  141.2 15.9 %all_to_all.20 = bf16[8,128,192]{1,2,0:T(8,128)(2,1)S(1)} all-to-all(bf16[8,128,192]{1,2,0:T(8,128)(2,1)} %bitcast.236), channel_id=1, replica_groups=mesh['row'=4,'seq'=8] {'seq'}, dimensions={0} | all-to-all | bytes 786432 | tf_op jit(solution)/shard_map/all_to_all | solution.py:410
  157.1 3.5 multiply_reduce_fusion
  172.4 23.4 %collective-permute-done = bf16[384,1536]{1,0:T(8,128)(2,1)} collective-permute-done((bf16[384,1536]{1,0:T(8,128)(2,1)}, bf16[384,1536]{1,0:T(8,128)(2,1)}, u32[]{:S(2)}, u32[]{:S(2)}) %collective-permute-start) | collective-permute-done | bytes 1179680 | tf_op jit(solution)/shard_map/ppermute | solution.py:427
  197.2 24.7 %collective-permute-done.1 = bf16[384,1536]{1,0:T(8,128)(2,1)} collective-permute-done((bf16[384,1536]{1,0:T(8,128)(2,1)}, bf16[384,1536]{1,0:T(8,128)(2,1)}, u32[]{:S(2)}, u32[]{:S(2)}) %collective-permute-start.1) | collective-permute-done | bytes 1179680 | tf_op jit(solution)/shard_map/ppermute | solution.py:427
  231.5 8.3 %fusion.3 = f32[1024,1024]{0,1:T(8,128)} fusion(bf16[1024,1536]{1,0:T(8,128)(2,1)} %all-gather.7.cloned.1.call-done, bf16[1536,1536]{1,0:T(8,128)(2,1)} %bitcast.206), kind=kOutput, calls=%fused_computation.9 | convolution fusion | flops 3221225472 | bytes 10485760 | tf_op jit(solution)/shard_map/dot_general | solution.py:26
  239.8 7.3 %fusion.13 = (bf16[1024,512]{0,1:T(8,128)(2,1)S(1)}, bf16[1024,512]{0,1:T(8,128)(2,1)S(1)}, bf16[1024,512]{0,1:T(8,128)(2,1)}) fusion(f32[1024,1024]{0,1:T(8,128)} %fusion.3, bf16[1024,1536]{1,0:T(8,128)(2,1)} %all-gather.9.cloned.1.call-done, bf16[1536,1536]{1,0:T(8,128)(2,1)} %bitcast.207), kind=kOutput, calls=%fused_computation.27 | convolution fusion | flops 1619001344 | bytes 12058624 | tf_op jit(solution)/shard_map/dot_general | solution.py:36
  248.5 4.9 convolution_convert_fusion.2
  253.5 38.0 %reduce-scatter.5.cloned.1.call-done = bf16[128,1536]{1,0:T(8,128)(2,1)} async-done(((bf16[1024,1536]{1,0:T(8,128)(2,1)}), bf16[128,1536]{1,0:T(8,128)(2,1)}) %reduce-scatter.5.cloned.1.call-update) | async-done | bytes 393232 | tf_op jit(solution)/shard_map/reduce_scatter | solution.py:449
  297.8 5.2 convolution_convert_fusion
  303.1 30.3 %all-gather.11.cloned.1.call-done = bf16[1024,1536]{1,0:T(8,128)(2,1)} async-done(((bf16[128,1536]{1,0:T(8,128)(2,1)}), bf16[1024,1536]{1,0:T(8,128)(2,1)}) %all-gather.11.cloned.1.call-update) | async-done | bytes 3145744 | tf_op jit(solution)/shard_map/all_gather | solution.py:474
  341.3 129.8 %shard_map.238 = (bf16[8,2,128,96]{3,2,1,0:T(8,128)(2,1)}, f32[2,96,1024]{2,1,0:T(8,128)}, f32[2,96,1024]{2,1,0:T(8,128)}, f32[132,8,128]{2,1,0:T(8,128)}, f32[4,768]{1,0:T(4,128)}) custom-call(s32[1]{0:T(128)} %constant.96.clone.1.refs_0_, f32[132]{0:T(256)} %reshape.202.refs_1_, f32[4]{0:T(128)} %reshape.203.refs_2_, ...), custom_call_target="tpu_custom_call" | custom-call | flops 1869742080 | bytes 9437184 | tf_op jit(solution)/shard_map/pallas_call | solution.py:280
  490.7 5.6 convolution_convert_fusion.1
  500.6 6.7 copy.127
  507.3 4.0 dynamic-slice_bitcast_fusion.2
  517.6 3.6 all-to-all-start.1
  521.1 29.6 %collective-permute-done.4 = bf16[384,1536]{1,0:T(8,128)(2,1)S(1)} collective-permute-done((bf16[384,1536]{1,0:T(8,128)(2,1)}, bf16[384,1536]{1,0:T(8,128)(2,1)S(1)}, u32[]{:S(2)}, u32[]{:S(2)}) %collective-permute-start.4) | collective-permute-done | bytes 1179680 | tf_op jit(solution)/shard_map/ppermute | solution.py:462
  550.7 30.1 %collective-permute-done.5 = bf16[384,1536]{1,0:T(8,128)(2,1)} collective-permute-done((bf16[384,1536]{1,0:T(8,128)(2,1)}, bf16[384,1536]{1,0:T(8,128)(2,1)}, u32[]{:S(2)}, u32[]{:S(2)}) %collective-permute-start.5) | collective-permute-done | bytes 1179680 | tf_op jit(solution)/shard_map/ppermute | solution.py:462
  589.0 4.6 fusion.60
  598.8 3.6 all-to-all-start.2
  602.5 5.1 fusion.35
  612.0 80.6 %psum.7 = f32[4160]{0:T(1024)S(1)} all-reduce(f32[4160]{0:T(1024)S(1)} %concatenate.25), channel_id=1, replica_groups=mesh['row'=4,'seq'=8] {'row','seq'}, use_global_device_ids=true, to_apply=%region_12.13 | all-reduce | flops 4160 | bytes 33280 | tf_op jit(solution)/shard_map/psum | solution.py:564
  (192 shorter events, 123.0 us)
Async XLA Ops:
  7.2 44.5 %all-gather.5.cloned.1.call-start = ((), (), s32[]{:S(2)}) async-start(), calls=%async_computation.7 | async-start | bytes 3538944 | tf_op jit(solution)/shard_map/all_gather | solution.py:363
  10.6 220.9 %all-gather.7.cloned.1.call-start = ((), (), s32[]{:S(2)}) async-start(), calls=%async_computation.8 | async-start | bytes 3538944 | tf_op jit(solution)/shard_map/all_gather | solution.py:433
  162.3 77.5 %all-gather.9.cloned.1.call-start = ((), (), s32[]{:S(2)}) async-start(), calls=%async_computation.9 | async-start | bytes 3538944 | tf_op jit(solution)/shard_map/all_gather | solution.py:441
  166.7 29.2 %collective-permute-start = (bf16[384,1536]{1,0:T(8,128)(2,1)}, bf16[384,1536]{1,0:T(8,128)(2,1)}, u32[]{:S(2)}, u32[]{:S(2)}) collective-permute-start(bf16[384,1536]{1,0:T(8,128)(2,1)} %pad_maximum_fusion.5), channel_id=1, source_target_pairs={{0,24},{8,0},{16,8},{24,16},{1,25},{9,1},{17,9},{25,17},{2,26},{10... | collective-permute-start | bytes 3538952 | tf_op jit(solution)/shard_map/ppermute | solution.py:427
  169.1 52.8 %collective-permute-start.1 = (bf16[384,1536]{1,0:T(8,128)(2,1)}, bf16[384,1536]{1,0:T(8,128)(2,1)}, u32[]{:S(2)}, u32[]{:S(2)}) collective-permute-start(bf16[384,1536]{1,0:T(8,128)(2,1)} %pad_maximum_fusion.5), channel_id=1, source_target_pairs={{0,16},{8,24},{16,0},{24,8},{1,17},{9,25},{17,1},{25,9},{2,18},{10... | collective-permute-start | bytes 3538952 | tf_op jit(solution)/shard_map/ppermute | solution.py:427
  171.6 119.9 %reduce-scatter.5.cloned.1.call-start = ((), (), s32[]{:S(2)}) async-start(), calls=%async_computation.10 | async-start | bytes 3538944 | tf_op jit(solution)/shard_map/reduce_scatter | solution.py:449
  171.6 51.6 %collective-permute-start.2 = (bf16[384,1536]{1,0:T(8,128)(2,1)}, bf16[384,1536]{1,0:T(8,128)(2,1)}, u32[]{:S(2)}, u32[]{:S(2)}) collective-permute-start(bf16[384,1536]{1,0:T(8,128)(2,1)} %pad_maximum_fusion.5), channel_id=1, source_target_pairs={{0,8},{8,16},{16,24},{24,0},{1,9},{9,17},{17,25},{25,1},{2,10},{10... | collective-permute-start | bytes 3538952 | tf_op jit(solution)/shard_map/ppermute | solution.py:427
  172.4 52.2 %copy-start.6 = (bf16[512,384]{0,1:T(8,128)(2,1)S(1)}, bf16[512,384]{0,1:T(8,128)(2,1)}, u32[]{:S(2)}) copy-start(bf16[512,384]{0,1:T(8,128)(2,1)} %copy.102) | copy-start | bytes 1179652
  172.4 52.2 %copy-start.8 = (bf16[384,512]{1,0:T(8,128)(2,1)S(1)}, bf16[384,512]{1,0:T(8,128)(2,1)}, u32[]{:S(2)}) copy-start(bf16[384,512]{1,0:T(8,128)(2,1)} %param.25) | copy-start | bytes 1179652
  172.4 52.2 %copy-start.9 = (bf16[384,512]{1,0:T(8,128)(2,1)S(1)}, bf16[384,512]{1,0:T(8,128)(2,1)}, u32[]{:S(2)}) copy-start(bf16[384,512]{1,0:T(8,128)(2,1)} %param.24) | copy-start | bytes 1179652
  253.5 79.9 %all-gather.11.cloned.1.call-start = ((), (), s32[]{:S(2)}) async-start(), calls=%async_computation.11 | async-start | bytes 3538944 | tf_op jit(solution)/shard_map/all_gather | solution.py:474
  295.8 300.4 %reduce-scatter.9.cloned.1.call-start = ((), (), s32[]{:S(2)}) async-start(), calls=%async_computation.13 | async-start | bytes 4423680 | tf_op jit(solution)/shard_map/reduce_scatter | solution.py:521
  483.4 124.2 %reduce-scatter.11.cloned.1.call-start = ((), (), s32[]{:S(2)}) async-start(), calls=%async_computation.14 | async-start | bytes 1474560 | tf_op jit(solution)/shard_map/reduce_scatter | solution.py:527
  488.5 206.4 %reduce-scatter.7.cloned.1.call-start = ((), (), s32[]{:S(2)}) async-start(), calls=%async_computation.12 | async-start | bytes 3538944 | tf_op jit(solution)/shard_map/reduce_scatter | solution.py:476
  507.3 8.9 %copy-start.11 = (bf16[2,96,1024]{2,1,0:T(8,128)(2,1)S(1)}, bf16[2,96,1024]{2,1,0:T(8,128)(2,1)}, u32[]{:S(2)}) copy-start(bf16[2,96,1024]{2,1,0:T(8,128)(2,1)} %convert_element_type.102) | copy-start | bytes 1179652
  507.3 9.0 %copy-start.10 = (bf16[2,96,1024]{2,1,0:T(8,128)(2,1)S(1)}, bf16[2,96,1024]{2,1,0:T(8,128)(2,1)}, u32[]{:S(2)}) copy-start(bf16[2,96,1024]{2,1,0:T(8,128)(2,1)} %convert_element_type.105) | copy-start | bytes 1179652
  511.3 39.5 %collective-permute-start.4 = (bf16[384,1536]{1,0:T(8,128)(2,1)}, bf16[384,1536]{1,0:T(8,128)(2,1)S(1)}, u32[]{:S(2)}, u32[]{:S(2)}) collective-permute-start(bf16[384,1536]{1,0:T(8,128)(2,1)} %get-tuple-element.91), channel_id=1, source_target_pairs={{0,8},{8,16},{16,24},{24,0},{1,9},{9,17},{17,25},{25,1},{2,10},{10... | collective-permute-start | bytes 3538952 | tf_op jit(solution)/shard_map/ppermute | solution.py:462
  513.0 67.8 %collective-permute-start.5 = (bf16[384,1536]{1,0:T(8,128)(2,1)}, bf16[384,1536]{1,0:T(8,128)(2,1)}, u32[]{:S(2)}, u32[]{:S(2)}) collective-permute-start(bf16[384,1536]{1,0:T(8,128)(2,1)} %get-tuple-element.93), channel_id=1, source_target_pairs={{0,16},{8,24},{16,0},{24,8},{1,17},{9,25},{17,1},{25,9},{2,18},{10... | collective-permute-start | bytes 3538952 | tf_op jit(solution)/shard_map/ppermute | solution.py:462
  514.6 66.6 %collective-permute-start.6 = (bf16[384,1536]{1,0:T(8,128)(2,1)}, bf16[384,1536]{1,0:T(8,128)(2,1)}, u32[]{:S(2)}, u32[]{:S(2)}) collective-permute-start(bf16[384,1536]{1,0:T(8,128)(2,1)} %get-tuple-element.92), channel_id=1, source_target_pairs={{0,24},{8,0},{16,8},{24,16},{1,25},{9,1},{17,9},{25,17},{2,26},{10... | collective-permute-start | bytes 3538952 | tf_op jit(solution)/shard_map/ppermute | solution.py:462
  517.6 70.6 %all-to-all-start.1 = ((bf16[8,128,576]{1,2,0:T(8,128)(2,1)}), bf16[8,128,576]{1,2,0:T(8,128)(2,1)S(1)}, u32[]{:S(2)}, u32[]{:S(2)}) async-start(bf16[8,128,576]{1,2,0:T(8,128)(2,1)} %pad_maximum_fusion.6), calls=%async_computation.3 | async-start | bytes 2359296 | tf_op jit(solution)/shard_map/all_to_all | solution.py:410
  583.9 9.6 %slice-start = ((s8[4718592]{0:T(1024)(128)(4,1)}), s8[524288]{0:T(1024)(128)(4,1)S(1)}, s32[]{:S(2)}) async-start(s8[4718592]{0:T(1024)(128)(4,1)} %bitcast.204), calls=%async_computation.15 | async-start | bytes 1048576
  598.8 98.1 %all-to-all-start.2 = ((f32[3,384,192]{2,0,1:T(4,128)}), f32[3,384,192]{2,0,1:T(4,128)S(1)}, u32[]{:S(2)}, u32[]{:S(2)}) async-start(f32[3,384,192]{2,0,1:T(4,128)} %copy.114), calls=%async_computation.5 | async-start | bytes 3145728 | tf_op jit(solution)/shard_map/all_to_all | solution.py:522
  607.6 87.3 %copy-start.4 = (f32[128,1536]{1,0:T(8,128)S(1)}, f32[128,1536]{1,0:T(8,128)}, u32[]{:S(2)}) copy-start(f32[128,1536]{1,0:T(8,128)} %copy-done.3) | copy-start | bytes 2359300
  607.6 87.3 %collective-permute-start.3 = (f32[48,1536]{1,0:T(8,128)}, f32[48,1536]{1,0:T(8,128)S(1)}, u32[]{:S(2)}, u32[]{:S(2)}) collective-permute-start(f32[48,1536]{1,0:T(8,128)} %reduce-scatter.11.cloned.1.call-done), channel_id=1, source_target_pairs={{0,0},{1,4},{2,8},{3,12},{4,16},{5,20},{6,24},{7,28},{8,1},{9,5},{... | collective-permute-start | bytes 884744 | tf_op jit(solution)/shard_map/ppermute | solution.py:538
  (21 other events, 98.0 us)
Sparse Core Ops, SparseCore 0:
  10.7 40.9 all-gather.4
  162.5 37.0 all-gather.6
  201.2 37.1 all-gather.8
  253.6 37.8 reduce-scatter.4
  295.9 37.4 all-gather.10
  483.6 77.6 reduce-scatter.8
  564.2 29.5 reduce-scatter.10
  596.0 73.3 reduce-scatter.6

commit v8 on v7

--- a/solution.py
+++ b/solution.py
@@ -561,7 +561,13 @@
     small = jnp.concatenate(
         [gain_attn_part, gain_ffn_part, taps_full.reshape(-1), mix_full.reshape(-1)]
     )
-    small = lax.psum(small, ("row", "seq"))
+    devices = row_count * seq_count
+    assert devices & (devices - 1) == 0
+    mask = 1
+    while mask < devices:
+        route = [(i, i ^ mask) for i in range(devices)]
+        small = small + lax.ppermute(small, ("row", "seq"), route)
+        mask *= 2
     gain_rows = width // (row_count * seq_count)
     gain_at = (row_index * seq_count + seq_index) * gain_rows
     grad_gain_attn = lax.dynamic_slice_in_dim(small, gain_at, gain_rows, 0)

time: 718 us -> 695 us (0.968)
  blocking collectives: 96.5 us -> 15.9 us
  waiting for transfers between devices: 214 us -> 261 us
    psum x1 -> x0, blocking collectives: 80.6 us -> none  [shards_body(): small = lax.psum(small, ('row', 'seq'))]
    reduce_scatter x1, waiting for transfers between devices: 0.01 us -> 57.4 us  [shards_body(): lax.psum_scatter(ffn_part, 'seq', scatter_dimension=0, tiled=True)]
    ppermute x3, waiting for transfers between devices: 60.1 us -> 44.3 us  [shards_body(): ffn_grad = ffn_grad + lax.ppermute(sent, 'row', route).astype(jnp.float32)]
    unnamed x77 -> x75, local copies, waits for them, and re-layouts: 22.6 us -> 23.4 us
  transfers between devices with their start and end apart: 17 -> 22, of which waited for: 8 -> 12; matrix products, arithmetic and copies ran while one was open for 13% -> 14% of each run, Pallas kernels for 0% -> 0%
where the time goes in v8:
time: 695 us; the launch traced here: 684 us
  waiting for transfers between devices  261 us (38%)
  Pallas kernels  195 us (28%)
  matrix products  71.8 us (10%)
  local copies, waits for them, and re-layouts  70.9 us (10%)
  other arithmetic  31.1 us (4%)
  starting transfers between devices  22.2 us (3%)
  blocking collectives  15.9 us (2%)
  between operations  15 us (2%)
    pallas_call x1, Pallas kernels, attention_backward(): pl.pallas_call(lambda *refs: bwd_kernel(*refs, nw=nw, length=length, nb=n...  130 us
    pallas_call x1, Pallas kernels, attention_forward(): pl.pallas_call(lambda *refs: fwd_kernel(*refs, nw=nw, length=length), gri...  65.5 us
    reduce_scatter x1, waiting for transfers between devices, shards_body(): lax.psum_scatter(ffn_part, 'seq', scatter_dimension=0, tiled=True)  57.4 us
    ppermute x3, waiting for transfers between devices, shards_body(): pieces.append(lax.ppermute(packed, 'row', route))  47.8 us
    ppermute x3, waiting for transfers between devices, shards_body(): ffn_grad = ffn_grad + lax.ppermute(sent, 'row', route).astype(jnp.float32)  44.3 us
    reduce_scatter x1, waiting for transfers between devices, shards_body(): lax.psum_scatter(contract_cols(grad_joint, joint).astype(jnp.bfloat16), '...  38 us
    all_gather x1, waiting for transfers between devices, shards_body(): normed_all = lax.all_gather(normed, 'seq', axis=0, tiled=True)  36.7 us
    all_gather x1, waiting for transfers between devices, shards_body(): grad_attn_all = lax.all_gather(grad_attn, 'seq', axis=0, tiled=True)  30.3 us
  transfers between devices with their start and end apart: 22, of which 12 were waited for; matrix products, arithmetic and copies ran while one was open for 14% of the time, Pallas kernels for 0%

profile of v8, /device:TPU:0, one launch (start us, length us, event | category | flops | bytes accessed | tf_op | source)
XLA Modules:
  0.0 683.6 jit_solution(3849560507227580838)
XLA Ops:
  15.0 36.7 %all-gather.5.cloned.1.call-done = bf16[1024,1536]{1,0:T(8,128)(2,1)} async-done(((bf16[128,1536]{1,0:T(8,128)(2,1)}), bf16[1024,1536]{1,0:T(8,128)(2,1)}) %all-gather.5.cloned.1.call-update) | async-done | bytes 3145744 | tf_op jit(solution)/shard_map/all_gather | solution.py:363
  73.7 65.5 %shard_map.237 = (bf16[8,2,128,96]{3,2,1,0:T(8,128)(2,1)}, f32[8,2,128,768]{3,2,1,0:T(8,128)}) custom-call(s32[1]{0:T(128)} %constant.96.clone.1.refs_0_, f32[132]{0:T(256)} %reshape.200.refs_1_, f32[4]{0:T(128)} %reshape.201.refs_2_, bf16[8,2,136,96]{3,2,1,0:T(8,128)(2,1)} %copy.99.refs_3_, bf16[2,1024,96]{2,1,0:T(8,128)(2,1)} %bitcast.216, ...), custom_call_target="tpu_custom_call" | custom-call | flops 862322688 | bytes 7077888 | tf_op jit(solution)/shard_map/pallas_call | solution.py:145
  141.2 15.9 %all_to_all.20 = bf16[8,128,192]{1,2,0:T(8,128)(2,1)S(1)} all-to-all(bf16[8,128,192]{1,2,0:T(8,128)(2,1)} %bitcast.234), channel_id=1, replica_groups=mesh['row'=4,'seq'=8] {'seq'}, dimensions={0} | all-to-all | bytes 786432 | tf_op jit(solution)/shard_map/all_to_all | solution.py:410
  172.7 23.1 %collective-permute-done = bf16[384,1536]{1,0:T(8,128)(2,1)} collective-permute-done((bf16[384,1536]{1,0:T(8,128)(2,1)}, bf16[384,1536]{1,0:T(8,128)(2,1)}, u32[]{:S(2)}, u32[]{:S(2)}) %collective-permute-start) | collective-permute-done | bytes 1179680 | tf_op jit(solution)/shard_map/ppermute | solution.py:427
  197.1 24.7 %collective-permute-done.1 = bf16[384,1536]{1,0:T(8,128)(2,1)} collective-permute-done((bf16[384,1536]{1,0:T(8,128)(2,1)}, bf16[384,1536]{1,0:T(8,128)(2,1)}, u32[]{:S(2)}, u32[]{:S(2)}) %collective-permute-start.1) | collective-permute-done | bytes 1179680 | tf_op jit(solution)/shard_map/ppermute | solution.py:427
  231.4 8.4 %fusion.3 = f32[1024,1024]{0,1:T(8,128)} fusion(bf16[1024,1536]{1,0:T(8,128)(2,1)} %all-gather.7.cloned.1.call-done, bf16[1536,1536]{1,0:T(8,128)(2,1)} %bitcast.204), kind=kOutput, calls=%fused_computation.9 | convolution fusion | flops 3221225472 | bytes 10485760 | tf_op jit(solution)/shard_map/dot_general | solution.py:26
  239.8 7.3 %fusion.13 = (bf16[1024,512]{0,1:T(8,128)(2,1)S(1)}, bf16[1024,512]{0,1:T(8,128)(2,1)S(1)}, bf16[1024,512]{0,1:T(8,128)(2,1)}) fusion(f32[1024,1024]{0,1:T(8,128)} %fusion.3, bf16[1024,1536]{1,0:T(8,128)(2,1)} %all-gather.9.cloned.1.call-done, bf16[1536,1536]{1,0:T(8,128)(2,1)} %bitcast.205), kind=kOutput, calls=%fused_computation.27 | convolution fusion | flops 1619001344 | bytes 12058624 | tf_op jit(solution)/shard_map/dot_general | solution.py:36
  248.4 5.0 convolution_convert_fusion.2
  253.4 38.0 %reduce-scatter.5.cloned.1.call-done = bf16[128,1536]{1,0:T(8,128)(2,1)} async-done(((bf16[1024,1536]{1,0:T(8,128)(2,1)}), bf16[128,1536]{1,0:T(8,128)(2,1)}) %reduce-scatter.5.cloned.1.call-update) | async-done | bytes 393232 | tf_op jit(solution)/shard_map/reduce_scatter | solution.py:449
  297.8 5.2 convolution_convert_fusion
  303.0 30.3 %all-gather.11.cloned.1.call-done = bf16[1024,1536]{1,0:T(8,128)(2,1)} async-done(((bf16[128,1536]{1,0:T(8,128)(2,1)}), bf16[1024,1536]{1,0:T(8,128)(2,1)}) %all-gather.11.cloned.1.call-update) | async-done | bytes 3145744 | tf_op jit(solution)/shard_map/all_gather | solution.py:474
  341.2 129.8 %shard_map.238 = (bf16[8,2,128,96]{3,2,1,0:T(8,128)(2,1)}, f32[2,96,1024]{2,1,0:T(8,128)}, f32[2,96,1024]{2,1,0:T(8,128)}, f32[132,8,128]{2,1,0:T(8,128)}, f32[4,768]{1,0:T(4,128)}) custom-call(s32[1]{0:T(128)} %constant.96.clone.1.refs_0_, f32[132]{0:T(256)} %reshape.200.refs_1_, f32[4]{0:T(128)} %reshape.201.refs_2_, ...), custom_call_target="tpu_custom_call" | custom-call | flops 1869742080 | bytes 9437184 | tf_op jit(solution)/shard_map/pallas_call | solution.py:280
  491.4 3.8 all-to-all-start.1
  495.2 3.8 fusion.5
  499.1 4.5 convolution_convert_fusion.1
  506.0 6.7 copy.127
  512.7 3.9 dynamic-slice_bitcast_fusion.2
  524.6 4.0 fusion.60
  528.6 4.1 convolution_add_fusion.1
  532.7 5.1 fusion.35
  539.1 14.3 %collective-permute-done.10 = bf16[384,1536]{1,0:T(8,128)(2,1)S(1)} collective-permute-done((bf16[384,1536]{1,0:T(8,128)(2,1)}, bf16[384,1536]{1,0:T(8,128)(2,1)S(1)}, u32[]{:S(2)}, u32[]{:S(2)}) %collective-permute-start.10) | collective-permute-done | bytes 1179680 | tf_op jit(solution)/shard_map/ppermute | solution.py:462
  554.5 29.7 %collective-permute-done.9 = bf16[384,1536]{1,0:T(8,128)(2,1)} collective-permute-done((bf16[384,1536]{1,0:T(8,128)(2,1)}, bf16[384,1536]{1,0:T(8,128)(2,1)}, u32[]{:S(2)}, u32[]{:S(2)}) %collective-permute-start.9) | collective-permute-done | bytes 1179680 | tf_op jit(solution)/shard_map/ppermute | solution.py:462
  592.3 4.3 all-to-all-start.2
  611.4 57.4 %reduce-scatter.7.cloned.1.call-done = bf16[128,1536]{1,0:T(8,128)(2,1)} async-done(((bf16[1024,1536]{1,0:T(8,128)(2,1)}), bf16[128,1536]{1,0:T(8,128)(2,1)}) %reduce-scatter.7.cloned.1.call-update) | async-done | bytes 393232 | tf_op jit(solution)/shard_map/reduce_scatter | solution.py:476
  (203 shorter events, 137.2 us)
Async XLA Ops:
  7.2 44.5 %all-gather.5.cloned.1.call-start = ((), (), s32[]{:S(2)}) async-start(), calls=%async_computation.7 | async-start | bytes 3538944 | tf_op jit(solution)/shard_map/all_gather | solution.py:363
  10.6 220.8 %all-gather.7.cloned.1.call-start = ((), (), s32[]{:S(2)}) async-start(), calls=%async_computation.8 | async-start | bytes 3538944 | tf_op jit(solution)/shard_map/all_gather | solution.py:433
  162.3 77.4 %all-gather.9.cloned.1.call-start = ((), (), s32[]{:S(2)}) async-start(), calls=%async_computation.9 | async-start | bytes 3538944 | tf_op jit(solution)/shard_map/all_gather | solution.py:441
  166.6 29.2 %collective-permute-start = (bf16[384,1536]{1,0:T(8,128)(2,1)}, bf16[384,1536]{1,0:T(8,128)(2,1)}, u32[]{:S(2)}, u32[]{:S(2)}) collective-permute-start(bf16[384,1536]{1,0:T(8,128)(2,1)} %pad_maximum_fusion.5), channel_id=1, source_target_pairs={{0,24},{8,0},{16,8},{24,16},{1,25},{9,1},{17,9},{25,17},{2,26},{10... | collective-permute-start | bytes 3538952 | tf_op jit(solution)/shard_map/ppermute | solution.py:427
  169.0 52.8 %collective-permute-start.1 = (bf16[384,1536]{1,0:T(8,128)(2,1)}, bf16[384,1536]{1,0:T(8,128)(2,1)}, u32[]{:S(2)}, u32[]{:S(2)}) collective-permute-start(bf16[384,1536]{1,0:T(8,128)(2,1)} %pad_maximum_fusion.5), channel_id=1, source_target_pairs={{0,16},{8,24},{16,0},{24,8},{1,17},{9,25},{17,1},{25,9},{2,18},{10... | collective-permute-start | bytes 3538952 | tf_op jit(solution)/shard_map/ppermute | solution.py:427
  171.5 119.9 %reduce-scatter.5.cloned.1.call-start = ((), (), s32[]{:S(2)}) async-start(), calls=%async_computation.10 | async-start | bytes 3538944 | tf_op jit(solution)/shard_map/reduce_scatter | solution.py:449
  171.6 51.6 %collective-permute-start.2 = (bf16[384,1536]{1,0:T(8,128)(2,1)}, bf16[384,1536]{1,0:T(8,128)(2,1)}, u32[]{:S(2)}, u32[]{:S(2)}) collective-permute-start(bf16[384,1536]{1,0:T(8,128)(2,1)} %pad_maximum_fusion.5), channel_id=1, source_target_pairs={{0,8},{8,16},{16,24},{24,0},{1,9},{9,17},{17,25},{25,1},{2,10},{10... | collective-permute-start | bytes 3538952 | tf_op jit(solution)/shard_map/ppermute | solution.py:427
  172.7 51.9 %copy-start.9 = (bf16[384,512]{1,0:T(8,128)(2,1)S(1)}, bf16[384,512]{1,0:T(8,128)(2,1)}, u32[]{:S(2)}) copy-start(bf16[384,512]{1,0:T(8,128)(2,1)} %param.24) | copy-start | bytes 1179652
  253.4 79.9 %all-gather.11.cloned.1.call-start = ((), (), s32[]{:S(2)}) async-start(), calls=%async_computation.11 | async-start | bytes 3538944 | tf_op jit(solution)/shard_map/all_gather | solution.py:474
  295.7 294.1 %reduce-scatter.9.cloned.1.call-start = ((), (), s32[]{:S(2)}) async-start(), calls=%async_computation.13 | async-start | bytes 4423680 | tf_op jit(solution)/shard_map/reduce_scatter | solution.py:521
  483.4 121.4 %reduce-scatter.11.cloned.1.call-start = ((), (), s32[]{:S(2)}) async-start(), calls=%async_computation.14 | async-start | bytes 1474560 | tf_op jit(solution)/shard_map/reduce_scatter | solution.py:527
  488.5 180.3 %reduce-scatter.7.cloned.1.call-start = ((), (), s32[]{:S(2)}) async-start(), calls=%async_computation.12 | async-start | bytes 3538944 | tf_op jit(solution)/shard_map/reduce_scatter | solution.py:476
  491.4 33.1 %all-to-all-start.1 = ((bf16[8,128,576]{1,2,0:T(8,128)(2,1)}), bf16[8,128,576]{1,2,0:T(8,128)(2,1)S(1)}, u32[]{:S(2)}, u32[]{:S(2)}) async-start(bf16[8,128,576]{1,2,0:T(8,128)(2,1)} %pad_maximum_fusion.6), calls=%async_computation.3 | async-start | bytes 2359296 | tf_op jit(solution)/shard_map/all_to_all | solution.py:410
  516.6 36.9 %collective-permute-start.10 = (bf16[384,1536]{1,0:T(8,128)(2,1)}, bf16[384,1536]{1,0:T(8,128)(2,1)S(1)}, u32[]{:S(2)}, u32[]{:S(2)}) collective-permute-start(bf16[384,1536]{1,0:T(8,128)(2,1)} %get-tuple-element.93), channel_id=1, source_target_pairs={{0,16},{8,24},{16,0},{24,8},{1,17},{9,25},{17,1},{25,9},{2,18},{10... | collective-permute-start | bytes 3538952 | tf_op jit(solution)/shard_map/ppermute | solution.py:462
  518.1 35.7 %collective-permute-start.11 = (bf16[384,1536]{1,0:T(8,128)(2,1)}, bf16[384,1536]{1,0:T(8,128)(2,1)}, u32[]{:S(2)}, u32[]{:S(2)}) collective-permute-start(bf16[384,1536]{1,0:T(8,128)(2,1)} %get-tuple-element.92), channel_id=1, source_target_pairs={{0,24},{8,0},{16,8},{24,16},{1,25},{9,1},{17,9},{25,17},{2,26},{10... | collective-permute-start | bytes 3538952 | tf_op jit(solution)/shard_map/ppermute | solution.py:462
  519.5 64.7 %collective-permute-start.9 = (bf16[384,1536]{1,0:T(8,128)(2,1)}, bf16[384,1536]{1,0:T(8,128)(2,1)}, u32[]{:S(2)}, u32[]{:S(2)}) collective-permute-start(bf16[384,1536]{1,0:T(8,128)(2,1)} %get-tuple-element.91), channel_id=1, source_target_pairs={{0,8},{8,16},{16,24},{24,0},{1,9},{9,17},{17,25},{25,1},{2,10},{10... | collective-permute-start | bytes 3538952 | tf_op jit(solution)/shard_map/ppermute | solution.py:462
  537.9 1.2 collective-permute-start.4
  539.1 48.0 %collective-permute-start.5 = (f32[4160]{0:T(1024)S(1)}, f32[4160]{0:T(1024)S(1)}, u32[]{:S(2)}, u32[]{:S(2)}) collective-permute-start(f32[4160]{0:T(1024)S(1)} %add.173), channel_id=1, source_target_pairs={{0,2},{1,3},{2,0},{3,1},{4,6},{5,7},{6,4},{7,5},{8,10},{9,11},{10,... | collective-permute-start | bytes 49928 | tf_op jit(solution)/shard_map/ppermute | solution.py:569
  587.2 13.3 %collective-permute-start.6 = (f32[4160]{0:T(1024)S(1)}, f32[4160]{0:T(1024)S(1)}, u32[]{:S(2)}, u32[]{:S(2)}) collective-permute-start(f32[4160]{0:T(1024)S(1)} %add.174), channel_id=1, source_target_pairs={{0,4},{1,5},{2,6},{3,7},{4,0},{5,1},{6,2},{7,3},{8,12},{9,13},{10,... | collective-permute-start | bytes 49928 | tf_op jit(solution)/shard_map/ppermute | solution.py:569
  592.3 78.5 %all-to-all-start.2 = ((f32[3,384,192]{2,0,1:T(4,128)}), f32[3,384,192]{2,0,1:T(4,128)}, u32[]{:S(2)}, u32[]{:S(2)}) async-start(f32[3,384,192]{2,0,1:T(4,128)} %copy.114), calls=%async_computation.5 | async-start | bytes 3145728 | tf_op jit(solution)/shard_map/all_to_all | solution.py:522
  598.1 70.7 %copy-start.4 = (f32[128,1536]{1,0:T(8,128)S(1)}, f32[128,1536]{1,0:T(8,128)}, u32[]{:S(2)}) copy-start(f32[128,1536]{1,0:T(8,128)} %copy-done.3) | copy-start | bytes 2359300
  600.4 3.8 collective-permute-start.7
  604.3 4.7 collective-permute-start.8
  604.8 6.5 collective-permute-start.3
  (25 other events, 195.3 us)
Sparse Core Ops, SparseCore 0:
  10.7 40.9 all-gather.4
  162.4 37.0 all-gather.6
  201.2 37.1 all-gather.8
  253.5 37.8 reduce-scatter.4
  295.8 37.4 all-gather.10
  483.6 54.4 reduce-scatter.8
  541.0 56.8 reduce-scatter.10
  600.2 68.5 reduce-scatter.6

commit v9 on v8

--- a/solution.py
+++ b/solution.py
@@ -46,32 +46,31 @@
     return pl.multiple_of(jnp.clip((block - nw + 1) * TQ, 0, length - nw * TQ), TQ)
 
 
-def tap_accumulate(sh_ref, acc_ref, taps_ref, head, width):
-    cw = 256 if (width // 128) % 2 == 0 else 128
-
-    def body(chunk, carry):
-        r0 = pl.multiple_of(chunk * 8, 8)
-        for c0 in range(0, width, cw):
-            tiles = [sh_ref[b, pl.ds(r0, 8), pl.ds(c0, cw)] for b in range(KCONV)]
+def tap_accumulate(sh_ref, acc_ref, taps_ref, head, live):
+
+    def body(col, carry):
+        c0 = pl.multiple_of(col * 128, 128)
+        for r0 in range(0, EXT, 8):
+            tiles = [sh_ref[b, pl.ds(r0, 8), pl.ds(c0, 128)] for b in range(KCONV)]
             for a in range(QCONV):
                 base = head * TAPS + a * KCONV
                 total = taps_ref[base] * tiles[0]
                 for b in range(1, KCONV):
                     total = total + taps_ref[base + b] * tiles[b]
-                acc_ref[a, pl.ds(r0, 8), pl.ds(c0, cw)] = total
+                acc_ref[a, pl.ds(r0, 8), pl.ds(c0, 128)] = total
         return carry
 
-    lax.fori_loop(0, EXT // 8, body, 0)
-
-
-def tap_products(sh_ref, g_ref, width):
+    lax.fori_loop(0, live, body, 0)
+
+
+def tap_products(sh_ref, g_ref, live):
     sums = {}
     for a0 in range(0, QCONV, 2):
 
-        def body(chunk, accs):
-            r0 = pl.multiple_of(chunk * 8, 8)
+        def body(col, accs):
+            c0 = pl.multiple_of(col * 128, 128)
             out = list(accs)
-            for c0 in range(0, width, 128):
+            for r0 in range(0, EXT, 8):
                 ga = [g_ref[a0 + k, pl.ds(r0, 8), pl.ds(c0, 128)] for k in range(2)]
                 for b in range(KCONV):
                     tile = sh_ref[b, pl.ds(r0, 8), pl.ds(c0, 128)]
@@ -80,11 +79,15 @@
             return tuple(out)
 
         start = tuple(jnp.zeros((8, 128), jnp.float32) for _ in range(2 * KCONV))
-        res = lax.fori_loop(0, EXT // 8, body, start)
+        res = lax.fori_loop(0, live, body, start)
         for k in range(2):
             for b in range(KCONV):
                 sums[(a0 + k, b)] = res[k * KCONV + b]
     return sums
+
+
+def live_tiles(block, kstart, nw):
+    return jnp.clip(block + 1 - kstart // TQ, 1, nw)
 
 
 def masks(block, kstart, width, rdoc_ref, kdoc_ref):
@@ -118,7 +121,7 @@
     allowed_ext, allowed_own = masks(block, kstart, width, rdoc_ref, kdoc_ref)
     for head in range(2):
         masked_shifts(q_ref, k_ref, head, kstart, width, allowed_ext, sh_ref)
-        tap_accumulate(sh_ref, acc_ref, taps_ref, head, width)
+        tap_accumulate(sh_ref, acc_ref, taps_ref, head, live_tiles(block, kstart, nw))
         conv = acc_ref[0]
         for a in range(1, QCONV):
             conv = conv + pltpu.roll(acc_ref[a], a, 0)
@@ -224,7 +227,7 @@
         g_ref[0] = gcp
         for a in range(1, QCONV):
             g_ref[a] = pltpu.roll(gcp, EXT - a, 0)
-        sums = tap_products(sh_ref, g_ref, width)
+        sums = tap_products(sh_ref, g_ref, live_tiles(block, kstart, nw))
         for b in range(KCONV):
             for a in range(QCONV):
                 tacc_ref[e * TAPS + a * KCONV + b] += sums[(a, b)]
@@ -251,7 +254,7 @@
         sh_ref[0] = gxv[:, :width]
         for b in range(1, KCONV):
             sh_ref[b] = pltpu.roll(gxv, width + TQ - b, 1)[:, :width]
-        tap_accumulate(sh_ref, acc_ref, taps_ref, e, width)
+        tap_accumulate(sh_ref, acc_ref, taps_ref, e, live_tiles(block, kstart, nw))
         gmk = acc_ref[0]
         for a in range(1, QCONV):
             gmk = gmk + pltpu.roll(acc_ref[a], EXT - a, 0)
@@ -518,8 +521,8 @@
             contract_rows(normed_own, grad_v_own),
         ]
     )
-    red = lax.psum_scatter(partials, "row", scatter_dimension=1, tiled=True)
-    got = lax.all_to_all(red, "seq", 1, 1, tiled=True)
+    red = lax.psum_scatter(partials.astype(jnp.bfloat16), "row", scatter_dimension=1, tiled=True)
+    got = lax.all_to_all(red, "seq", 1, 1, tiled=True).astype(jnp.float32)
     got = got.reshape(3, groups, splits, rows_per_dev, pw).sum(axis=2)
     got = jnp.transpose(got, (0, 2, 1, 3)).reshape(3, rows_per_dev, width)
     grad_w_query, grad_w_key, grad_w_value = got[0], got[1], got[2]

time: 695 us -> 638 us (0.918)
  the two profiles are of different devices: /device:TPU:0 before, /device:TPU:5 now
where the time goes in v9:
time: 638 us; the launch traced here: 628 us
  waiting for transfers between devices  231 us (36%)
  Pallas kernels  165 us (26%)
  local copies, waits for them, and re-layouts  74.2 us (12%)
  matrix products  71.2 us (11%)
  other arithmetic  29.2 us (5%)
  starting transfers between devices  27.7 us (4%)
  blocking collectives  15.3 us (2%)
  between operations  15 us (2%)
    pallas_call x1, Pallas kernels, attention_backward(): pl.pallas_call(lambda *refs: bwd_kernel(*refs, nw=nw, length=length, nb=n...  107 us
    pallas_call x1, Pallas kernels, attention_forward(): pl.pallas_call(lambda *refs: fwd_kernel(*refs, nw=nw, length=length), gri...  57.4 us
    ppermute x3, waiting for transfers between devices, shards_body(): pieces.append(lax.ppermute(packed, 'row', route))  44.9 us
    ppermute x3, waiting for transfers between devices, shards_body(): ffn_grad = ffn_grad + lax.ppermute(sent, 'row', route).astype(jnp.float32)  42.2 us
    reduce_scatter x1, waiting for transfers between devices, shards_body(): lax.psum_scatter(contract_cols(grad_joint, joint).astype(jnp.bfloat16), '...  36.7 us
    all_gather x1, waiting for transfers between devices, shards_body(): normed_all = lax.all_gather(normed, 'seq', axis=0, tiled=True)  35.5 us
    all_gather x1, waiting for transfers between devices, shards_body(): grad_attn_all = lax.all_gather(grad_attn, 'seq', axis=0, tiled=True)  33 us
    ppermute x1, waiting for transfers between devices, shards_body(): grad_w_out = grad_w_out + lax.ppermute(red_out[j], ('row', 'seq'), route)  31.7 us
  transfers between devices with their start and end apart: 22, of which 12 were waited for; matrix products, arithmetic and copies ran while one was open for 15% of the time, Pallas kernels for 0%

profile of v9, /device:TPU:5, one launch (start us, length us, event | category | flops | bytes accessed | tf_op | source)
XLA Modules:
  0.0 628.2 jit_solution(15032260438762039602)
XLA Ops:
  15.0 35.5 %all-gather.5.cloned.1.call-done = bf16[1024,1536]{1,0:T(8,128)(2,1)} async-done(((bf16[128,1536]{1,0:T(8,128)(2,1)}), bf16[1024,1536]{1,0:T(8,128)(2,1)}) %all-gather.5.cloned.1.call-update) | async-done | bytes 3145744 | tf_op jit(solution)/shard_map/all_gather | solution.py:366
  72.6 57.4 %shard_map.237 = (bf16[8,2,128,96]{3,2,1,0:T(8,128)(2,1)}, f32[8,2,128,768]{3,2,1,0:T(8,128)}) custom-call(s32[1]{0:T(128)} %constant.96.clone.1.refs_0_, f32[132]{0:T(256)} %reshape.201.refs_1_, f32[4]{0:T(128)} %reshape.202.refs_2_, bf16[8,2,136,96]{3,2,1,0:T(8,128)(2,1)} %copy.99.refs_3_, bf16[2,1024,96]{2,1,0:T(8,128)(2,1)} %bitcast.221, ...), custom_call_target="tpu_custom_call" | custom-call | flops 862322688 | bytes 7077888 | tf_op jit(solution)/shard_map/pallas_call | solution.py:148
  132.0 15.3 %all_to_all.20 = bf16[8,128,192]{1,2,0:T(8,128)(2,1)S(1)} all-to-all(bf16[8,128,192]{1,2,0:T(8,128)(2,1)} %bitcast.238), channel_id=1, replica_groups=mesh['row'=4,'seq'=8] {'seq'}, dimensions={0} | all-to-all | bytes 786432 | tf_op jit(solution)/shard_map/all_to_all | solution.py:413
  161.6 22.3 %collective-permute-done = bf16[384,1536]{1,0:T(8,128)(2,1)} collective-permute-done((bf16[384,1536]{1,0:T(8,128)(2,1)}, bf16[384,1536]{1,0:T(8,128)(2,1)}, u32[]{:S(2)}, u32[]{:S(2)}) %collective-permute-start) | collective-permute-done | bytes 1179680 | tf_op jit(solution)/shard_map/ppermute | solution.py:430
  187.0 22.2 %collective-permute-done.2 = bf16[384,1536]{1,0:T(8,128)(2,1)} collective-permute-done((bf16[384,1536]{1,0:T(8,128)(2,1)}, bf16[384,1536]{1,0:T(8,128)(2,1)}, u32[]{:S(2)}, u32[]{:S(2)}) %collective-permute-start.2) | collective-permute-done | bytes 1179680 | tf_op jit(solution)/shard_map/ppermute | solution.py:430
  217.4 8.4 %fusion.3 = f32[1024,1024]{0,1:T(8,128)} fusion(bf16[1024,1536]{1,0:T(8,128)(2,1)} %all-gather.7.cloned.1.call-done, bf16[1536,1536]{1,0:T(8,128)(2,1)} %bitcast.209), kind=kOutput, calls=%fused_computation.8 | convolution fusion | flops 3221225472 | bytes 10485760 | tf_op jit(solution)/shard_map/dot_general | solution.py:26
  229.2 7.3 %fusion.16 = (bf16[1024,512]{0,1:T(8,128)(2,1)S(1)}, bf16[1024,512]{0,1:T(8,128)(2,1)S(1)}, bf16[1024,512]{0,1:T(8,128)(2,1)}) fusion(f32[1024,1024]{0,1:T(8,128)} %fusion.3, bf16[1024,1536]{1,0:T(8,128)(2,1)} %all-gather.9.cloned.1.call-done, bf16[1536,1536]{1,0:T(8,128)(2,1)} %bitcast.210), kind=kOutput, calls=%fused_computation.29 | convolution fusion | flops 1619001344 | bytes 12058624 | tf_op jit(solution)/shard_map/dot_general | solution.py:36
  237.8 5.0 convolution_convert_fusion.2
  242.9 36.7 %reduce-scatter.7.cloned.1.call-done = bf16[128,1536]{1,0:T(8,128)(2,1)} async-done(((bf16[1024,1536]{1,0:T(8,128)(2,1)}), bf16[128,1536]{1,0:T(8,128)(2,1)}) %reduce-scatter.7.cloned.1.call-update) | async-done | bytes 393232 | tf_op jit(solution)/shard_map/reduce_scatter | solution.py:452
  286.0 5.3 convolution_convert_fusion
  291.3 33.0 %all-gather.11.cloned.1.call-done = bf16[1024,1536]{1,0:T(8,128)(2,1)} async-done(((bf16[128,1536]{1,0:T(8,128)(2,1)}), bf16[1024,1536]{1,0:T(8,128)(2,1)}) %all-gather.11.cloned.1.call-update) | async-done | bytes 3145744 | tf_op jit(solution)/shard_map/all_gather | solution.py:477
  332.1 107.1 %shard_map.238 = (bf16[8,2,128,96]{3,2,1,0:T(8,128)(2,1)}, f32[2,96,1024]{2,1,0:T(8,128)}, f32[2,96,1024]{2,1,0:T(8,128)}, f32[132,8,128]{2,1,0:T(8,128)}, f32[4,768]{1,0:T(4,128)}) custom-call(s32[1]{0:T(128)} %constant.96.clone.1.refs_0_, f32[132]{0:T(256)} %reshape.201.refs_1_, f32[4]{0:T(128)} %reshape.202.refs_2_, ...), custom_call_target="tpu_custom_call" | custom-call | flops 1869742080 | bytes 9437184 | tf_op jit(solution)/shard_map/pallas_call | solution.py:283
  450.0 4.1 copy.127
  473.0 4.5 convolution_convert_fusion.1
  479.9 6.6 %copy.129 = bf16[1536,1536]{1,0:T(8,128)(2,1)} copy(bf16[1536,1536]{0,1:T(8,128)(2,1)} %pad_maximum_fusion) | data formatting | bytes 9437184 | tf_op jit(solution)/shard_map/convert_element_type | solution.py:460
  486.6 4.1 dynamic-slice_bitcast_fusion.2
  497.5 4.0 fusion.63
  501.5 4.1 convolution_add_fusion.1
  505.7 4.3 fusion.38
  511.8 12.8 %collective-permute-done.10 = bf16[384,1536]{1,0:T(8,128)(2,1)} collective-permute-done((bf16[384,1536]{1,0:T(8,128)(2,1)}, bf16[384,1536]{1,0:T(8,128)(2,1)}, u32[]{:S(2)}, u32[]{:S(2)}) %collective-permute-start.10) | collective-permute-done | bytes 1179680 | tf_op jit(solution)/shard_map/ppermute | solution.py:465
  524.7 29.3 %collective-permute-done.9 = bf16[384,1536]{1,0:T(8,128)(2,1)} collective-permute-done((bf16[384,1536]{1,0:T(8,128)(2,1)}, bf16[384,1536]{1,0:T(8,128)(2,1)}, u32[]{:S(2)}, u32[]{:S(2)}) %collective-permute-start.9) | collective-permute-done | bytes 1179680 | tf_op jit(solution)/shard_map/ppermute | solution.py:465
  565.4 7.4 %all-to-all-start.2 = ((bf16[3,384,192]{2,0,1:T(4,128)(2,1)}), bf16[3,384,192]{2,0,1:T(4,128)(2,1)S(1)}, u32[]{:S(2)}, u32[]{:S(2)}) async-start(bf16[3,384,192]{2,0,1:T(4,128)(2,1)} %bitcast.64), calls=%async_computation.4 | async-start | bytes 1572864 | tf_op jit(solution)/shard_map/all_to_all | solution.py:525
  573.1 6.5 %collective-permute-start.3 = (f32[48,1536]{1,0:T(8,128)}, f32[48,1536]{1,0:T(8,128)S(1)}, u32[]{:S(2)}, u32[]{:S(2)}) collective-permute-start(f32[48,1536]{1,0:T(8,128)} %reduce-scatter.11.cloned.1.call-done), channel_id=1, source_target_pairs={{0,0},{1,4},{2,8},{3,12},{4,16},{5,20},{6,24},{7,28},{8,1},{9,5},{... | collective-permute-start | bytes 884744 | tf_op jit(solution)/shard_map/ppermute | solution.py:541
  583.1 31.7 %collective-permute-done.3 = f32[48,1536]{1,0:T(8,128)S(1)} collective-permute-done((f32[48,1536]{1,0:T(8,128)}, f32[48,1536]{1,0:T(8,128)S(1)}, u32[]{:S(2)}, u32[]{:S(2)}) %collective-permute-start.3) | collective-permute-done | bytes 294944 | tf_op jit(solution)/shard_map/ppermute | solution.py:541
  (206 shorter events, 138.4 us)
Async XLA Ops:
  7.2 43.3 %all-gather.5.cloned.1.call-start = ((), (), s32[]{:S(2)}) async-start(), calls=%async_computation.7 | async-start | bytes 3538944 | tf_op jit(solution)/shard_map/all_gather | solution.py:366
  10.6 206.8 %all-gather.7.cloned.1.call-start = ((), (), s32[]{:S(2)}) async-start(), calls=%async_computation.8 | async-start | bytes 3538944 | tf_op jit(solution)/shard_map/all_gather | solution.py:436
  152.6 76.6 %all-gather.9.cloned.1.call-start = ((), (), s32[]{:S(2)}) async-start(), calls=%async_computation.9 | async-start | bytes 3538944 | tf_op jit(solution)/shard_map/all_gather | solution.py:444
  156.9 27.0 %collective-permute-start = (bf16[384,1536]{1,0:T(8,128)(2,1)}, bf16[384,1536]{1,0:T(8,128)(2,1)}, u32[]{:S(2)}, u32[]{:S(2)}) collective-permute-start(bf16[384,1536]{1,0:T(8,128)(2,1)} %pad_maximum_fusion.5), channel_id=1, source_target_pairs={{0,24},{8,0},{16,8},{24,16},{1,25},{9,1},{17,9},{25,17},{2,26},{10... | collective-permute-start | bytes 3538952 | tf_op jit(solution)/shard_map/ppermute | solution.py:430
  158.1 27.6 %collective-permute-start.1 = (bf16[384,1536]{1,0:T(8,128)(2,1)}, bf16[384,1536]{1,0:T(8,128)(2,1)}, u32[]{:S(2)}, u32[]{:S(2)}) collective-permute-start(bf16[384,1536]{1,0:T(8,128)(2,1)} %pad_maximum_fusion.5), channel_id=1, source_target_pairs={{0,16},{8,24},{16,0},{24,8},{1,17},{9,25},{17,1},{25,9},{2,18},{10... | collective-permute-start | bytes 3538952 | tf_op jit(solution)/shard_map/ppermute | solution.py:430
  161.3 118.3 %reduce-scatter.7.cloned.1.call-start = ((), (), s32[]{:S(2)}) async-start(), calls=%async_computation.10 | async-start | bytes 3538944 | tf_op jit(solution)/shard_map/reduce_scatter | solution.py:452
  161.3 47.9 %collective-permute-start.2 = (bf16[384,1536]{1,0:T(8,128)(2,1)}, bf16[384,1536]{1,0:T(8,128)(2,1)}, u32[]{:S(2)}, u32[]{:S(2)}) collective-permute-start(bf16[384,1536]{1,0:T(8,128)(2,1)} %pad_maximum_fusion.5), channel_id=1, source_target_pairs={{0,8},{8,16},{16,24},{24,0},{1,9},{9,17},{17,25},{25,1},{2,10},{10... | collective-permute-start | bytes 3538952 | tf_op jit(solution)/shard_map/ppermute | solution.py:430
  161.6 49.0 %copy-start.6 = (bf16[512,384]{0,1:T(8,128)(2,1)S(1)}, bf16[512,384]{0,1:T(8,128)(2,1)}, u32[]{:S(2)}) copy-start(bf16[512,384]{0,1:T(8,128)(2,1)} %copy.102) | copy-start | bytes 1179652
  161.6 49.0 %copy-start.8 = (bf16[384,512]{1,0:T(8,128)(2,1)S(1)}, bf16[384,512]{1,0:T(8,128)(2,1)}, u32[]{:S(2)}) copy-start(bf16[384,512]{1,0:T(8,128)(2,1)} %param.25) | copy-start | bytes 1179652
  242.8 81.4 %all-gather.11.cloned.1.call-start = ((), (), s32[]{:S(2)}) async-start(), calls=%async_computation.11 | async-start | bytes 3538944 | tf_op jit(solution)/shard_map/all_gather | solution.py:477
  283.9 278.9 %reduce-scatter.13.cloned.1.call-start = ((), (), s32[]{:S(2)}) async-start(), calls=%async_computation.14 | async-start | bytes 2457600
  458.0 115.1 %reduce-scatter.11.cloned.1.call-start = ((), (), s32[]{:S(2)}) async-start(), calls=%async_computation.13 | async-start | bytes 1474560 | tf_op jit(solution)/shard_map/reduce_scatter | solution.py:530
  463.2 155.3 %reduce-scatter.9.cloned.1.call-start = ((), (), s32[]{:S(2)}) async-start(), calls=%async_computation.12 | async-start | bytes 3538944 | tf_op jit(solution)/shard_map/reduce_scatter | solution.py:479
  465.2 32.2 %all-to-all-start.1 = ((bf16[8,128,576]{1,2,0:T(8,128)(2,1)}), bf16[8,128,576]{1,2,0:T(8,128)(2,1)S(1)}, u32[]{:S(2)}, u32[]{:S(2)}) async-start(bf16[8,128,576]{1,2,0:T(8,128)(2,1)} %pad_maximum_fusion.6), calls=%async_computation.3 | async-start | bytes 2359296 | tf_op jit(solution)/shard_map/all_to_all | solution.py:413
  490.6 34.0 %collective-permute-start.10 = (bf16[384,1536]{1,0:T(8,128)(2,1)}, bf16[384,1536]{1,0:T(8,128)(2,1)}, u32[]{:S(2)}, u32[]{:S(2)}) collective-permute-start(bf16[384,1536]{1,0:T(8,128)(2,1)} %get-tuple-element.93), channel_id=1, source_target_pairs={{0,16},{8,24},{16,0},{24,8},{1,17},{9,25},{17,1},{25,9},{2,18},{10... | collective-permute-start | bytes 3538952 | tf_op jit(solution)/shard_map/ppermute | solution.py:465
  490.9 33.8 %collective-permute-start.11 = (bf16[384,1536]{1,0:T(8,128)(2,1)}, bf16[384,1536]{1,0:T(8,128)(2,1)}, u32[]{:S(2)}, u32[]{:S(2)}) collective-permute-start(bf16[384,1536]{1,0:T(8,128)(2,1)} %get-tuple-element.92), channel_id=1, source_target_pairs={{0,24},{8,0},{16,8},{24,16},{1,25},{9,1},{17,9},{25,17},{2,26},{10... | collective-permute-start | bytes 3538952 | tf_op jit(solution)/shard_map/ppermute | solution.py:465
  492.9 61.1 %collective-permute-start.9 = (bf16[384,1536]{1,0:T(8,128)(2,1)}, bf16[384,1536]{1,0:T(8,128)(2,1)}, u32[]{:S(2)}, u32[]{:S(2)}) collective-permute-start(bf16[384,1536]{1,0:T(8,128)(2,1)} %get-tuple-element.91), channel_id=1, source_target_pairs={{0,8},{8,16},{16,24},{24,0},{1,9},{9,17},{17,25},{25,1},{2,10},{10... | collective-permute-start | bytes 3538952 | tf_op jit(solution)/shard_map/ppermute | solution.py:465
  510.0 1.8 collective-permute-start.4
  511.8 45.1 %collective-permute-start.5 = (f32[4160]{0:T(1024)S(1)}, f32[4160]{0:T(1024)S(1)}, u32[]{:S(2)}, u32[]{:S(2)}) collective-permute-start(f32[4160]{0:T(1024)S(1)} %add.173), channel_id=1, source_target_pairs={{0,2},{1,3},{2,0},{3,1},{4,6},{5,7},{6,4},{7,5},{8,10},{9,11},{10,... | collective-permute-start | bytes 49928 | tf_op jit(solution)/shard_map/ppermute | solution.py:572
  556.9 4.7 collective-permute-start.6
  561.6 11.1 %collective-permute-start.7 = (f32[4160]{0:T(1024)S(1)}, f32[4160]{0:T(1024)S(1)}, u32[]{:S(2)}, u32[]{:S(2)}) collective-permute-start(f32[4160]{0:T(1024)S(1)} %add.175), channel_id=1, source_target_pairs={{0,8},{1,9},{2,10},{3,11},{4,12},{5,13},{6,14},{7,15},{8,0},{9,1},... | collective-permute-start | bytes 49928 | tf_op jit(solution)/shard_map/ppermute | solution.py:572
  565.4 49.5 %all-to-all-start.2 = ((bf16[3,384,192]{2,0,1:T(4,128)(2,1)}), bf16[3,384,192]{2,0,1:T(4,128)(2,1)S(1)}, u32[]{:S(2)}, u32[]{:S(2)}) async-start(bf16[3,384,192]{2,0,1:T(4,128)(2,1)} %bitcast.64), calls=%async_computation.4 | async-start | bytes 1572864 | tf_op jit(solution)/shard_map/all_to_all | solution.py:525
  572.8 8.0 %collective-permute-start.8 = (f32[4160]{0:T(1024)S(1)}, f32[4160]{0:T(1024)S(1)}, u32[]{:S(2)}, u32[]{:S(2)}) collective-permute-start(f32[4160]{0:T(1024)S(1)} %add.176), channel_id=1, source_target_pairs={{0,16},{1,17},{2,18},{3,19},{4,20},{5,21},{6,22},{7,23},{8,24},{9,... | collective-permute-start | bytes 49928 | tf_op jit(solution)/shard_map/ppermute | solution.py:572
  573.1 41.7 %collective-permute-start.3 = (f32[48,1536]{1,0:T(8,128)}, f32[48,1536]{1,0:T(8,128)S(1)}, u32[]{:S(2)}, u32[]{:S(2)}) collective-permute-start(f32[48,1536]{1,0:T(8,128)} %reduce-scatter.11.cloned.1.call-done), channel_id=1, source_target_pairs={{0,0},{1,4},{2,8},{3,12},{4,16},{5,20},{6,24},{7,28},{8,1},{9,5},{... | collective-permute-start | bytes 884744 | tf_op jit(solution)/shard_map/ppermute | solution.py:541
  (25 other events, 171.3 us)
Sparse Core Ops, SparseCore 0:
  10.7 39.7 all-gather.4
  152.7 37.6 all-gather.6
  192.0 37.1 all-gather.8
  243.0 36.5 reduce-scatter.6
  284.0 40.1 all-gather.10
  458.1 32.4 reduce-scatter.12
  493.5 56.0 reduce-scatter.10
  551.9 53.3 reduce-scatter.8

commit v10 on v9

--- a/solution.py
+++ b/solution.py
@@ -448,13 +448,9 @@
     grad_gate_vals = grad_hidden * up_vals * sigmoid_gate * (1.0 + gate_vals * (1.0 - sigmoid_gate))
     grad_up_vals = grad_hidden * gate_vals * sigmoid_gate
     grad_joint = jnp.concatenate([grad_gate_vals, grad_up_vals], axis=1).astype(jnp.bfloat16)
+    gnf_part = contract_cols(grad_joint, joint).astype(jnp.bfloat16)
+    grad_normed_ffn = lax.psum_scatter(gnf_part, "seq", scatter_dimension=0, tiled=True).astype(jnp.float32)
     grad_joint_w = contract_rows(ffn_rows, grad_joint)
-    grad_normed_ffn = lax.psum_scatter(
-        contract_cols(grad_joint, joint).astype(jnp.bfloat16),
-        "seq",
-        scatter_dimension=0,
-        tiled=True,
-    ).astype(jnp.float32)
     grad_pack = jnp.concatenate([grad_joint_w, jnp.transpose(grad_down_part)], axis=1)
     band = grad_pack.shape[0] // row_count
     grad_blocks = grad_pack.reshape(row_count, band, grad_pack.shape[1]).astype(jnp.bfloat16)

time: 638 us -> 638 us (level)
  no operation moved by 1% of the time
where the time goes in v10:
time: 638 us; the launch traced here: 628 us
  waiting for transfers between devices  231 us (36%)
  Pallas kernels  165 us (26%)
  local copies, waits for them, and re-layouts  74.2 us (12%)
  matrix products  71.2 us (11%)
  other arithmetic  29.2 us (5%)
  starting transfers between devices  27.7 us (4%)
  blocking collectives  15.3 us (2%)
  between operations  15 us (2%)
    pallas_call x1, Pallas kernels, attention_backward(): pl.pallas_call(lambda *refs: bwd_kernel(*refs, nw=nw, length=length, nb=n...  107 us
    pallas_call x1, Pallas kernels, attention_forward(): pl.pallas_call(lambda *refs: fwd_kernel(*refs, nw=nw, length=length), gri...  57.4 us
    ppermute x3, waiting for transfers between devices, shards_body(): pieces.append(lax.ppermute(packed, 'row', route))  44.9 us
    ppermute x3, waiting for transfers between devices, shards_body(): ffn_grad = ffn_grad + lax.ppermute(sent, 'row', route).astype(jnp.float32)  42.2 us
    reduce_scatter x1, waiting for transfers between devices, shards_body(): lax.psum_scatter(gnf_part, 'seq', scatter_dimension=0, tiled=True)  36.7 us
    all_gather x1, waiting for transfers between devices, shards_body(): normed_all = lax.all_gather(normed, 'seq', axis=0, tiled=True)  35.5 us
    all_gather x1, waiting for transfers between devices, shards_body(): grad_attn_all = lax.all_gather(grad_attn, 'seq', axis=0, tiled=True)  33 us
    ppermute x1, waiting for transfers between devices, shards_body(): grad_w_out = grad_w_out + lax.ppermute(red_out[j], ('row', 'seq'), route)  31.7 us
  transfers between devices with their start and end apart: 22, of which 12 were waited for; matrix products, arithmetic and copies ran while one was open for 15% of the time, Pallas kernels for 0%

profile of v10, /device:TPU:5, one launch (start us, length us, event | category | flops | bytes accessed | tf_op | source)
XLA Modules:
  0.0 628.2 jit_solution(15032260438762039602)
XLA Ops:
  15.0 35.5 %all-gather.5.cloned.1.call-done = bf16[1024,1536]{1,0:T(8,128)(2,1)} async-done(((bf16[128,1536]{1,0:T(8,128)(2,1)}), bf16[1024,1536]{1,0:T(8,128)(2,1)}) %all-gather.5.cloned.1.call-update) | async-done | bytes 3145744 | tf_op jit(solution)/shard_map/all_gather | solution.py:366
  72.6 57.4 %shard_map.237 = (bf16[8,2,128,96]{3,2,1,0:T(8,128)(2,1)}, f32[8,2,128,768]{3,2,1,0:T(8,128)}) custom-call(s32[1]{0:T(128)} %constant.96.clone.1.refs_0_, f32[132]{0:T(256)} %reshape.201.refs_1_, f32[4]{0:T(128)} %reshape.202.refs_2_, bf16[8,2,136,96]{3,2,1,0:T(8,128)(2,1)} %copy.99.refs_3_, bf16[2,1024,96]{2,1,0:T(8,128)(2,1)} %bitcast.221, ...), custom_call_target="tpu_custom_call" | custom-call | flops 862322688 | bytes 7077888 | tf_op jit(solution)/shard_map/pallas_call | solution.py:148
  132.0 15.3 %all_to_all.20 = bf16[8,128,192]{1,2,0:T(8,128)(2,1)S(1)} all-to-all(bf16[8,128,192]{1,2,0:T(8,128)(2,1)} %bitcast.238), channel_id=1, replica_groups=mesh['row'=4,'seq'=8] {'seq'}, dimensions={0} | all-to-all | bytes 786432 | tf_op jit(solution)/shard_map/all_to_all | solution.py:413
  161.6 22.3 %collective-permute-done = bf16[384,1536]{1,0:T(8,128)(2,1)} collective-permute-done((bf16[384,1536]{1,0:T(8,128)(2,1)}, bf16[384,1536]{1,0:T(8,128)(2,1)}, u32[]{:S(2)}, u32[]{:S(2)}) %collective-permute-start) | collective-permute-done | bytes 1179680 | tf_op jit(solution)/shard_map/ppermute | solution.py:430
  187.0 22.2 %collective-permute-done.2 = bf16[384,1536]{1,0:T(8,128)(2,1)} collective-permute-done((bf16[384,1536]{1,0:T(8,128)(2,1)}, bf16[384,1536]{1,0:T(8,128)(2,1)}, u32[]{:S(2)}, u32[]{:S(2)}) %collective-permute-start.2) | collective-permute-done | bytes 1179680 | tf_op jit(solution)/shard_map/ppermute | solution.py:430
  217.4 8.4 %fusion.3 = f32[1024,1024]{0,1:T(8,128)} fusion(bf16[1024,1536]{1,0:T(8,128)(2,1)} %all-gather.7.cloned.1.call-done, bf16[1536,1536]{1,0:T(8,128)(2,1)} %bitcast.209), kind=kOutput, calls=%fused_computation.8 | convolution fusion | flops 3221225472 | bytes 10485760 | tf_op jit(solution)/shard_map/dot_general | solution.py:26
  229.2 7.3 %fusion.16 = (bf16[1024,512]{0,1:T(8,128)(2,1)S(1)}, bf16[1024,512]{0,1:T(8,128)(2,1)S(1)}, bf16[1024,512]{0,1:T(8,128)(2,1)}) fusion(f32[1024,1024]{0,1:T(8,128)} %fusion.3, bf16[1024,1536]{1,0:T(8,128)(2,1)} %all-gather.9.cloned.1.call-done, bf16[1536,1536]{1,0:T(8,128)(2,1)} %bitcast.210), kind=kOutput, calls=%fused_computation.29 | convolution fusion | flops 1619001344 | bytes 12058624 | tf_op jit(solution)/shard_map/dot_general | solution.py:36
  237.8 5.0 convolution_convert_fusion.2
  242.9 36.7 %reduce-scatter.7.cloned.1.call-done = bf16[128,1536]{1,0:T(8,128)(2,1)} async-done(((bf16[1024,1536]{1,0:T(8,128)(2,1)}), bf16[128,1536]{1,0:T(8,128)(2,1)}) %reduce-scatter.7.cloned.1.call-update) | async-done | bytes 393232 | tf_op jit(solution)/shard_map/reduce_scatter | solution.py:452
  286.0 5.3 convolution_convert_fusion
  291.3 33.0 %all-gather.11.cloned.1.call-done = bf16[1024,1536]{1,0:T(8,128)(2,1)} async-done(((bf16[128,1536]{1,0:T(8,128)(2,1)}), bf16[1024,1536]{1,0:T(8,128)(2,1)}) %all-gather.11.cloned.1.call-update) | async-done | bytes 3145744 | tf_op jit(solution)/shard_map/all_gather | solution.py:473
  332.1 107.1 %shard_map.238 = (bf16[8,2,128,96]{3,2,1,0:T(8,128)(2,1)}, f32[2,96,1024]{2,1,0:T(8,128)}, f32[2,96,1024]{2,1,0:T(8,128)}, f32[132,8,128]{2,1,0:T(8,128)}, f32[4,768]{1,0:T(4,128)}) custom-call(s32[1]{0:T(128)} %constant.96.clone.1.refs_0_, f32[132]{0:T(256)} %reshape.201.refs_1_, f32[4]{0:T(128)} %reshape.202.refs_2_, ...), custom_call_target="tpu_custom_call" | custom-call | flops 1869742080 | bytes 9437184 | tf_op jit(solution)/shard_map/pallas_call | solution.py:283
  450.0 4.1 copy.127
  473.0 4.5 convolution_convert_fusion.1
  479.9 6.6 %copy.129 = bf16[1536,1536]{1,0:T(8,128)(2,1)} copy(bf16[1536,1536]{0,1:T(8,128)(2,1)} %pad_maximum_fusion) | data formatting | bytes 9437184 | tf_op jit(solution)/shard_map/convert_element_type | solution.py:456
  486.6 4.1 dynamic-slice_bitcast_fusion.2
  497.5 4.0 fusion.63
  501.5 4.1 convolution_add_fusion.1
  505.7 4.3 fusion.38
  511.8 12.8 %collective-permute-done.10 = bf16[384,1536]{1,0:T(8,128)(2,1)} collective-permute-done((bf16[384,1536]{1,0:T(8,128)(2,1)}, bf16[384,1536]{1,0:T(8,128)(2,1)}, u32[]{:S(2)}, u32[]{:S(2)}) %collective-permute-start.10) | collective-permute-done | bytes 1179680 | tf_op jit(solution)/shard_map/ppermute | solution.py:461
  524.7 29.3 %collective-permute-done.9 = bf16[384,1536]{1,0:T(8,128)(2,1)} collective-permute-done((bf16[384,1536]{1,0:T(8,128)(2,1)}, bf16[384,1536]{1,0:T(8,128)(2,1)}, u32[]{:S(2)}, u32[]{:S(2)}) %collective-permute-start.9) | collective-permute-done | bytes 1179680 | tf_op jit(solution)/shard_map/ppermute | solution.py:461
  565.4 7.4 %all-to-all-start.2 = ((bf16[3,384,192]{2,0,1:T(4,128)(2,1)}), bf16[3,384,192]{2,0,1:T(4,128)(2,1)S(1)}, u32[]{:S(2)}, u32[]{:S(2)}) async-start(bf16[3,384,192]{2,0,1:T(4,128)(2,1)} %bitcast.64), calls=%async_computation.4 | async-start | bytes 1572864 | tf_op jit(solution)/shard_map/all_to_all | solution.py:521
  573.1 6.5 %collective-permute-start.3 = (f32[48,1536]{1,0:T(8,128)}, f32[48,1536]{1,0:T(8,128)S(1)}, u32[]{:S(2)}, u32[]{:S(2)}) collective-permute-start(f32[48,1536]{1,0:T(8,128)} %reduce-scatter.11.cloned.1.call-done), channel_id=1, source_target_pairs={{0,0},{1,4},{2,8},{3,12},{4,16},{5,20},{6,24},{7,28},{8,1},{9,5},{... | collective-permute-start | bytes 884744 | tf_op jit(solution)/shard_map/ppermute | solution.py:537
  583.1 31.7 %collective-permute-done.3 = f32[48,1536]{1,0:T(8,128)S(1)} collective-permute-done((f32[48,1536]{1,0:T(8,128)}, f32[48,1536]{1,0:T(8,128)S(1)}, u32[]{:S(2)}, u32[]{:S(2)}) %collective-permute-start.3) | collective-permute-done | bytes 294944 | tf_op jit(solution)/shard_map/ppermute | solution.py:537
  (206 shorter events, 138.4 us)
Async XLA Ops:
  7.2 43.3 %all-gather.5.cloned.1.call-start = ((), (), s32[]{:S(2)}) async-start(), calls=%async_computation.7 | async-start | bytes 3538944 | tf_op jit(solution)/shard_map/all_gather | solution.py:366
  10.6 206.8 %all-gather.7.cloned.1.call-start = ((), (), s32[]{:S(2)}) async-start(), calls=%async_computation.8 | async-start | bytes 3538944 | tf_op jit(solution)/shard_map/all_gather | solution.py:436
  152.6 76.6 %all-gather.9.cloned.1.call-start = ((), (), s32[]{:S(2)}) async-start(), calls=%async_computation.9 | async-start | bytes 3538944 | tf_op jit(solution)/shard_map/all_gather | solution.py:444
  156.9 27.0 %collective-permute-start = (bf16[384,1536]{1,0:T(8,128)(2,1)}, bf16[384,1536]{1,0:T(8,128)(2,1)}, u32[]{:S(2)}, u32[]{:S(2)}) collective-permute-start(bf16[384,1536]{1,0:T(8,128)(2,1)} %pad_maximum_fusion.5), channel_id=1, source_target_pairs={{0,24},{8,0},{16,8},{24,16},{1,25},{9,1},{17,9},{25,17},{2,26},{10... | collective-permute-start | bytes 3538952 | tf_op jit(solution)/shard_map/ppermute | solution.py:430
  158.1 27.6 %collective-permute-start.1 = (bf16[384,1536]{1,0:T(8,128)(2,1)}, bf16[384,1536]{1,0:T(8,128)(2,1)}, u32[]{:S(2)}, u32[]{:S(2)}) collective-permute-start(bf16[384,1536]{1,0:T(8,128)(2,1)} %pad_maximum_fusion.5), channel_id=1, source_target_pairs={{0,16},{8,24},{16,0},{24,8},{1,17},{9,25},{17,1},{25,9},{2,18},{10... | collective-permute-start | bytes 3538952 | tf_op jit(solution)/shard_map/ppermute | solution.py:430
  161.3 118.3 %reduce-scatter.7.cloned.1.call-start = ((), (), s32[]{:S(2)}) async-start(), calls=%async_computation.10 | async-start | bytes 3538944 | tf_op jit(solution)/shard_map/reduce_scatter | solution.py:452
  161.3 47.9 %collective-permute-start.2 = (bf16[384,1536]{1,0:T(8,128)(2,1)}, bf16[384,1536]{1,0:T(8,128)(2,1)}, u32[]{:S(2)}, u32[]{:S(2)}) collective-permute-start(bf16[384,1536]{1,0:T(8,128)(2,1)} %pad_maximum_fusion.5), channel_id=1, source_target_pairs={{0,8},{8,16},{16,24},{24,0},{1,9},{9,17},{17,25},{25,1},{2,10},{10... | collective-permute-start | bytes 3538952 | tf_op jit(solution)/shard_map/ppermute | solution.py:430
  161.6 49.0 %copy-start.6 = (bf16[512,384]{0,1:T(8,128)(2,1)S(1)}, bf16[512,384]{0,1:T(8,128)(2,1)}, u32[]{:S(2)}) copy-start(bf16[512,384]{0,1:T(8,128)(2,1)} %copy.102) | copy-start | bytes 1179652
  161.6 49.0 %copy-start.8 = (bf16[384,512]{1,0:T(8,128)(2,1)S(1)}, bf16[384,512]{1,0:T(8,128)(2,1)}, u32[]{:S(2)}) copy-start(bf16[384,512]{1,0:T(8,128)(2,1)} %param.25) | copy-start | bytes 1179652
  242.8 81.4 %all-gather.11.cloned.1.call-start = ((), (), s32[]{:S(2)}) async-start(), calls=%async_computation.11 | async-start | bytes 3538944 | tf_op jit(solution)/shard_map/all_gather | solution.py:473
  283.9 278.9 %reduce-scatter.13.cloned.1.call-start = ((), (), s32[]{:S(2)}) async-start(), calls=%async_computation.14 | async-start | bytes 2457600
  458.0 115.1 %reduce-scatter.11.cloned.1.call-start = ((), (), s32[]{:S(2)}) async-start(), calls=%async_computation.13 | async-start | bytes 1474560 | tf_op jit(solution)/shard_map/reduce_scatter | solution.py:526
  463.2 155.3 %reduce-scatter.9.cloned.1.call-start = ((), (), s32[]{:S(2)}) async-start(), calls=%async_computation.12 | async-start | bytes 3538944 | tf_op jit(solution)/shard_map/reduce_scatter | solution.py:475
  465.2 32.2 %all-to-all-start.1 = ((bf16[8,128,576]{1,2,0:T(8,128)(2,1)}), bf16[8,128,576]{1,2,0:T(8,128)(2,1)S(1)}, u32[]{:S(2)}, u32[]{:S(2)}) async-start(bf16[8,128,576]{1,2,0:T(8,128)(2,1)} %pad_maximum_fusion.6), calls=%async_computation.3 | async-start | bytes 2359296 | tf_op jit(solution)/shard_map/all_to_all | solution.py:413
  490.6 34.0 %collective-permute-start.10 = (bf16[384,1536]{1,0:T(8,128)(2,1)}, bf16[384,1536]{1,0:T(8,128)(2,1)}, u32[]{:S(2)}, u32[]{:S(2)}) collective-permute-start(bf16[384,1536]{1,0:T(8,128)(2,1)} %get-tuple-element.93), channel_id=1, source_target_pairs={{0,16},{8,24},{16,0},{24,8},{1,17},{9,25},{17,1},{25,9},{2,18},{10... | collective-permute-start | bytes 3538952 | tf_op jit(solution)/shard_map/ppermute | solution.py:461
  490.9 33.8 %collective-permute-start.11 = (bf16[384,1536]{1,0:T(8,128)(2,1)}, bf16[384,1536]{1,0:T(8,128)(2,1)}, u32[]{:S(2)}, u32[]{:S(2)}) collective-permute-start(bf16[384,1536]{1,0:T(8,128)(2,1)} %get-tuple-element.92), channel_id=1, source_target_pairs={{0,24},{8,0},{16,8},{24,16},{1,25},{9,1},{17,9},{25,17},{2,26},{10... | collective-permute-start | bytes 3538952 | tf_op jit(solution)/shard_map/ppermute | solution.py:461
  492.9 61.1 %collective-permute-start.9 = (bf16[384,1536]{1,0:T(8,128)(2,1)}, bf16[384,1536]{1,0:T(8,128)(2,1)}, u32[]{:S(2)}, u32[]{:S(2)}) collective-permute-start(bf16[384,1536]{1,0:T(8,128)(2,1)} %get-tuple-element.91), channel_id=1, source_target_pairs={{0,8},{8,16},{16,24},{24,0},{1,9},{9,17},{17,25},{25,1},{2,10},{10... | collective-permute-start | bytes 3538952 | tf_op jit(solution)/shard_map/ppermute | solution.py:461
  510.0 1.8 collective-permute-start.4
  511.8 45.1 %collective-permute-start.5 = (f32[4160]{0:T(1024)S(1)}, f32[4160]{0:T(1024)S(1)}, u32[]{:S(2)}, u32[]{:S(2)}) collective-permute-start(f32[4160]{0:T(1024)S(1)} %add.173), channel_id=1, source_target_pairs={{0,2},{1,3},{2,0},{3,1},{4,6},{5,7},{6,4},{7,5},{8,10},{9,11},{10,... | collective-permute-start | bytes 49928 | tf_op jit(solution)/shard_map/ppermute | solution.py:568
  556.9 4.7 collective-permute-start.6
  561.6 11.1 %collective-permute-start.7 = (f32[4160]{0:T(1024)S(1)}, f32[4160]{0:T(1024)S(1)}, u32[]{:S(2)}, u32[]{:S(2)}) collective-permute-start(f32[4160]{0:T(1024)S(1)} %add.175), channel_id=1, source_target_pairs={{0,8},{1,9},{2,10},{3,11},{4,12},{5,13},{6,14},{7,15},{8,0},{9,1},... | collective-permute-start | bytes 49928 | tf_op jit(solution)/shard_map/ppermute | solution.py:568
  565.4 49.5 %all-to-all-start.2 = ((bf16[3,384,192]{2,0,1:T(4,128)(2,1)}), bf16[3,384,192]{2,0,1:T(4,128)(2,1)S(1)}, u32[]{:S(2)}, u32[]{:S(2)}) async-start(bf16[3,384,192]{2,0,1:T(4,128)(2,1)} %bitcast.64), calls=%async_computation.4 | async-start | bytes 1572864 | tf_op jit(solution)/shard_map/all_to_all | solution.py:521
  572.8 8.0 %collective-permute-start.8 = (f32[4160]{0:T(1024)S(1)}, f32[4160]{0:T(1024)S(1)}, u32[]{:S(2)}, u32[]{:S(2)}) collective-permute-start(f32[4160]{0:T(1024)S(1)} %add.176), channel_id=1, source_target_pairs={{0,16},{1,17},{2,18},{3,19},{4,20},{5,21},{6,22},{7,23},{8,24},{9,... | collective-permute-start | bytes 49928 | tf_op jit(solution)/shard_map/ppermute | solution.py:568
  573.1 41.7 %collective-permute-start.3 = (f32[48,1536]{1,0:T(8,128)}, f32[48,1536]{1,0:T(8,128)S(1)}, u32[]{:S(2)}, u32[]{:S(2)}) collective-permute-start(f32[48,1536]{1,0:T(8,128)} %reduce-scatter.11.cloned.1.call-done), channel_id=1, source_target_pairs={{0,0},{1,4},{2,8},{3,12},{4,16},{5,20},{6,24},{7,28},{8,1},{9,5},{... | collective-permute-start | bytes 884744 | tf_op jit(solution)/shard_map/ppermute | solution.py:537
  (25 other events, 171.3 us)
Sparse Core Ops, SparseCore 0:
  10.7 39.7 all-gather.4
  152.7 37.6 all-gather.6
  192.0 37.1 all-gather.8
  243.0 36.5 reduce-scatter.6
  284.0 40.1 all-gather.10
  458.1 32.4 reduce-scatter.12
  493.5 56.0 reduce-scatter.10
  551.9 53.3 reduce-scatter.8

commit v11 on v10

--- a/solution.py
+++ b/solution.py
@@ -517,10 +517,12 @@
             contract_rows(normed_own, grad_v_own),
         ]
     )
-    red = lax.psum_scatter(partials.astype(jnp.bfloat16), "row", scatter_dimension=1, tiled=True)
-    got = lax.all_to_all(red, "seq", 1, 1, tiled=True).astype(jnp.float32)
-    got = got.reshape(3, groups, splits, rows_per_dev, pw).sum(axis=2)
-    got = jnp.transpose(got, (0, 2, 1, 3)).reshape(3, rows_per_dev, width)
+    devices = row_count * seq_count
+    send = partials.astype(jnp.bfloat16).reshape(3, devices, rows_per_dev, pw)
+    send = jnp.transpose(send, (1, 0, 2, 3)).reshape(devices * 3 * rows_per_dev, pw)
+    got = lax.all_to_all(send, ("row", "seq"), 0, 0, tiled=True).astype(jnp.float32)
+    got = got.reshape(row_count, groups, splits, 3, rows_per_dev, pw).sum(axis=(0, 2))
+    got = jnp.transpose(got, (1, 2, 0, 3)).reshape(3, rows_per_dev, width)
     grad_w_query, grad_w_key, grad_w_value = got[0], got[1], got[2]
 
     red_out = lax.psum_scatter(grad_out_part, "row", scatter_dimension=0, tiled=True)
@@ -560,7 +562,6 @@
     small = jnp.concatenate(
         [gain_attn_part, gain_ffn_part, taps_full.reshape(-1), mix_full.reshape(-1)]
     )
-    devices = row_count * seq_count
     assert devices & (devices - 1) == 0
     mask = 1
     while mask < devices:

time: 638 us -> 619 us (0.970)
  the two profiles are of different devices: /device:TPU:5 before, /device:TPU:2 now
where the time goes in v11:
time: 619 us; the launch traced here: 610 us
  waiting for transfers between devices  223 us (36%)
  Pallas kernels  164 us (26%)
  matrix products  73.1 us (12%)
  local copies, waits for them, and re-layouts  52.6 us (8%)
  starting transfers between devices  36.2 us (6%)
  other arithmetic  30.6 us (5%)
  between operations  15.3 us (2%)
  blocking collectives  14.9 us (2%)
    pallas_call x1, Pallas kernels, attention_backward(): pl.pallas_call(lambda *refs: bwd_kernel(*refs, nw=nw, length=length, nb=n...  107 us
    pallas_call x1, Pallas kernels, attention_forward(): pl.pallas_call(lambda *refs: fwd_kernel(*refs, nw=nw, length=length), gri...  57.4 us
    ppermute x3, waiting for transfers between devices, shards_body(): pieces.append(lax.ppermute(packed, 'row', route))  46.6 us
    reduce_scatter x1, waiting for transfers between devices, shards_body(): lax.psum_scatter(gnf_part, 'seq', scatter_dimension=0, tiled=True)  39.4 us
    all_gather x1, waiting for transfers between devices, shards_body(): normed_all = lax.all_gather(normed, 'seq', axis=0, tiled=True)  35.2 us
    all_gather x1, waiting for transfers between devices, shards_body(): grad_attn_all = lax.all_gather(grad_attn, 'seq', axis=0, tiled=True)  32.1 us
    dot_general x6, matrix products, project(): return jnp.dot(values, weight, preferred_element_type=jnp.float32)  27.9 us
    dot_general x6, matrix products, contract_cols(): lax.dot_general(left, right, (((1,), (1,)), ((), ())), preferred_element_...  25.3 us
  transfers between devices with their start and end apart: 21, of which 14 were waited for; matrix products, arithmetic and copies ran while one was open for 18% of the time, Pallas kernels for 17%

profile of v11, /device:TPU:2, one launch (start us, length us, event | category | flops | bytes accessed | tf_op | source)
XLA Modules:
  0.0 610.0 jit_solution(17811265246658043275)
XLA Ops:
  15.0 35.2 %all-gather.5.cloned.1.call-done = bf16[1024,1536]{1,0:T(8,128)(2,1)} async-done(((bf16[128,1536]{1,0:T(8,128)(2,1)}), bf16[1024,1536]{1,0:T(8,128)(2,1)}) %all-gather.5.cloned.1.call-update) | async-done | bytes 3145744 | tf_op jit(solution)/shard_map/all_gather | solution.py:366
  64.4 57.4 %shard_map.237 = (bf16[8,2,128,96]{3,2,1,0:T(8,128)(2,1)}, f32[8,2,128,768]{3,2,1,0:T(8,128)}) custom-call(s32[1]{0:T(128)} %constant.96.clone.1.refs_0_, f32[132]{0:T(256)} %reshape.239.refs_1_, f32[4]{0:T(128)} %reshape.240.refs_2_, bf16[8,2,136,96]{3,2,1,0:T(8,128)(2,1)} %copy.98.refs_3_, bf16[2,1024,96]{2,1,0:T(8,128)(2,1)} %bitcast.226, ...), custom_call_target="tpu_custom_call" | custom-call | flops 862322688 | bytes 7077888 | tf_op jit(solution)/shard_map/pallas_call | solution.py:148
  123.1 14.9 %all_to_all.24 = bf16[8,128,192]{1,2,0:T(8,128)(2,1)S(1)} all-to-all(bf16[8,128,192]{1,2,0:T(8,128)(2,1)S(1)} %bitcast.243), channel_id=1, replica_groups=mesh['row'=4,'seq'=8] {'seq'}, dimensions={0} | all-to-all | bytes 786432 | tf_op jit(solution)/shard_map/all_to_all | solution.py:413
  150.4 23.2 %collective-permute-done = bf16[384,1536]{1,0:T(8,128)(2,1)S(1)} collective-permute-done((bf16[384,1536]{1,0:T(8,128)(2,1)}, bf16[384,1536]{1,0:T(8,128)(2,1)S(1)}, u32[]{:S(2)}, u32[]{:S(2)}) %collective-permute-start) | collective-permute-done | bytes 1179680 | tf_op jit(solution)/shard_map/ppermute | solution.py:430
  173.8 23.4 %collective-permute-done.1 = bf16[384,1536]{1,0:T(8,128)(2,1)} collective-permute-done((bf16[384,1536]{1,0:T(8,128)(2,1)}, bf16[384,1536]{1,0:T(8,128)(2,1)}, u32[]{:S(2)}, u32[]{:S(2)}) %collective-permute-start.1) | collective-permute-done | bytes 1179680 | tf_op jit(solution)/shard_map/ppermute | solution.py:430
  205.4 8.4 %fusion.3 = f32[1024,1024]{0,1:T(8,128)} fusion(bf16[1024,1536]{1,0:T(8,128)(2,1)} %all-gather.7.cloned.1.call-done, bf16[1536,1536]{1,0:T(8,128)(2,1)} %bitcast.215), kind=kOutput, calls=%fused_computation.9 | convolution fusion | flops 3221225472 | bytes 10485760 | tf_op jit(solution)/shard_map/dot_general | solution.py:26
  218.4 7.3 %fusion.13 = (bf16[1024,512]{0,1:T(8,128)(2,1)S(1)}, bf16[1024,512]{0,1:T(8,128)(2,1)S(1)}, bf16[1024,512]{0,1:T(8,128)(2,1)}) fusion(f32[1024,1024]{0,1:T(8,128)} %fusion.3, bf16[1024,1536]{1,0:T(8,128)(2,1)} %all-gather.9.cloned.1.call-done, bf16[1536,1536]{1,0:T(8,128)(2,1)} %bitcast.216), kind=kOutput, calls=%fused_computation.25 | convolution fusion | flops 1619001344 | bytes 12058624 | tf_op jit(solution)/shard_map/dot_general | solution.py:36
  227.0 4.9 convolution_convert_fusion.2
  232.0 39.4 %reduce-scatter.4.cloned.1.call-done = bf16[128,1536]{1,0:T(8,128)(2,1)} async-done(((bf16[1024,1536]{1,0:T(8,128)(2,1)}), bf16[128,1536]{1,0:T(8,128)(2,1)}) %reduce-scatter.4.cloned.1.call-update) | async-done | bytes 393232 | tf_op jit(solution)/shard_map/reduce_scatter | solution.py:452
  275.4 5.3 convolution_convert_fusion
  280.7 32.1 %all-gather.11.cloned.1.call-done = bf16[1024,1536]{1,0:T(8,128)(2,1)} async-done(((bf16[128,1536]{1,0:T(8,128)(2,1)}), bf16[1024,1536]{1,0:T(8,128)(2,1)}) %all-gather.11.cloned.1.call-update) | async-done | bytes 3145744 | tf_op jit(solution)/shard_map/all_gather | solution.py:473
  316.5 10.5 %reduce-scatter.6.cloned.1.call-start = ((), (), s32[]{:S(2)}) async-start(), calls=%async_computation.11 | async-start | bytes 3538944 | tf_op jit(solution)/shard_map/reduce_scatter | solution.py:475
  327.0 4.8 copy.112
  332.8 5.3 fusion.5
  338.1 5.7 convolution_convert_fusion.1
  348.1 106.7 %shard_map.238 = (bf16[8,2,128,96]{3,2,1,0:T(8,128)(2,1)}, f32[2,96,1024]{2,1,0:T(8,128)}, f32[2,96,1024]{2,1,0:T(8,128)}, f32[132,8,128]{2,1,0:T(8,128)}, f32[4,768]{1,0:T(4,128)}) custom-call(s32[1]{0:T(128)} %constant.96.clone.1.refs_0_, f32[132]{0:T(256)} %reshape.239.refs_1_, f32[4]{0:T(128)} %reshape.240.refs_2_, ...), custom_call_target="tpu_custom_call" | custom-call | flops 1869742080 | bytes 9437184 | tf_op jit(solution)/shard_map/pallas_call | solution.py:283
  462.0 5.0 pad_maximum_fusion
  467.0 6.6 %copy.126 = bf16[1536,1536]{1,0:T(8,128)(2,1)} copy(bf16[1536,1536]{0,1:T(8,128)(2,1)} %pad_maximum_fusion) | data formatting | bytes 9437184 | tf_op jit(solution)/shard_map/convert_element_type | solution.py:456
  495.1 15.8 %all-to-all-done.1 = bf16[8,128,576]{1,2,0:T(8,128)(2,1)S(1)} async-done(((bf16[8,128,576]{1,2,0:T(8,128)(2,1)}), bf16[8,128,576]{1,2,0:T(8,128)(2,1)S(1)}, u32[]{:S(2)}, u32[]{:S(2)}) %all-to-all-start.1) | async-done | bytes 1179680 | tf_op jit(solution)/shard_map/all_to_all | solution.py:413
  520.7 5.0 fusion.38
  528.6 14.6 %collective-permute-done.10 = bf16[384,1536]{1,0:T(8,128)(2,1)} collective-permute-done((bf16[384,1536]{1,0:T(8,128)(2,1)}, bf16[384,1536]{1,0:T(8,128)(2,1)}, u32[]{:S(2)}, u32[]{:S(2)}) %collective-permute-start.10) | collective-permute-done | bytes 1179680 | tf_op jit(solution)/shard_map/ppermute | solution.py:461
  548.1 8.3 %collective-permute-done.5 = f32[4160]{0:T(1024)S(1)} collective-permute-done((f32[4160]{0:T(1024)S(1)}, f32[4160]{0:T(1024)S(1)}, u32[]{:S(2)}, u32[]{:S(2)}) %collective-permute-start.5) | collective-permute-done | bytes 16672 | tf_op jit(solution)/shard_map/ppermute | solution.py:569
  561.3 11.0 %collective-permute-done.6 = f32[4160]{0:T(1024)S(1)} collective-permute-done((f32[4160]{0:T(1024)S(1)}, f32[4160]{0:T(1024)S(1)}, u32[]{:S(2)}, u32[]{:S(2)}) %collective-permute-start.6) | collective-permute-done | bytes 16672 | tf_op jit(solution)/shard_map/ppermute | solution.py:569
  584.8 9.6 %collective-permute-done.3 = f32[48,1536]{1,0:T(8,128)S(1)} collective-permute-done((f32[48,1536]{1,0:T(8,128)}, f32[48,1536]{1,0:T(8,128)S(1)}, u32[]{:S(2)}, u32[]{:S(2)}) %collective-permute-start.3) | collective-permute-done | bytes 294944 | tf_op jit(solution)/shard_map/ppermute | solution.py:539
  (215 shorter events, 134.4 us)
Async XLA Ops:
  7.2 43.0 %all-gather.5.cloned.1.call-start = ((), (), s32[]{:S(2)}) async-start(), calls=%async_computation.6 | async-start | bytes 3538944 | tf_op jit(solution)/shard_map/all_gather | solution.py:366
  10.6 194.8 %all-gather.7.cloned.1.call-start = ((), (), s32[]{:S(2)}) async-start(), calls=%async_computation.7 | async-start | bytes 3538944 | tf_op jit(solution)/shard_map/all_gather | solution.py:436
  63.4 74.7 %copy-start.2 = (f32[1,128,1536]{2,1,0:T(8,128)S(1)}, f32[1,128,1536]{2,1,0:T(8,128)}, u32[]{:S(2)}) copy-start(f32[1,128,1536]{2,1,0:T(8,128)} %param.14) | copy-start | bytes 2359300
  142.4 76.0 %all-gather.9.cloned.1.call-start = ((), (), s32[]{:S(2)}) async-start(), calls=%async_computation.8 | async-start | bytes 3538944 | tf_op jit(solution)/shard_map/all_gather | solution.py:444
  143.7 29.9 %collective-permute-start = (bf16[384,1536]{1,0:T(8,128)(2,1)}, bf16[384,1536]{1,0:T(8,128)(2,1)S(1)}, u32[]{:S(2)}, u32[]{:S(2)}) collective-permute-start(bf16[384,1536]{1,0:T(8,128)(2,1)} %pad_maximum_fusion.4), channel_id=1, source_target_pairs={{0,24},{8,0},{16,8},{24,16},{1,25},{9,1},{17,9},{25,17},{2,26},{10... | collective-permute-start | bytes 3538952 | tf_op jit(solution)/shard_map/ppermute | solution.py:430
  144.3 52.8 %collective-permute-start.1 = (bf16[384,1536]{1,0:T(8,128)(2,1)}, bf16[384,1536]{1,0:T(8,128)(2,1)}, u32[]{:S(2)}, u32[]{:S(2)}) collective-permute-start(bf16[384,1536]{1,0:T(8,128)(2,1)} %pad_maximum_fusion.4), channel_id=1, source_target_pairs={{0,16},{8,24},{16,0},{24,8},{1,17},{9,25},{17,1},{25,9},{2,18},{10... | collective-permute-start | bytes 3538952 | tf_op jit(solution)/shard_map/ppermute | solution.py:430
  147.7 123.7 %reduce-scatter.4.cloned.1.call-start = ((), (), s32[]{:S(2)}) async-start(), calls=%async_computation.9 | async-start | bytes 3538944 | tf_op jit(solution)/shard_map/reduce_scatter | solution.py:452
  147.8 50.7 %collective-permute-start.2 = (bf16[384,1536]{1,0:T(8,128)(2,1)}, bf16[384,1536]{1,0:T(8,128)(2,1)}, u32[]{:S(2)}, u32[]{:S(2)}) collective-permute-start(bf16[384,1536]{1,0:T(8,128)(2,1)} %pad_maximum_fusion.4), channel_id=1, source_target_pairs={{0,8},{8,16},{16,24},{24,0},{1,9},{9,17},{17,25},{25,1},{2,10},{10... | collective-permute-start | bytes 3538952 | tf_op jit(solution)/shard_map/ppermute | solution.py:430
  150.4 49.4 %copy-start.5 = (bf16[384,512]{1,0:T(8,128)(2,1)S(1)}, bf16[384,512]{1,0:T(8,128)(2,1)}, u32[]{:S(2)}) copy-start(bf16[384,512]{1,0:T(8,128)(2,1)} %param.25) | copy-start | bytes 1179652
  150.4 49.5 %copy-start.7 = (bf16[384,512]{1,0:T(8,128)(2,1)S(1)}, bf16[384,512]{1,0:T(8,128)(2,1)}, u32[]{:S(2)}) copy-start(bf16[384,512]{1,0:T(8,128)(2,1)} %param.24) | copy-start | bytes 1179652
  232.0 80.8 %all-gather.11.cloned.1.call-start = ((), (), s32[]{:S(2)}) async-start(), calls=%async_computation.10 | async-start | bytes 3538944 | tf_op jit(solution)/shard_map/all_gather | solution.py:473
  275.0 303.0 %reduce-scatter.8.cloned.1.call-start = ((), (), s32[]{:S(2)}) async-start(), calls=%async_computation.12 | async-start | bytes 1474560 | tf_op jit(solution)/shard_map/reduce_scatter | solution.py:528
  316.5 283.5 %reduce-scatter.6.cloned.1.call-start = ((), (), s32[]{:S(2)}) async-start(), calls=%async_computation.11 | async-start | bytes 3538944 | tf_op jit(solution)/shard_map/reduce_scatter | solution.py:475
  458.4 52.4 %all-to-all-start.1 = ((bf16[8,128,576]{1,2,0:T(8,128)(2,1)}), bf16[8,128,576]{1,2,0:T(8,128)(2,1)S(1)}, u32[]{:S(2)}, u32[]{:S(2)}) async-start(bf16[8,128,576]{1,2,0:T(8,128)(2,1)} %pad_maximum_fusion.5), calls=%async_computation.3 | async-start | bytes 2359296 | tf_op jit(solution)/shard_map/all_to_all | solution.py:413
  477.7 65.5 %collective-permute-start.10 = (bf16[384,1536]{1,0:T(8,128)(2,1)}, bf16[384,1536]{1,0:T(8,128)(2,1)}, u32[]{:S(2)}, u32[]{:S(2)}) collective-permute-start(bf16[384,1536]{1,0:T(8,128)(2,1)} %get-tuple-element.93), channel_id=1, source_target_pairs={{0,16},{8,24},{16,0},{24,8},{1,17},{9,25},{17,1},{25,9},{2,18},{10... | collective-permute-start | bytes 3538952 | tf_op jit(solution)/shard_map/ppermute | solution.py:461
  479.1 64.1 %collective-permute-start.11 = (bf16[384,1536]{1,0:T(8,128)(2,1)}, bf16[384,1536]{1,0:T(8,128)(2,1)}, u32[]{:S(2)}, u32[]{:S(2)}) collective-permute-start(bf16[384,1536]{1,0:T(8,128)(2,1)} %get-tuple-element.92), channel_id=1, source_target_pairs={{0,24},{8,0},{16,8},{24,16},{1,25},{9,1},{17,9},{25,17},{2,26},{10... | collective-permute-start | bytes 3538952 | tf_op jit(solution)/shard_map/ppermute | solution.py:461
  479.7 65.5 %collective-permute-start.9 = (bf16[384,1536]{1,0:T(8,128)(2,1)}, bf16[384,1536]{1,0:T(8,128)(2,1)}, u32[]{:S(2)}, u32[]{:S(2)}) collective-permute-start(bf16[384,1536]{1,0:T(8,128)(2,1)} %get-tuple-element.91), channel_id=1, source_target_pairs={{0,8},{8,16},{16,24},{24,0},{1,9},{9,17},{17,25},{25,1},{2,10},{10... | collective-permute-start | bytes 3538952 | tf_op jit(solution)/shard_map/ppermute | solution.py:461
  510.8 83.6 %all-to-all-start.2 = ((bf16[32,144,192]{2,1,0:T(8,128)(2,1)}), bf16[32,144,192]{2,1,0:T(8,128)(2,1)}, u32[]{:S(2)}, u32[]{:S(2)}) async-start(bf16[32,144,192]{2,1,0:T(8,128)(2,1)} %bitcast.208), calls=%async_computation.4 | async-start | bytes 4718592 | tf_op jit(solution)/shard_map/all_to_all | solution.py:523
  525.8 1.2 collective-permute-start.4
  527.0 29.4 %collective-permute-start.5 = (f32[4160]{0:T(1024)S(1)}, f32[4160]{0:T(1024)S(1)}, u32[]{:S(2)}, u32[]{:S(2)}) collective-permute-start(f32[4160]{0:T(1024)S(1)} %add.171), channel_id=1, source_target_pairs={{0,2},{1,3},{2,0},{3,1},{4,6},{5,7},{6,4},{7,5},{8,10},{9,11},{10,... | collective-permute-start | bytes 49928 | tf_op jit(solution)/shard_map/ppermute | solution.py:569
  556.4 15.9 %collective-permute-start.6 = (f32[4160]{0:T(1024)S(1)}, f32[4160]{0:T(1024)S(1)}, u32[]{:S(2)}, u32[]{:S(2)}) collective-permute-start(f32[4160]{0:T(1024)S(1)} %add.172), channel_id=1, source_target_pairs={{0,4},{1,5},{2,6},{3,7},{4,0},{5,1},{6,2},{7,3},{8,12},{9,13},{10,... | collective-permute-start | bytes 49928 | tf_op jit(solution)/shard_map/ppermute | solution.py:569
  572.3 3.8 collective-permute-start.7
  576.1 6.4 %collective-permute-start.8 = (f32[4160]{0:T(1024)S(1)}, f32[4160]{0:T(1024)S(1)}, u32[]{:S(2)}, u32[]{:S(2)}) collective-permute-start(f32[4160]{0:T(1024)S(1)} %add.174), channel_id=1, source_target_pairs={{0,16},{1,17},{2,18},{3,19},{4,20},{5,21},{6,22},{7,23},{8,24},{9,... | collective-permute-start | bytes 49928 | tf_op jit(solution)/shard_map/ppermute | solution.py:569
  578.0 16.4 %collective-permute-start.3 = (f32[48,1536]{1,0:T(8,128)}, f32[48,1536]{1,0:T(8,128)S(1)}, u32[]{:S(2)}, u32[]{:S(2)}) collective-permute-start(f32[48,1536]{1,0:T(8,128)} %reduce-scatter.8.cloned.1.call-done), channel_id=1, source_target_pairs={{0,0},{1,4},{2,8},{3,12},{4,16},{5,20},{6,24},{7,28},{8,1},{9,5},{... | collective-permute-start | bytes 884744 | tf_op jit(solution)/shard_map/ppermute | solution.py:539
  (30 other events, 226.9 us)
Sparse Core Ops, SparseCore 0:
  10.7 39.4 all-gather.4
  142.5 37.0 all-gather.6
  181.2 37.1 all-gather.8
  232.1 39.2 reduce-scatter.3
  275.2 37.5 all-gather.10
  316.6 27.5 reduce-scatter.7
  457.4 62.8 reduce-scatter.5

commit v12 on v11

--- a/solution.py
+++ b/solution.py
@@ -471,13 +471,15 @@
     )
     grad_attn = grad_middle.astype(jnp.bfloat16)
     grad_attn_all = lax.all_gather(grad_attn, "seq", axis=0, tiled=True)
-    ffn_part, grad_attn_all = lax.optimization_barrier((ffn_part, grad_attn_all))
+    ffn_part, grad_attn = lax.optimization_barrier((ffn_part, grad_attn))
     ffn_out = lax.psum_scatter(ffn_part, "seq", scatter_dimension=0, tiled=True).astype(jnp.float32)
     outputs = middle + ffn_out
-    grad_attn_tail = jnp.pad(grad_attn_all, ((0, TQ * extra), (0, 0)))
-    grad_heads_x = contract_cols(
-        lax.dynamic_slice_in_dim(grad_attn_tail, q0, nb_all * TQ, 0), wo_g
-    ).astype(jnp.bfloat16)
+    gh_tok = contract_cols(grad_attn, w_out).astype(jnp.bfloat16)
+    gh_send = jnp.repeat(gh_tok.reshape(blk, groups, pw), splits, axis=1)
+    gh_send = jnp.transpose(gh_send, (1, 0, 2)).reshape(seq_count * blk, pw)
+    gh_all = lax.all_to_all(gh_send, "seq", 0, 0, tiled=True)
+    gh_tail = jnp.pad(gh_all, ((0, TQ * extra), (0, 0)))
+    grad_heads_x = lax.dynamic_slice_in_dim(gh_tail, q0, nb_all * TQ, 0)
     gh_blocks = jnp.transpose(grad_heads_x.reshape(nb_all, TQ, 2, HD), (0, 2, 1, 3))
     grad_out_part = contract_rows(heads_own, lax.dynamic_slice_in_dim(grad_attn_all, q0, span, 0))
     gq_blk, gk_heads, gv_heads, tap_acc, mix_acc = attention_backward(
@@ -525,18 +527,19 @@
     got = jnp.transpose(got, (1, 2, 0, 3)).reshape(3, rows_per_dev, width)
     grad_w_query, grad_w_key, grad_w_value = got[0], got[1], got[2]
 
-    red_out = lax.psum_scatter(grad_out_part, "row", scatter_dimension=0, tiled=True)
-    red_out = red_out.reshape(splits, rows_per_dev, width)
+    nchunk = row_count * splits
+    out_chunks = grad_out_part.reshape(nchunk, rows_per_dev, width)
+    own_slot = row_index * splits + part
     grad_w_out = jnp.zeros((rows_per_dev, width), jnp.float32)
-    for src_part in range(splits):
-        for j in range(splits):
-            route = []
-            for r in range(row_count):
-                for g in range(groups):
-                    src = r * seq_count + g * splits + src_part
-                    dst = g * row_count * splits + r * splits + j
-                    route.append((src, dst))
-            grad_w_out = grad_w_out + lax.ppermute(red_out[j], ("row", "seq"), route)
+    for k in range(nchunk):
+        piece = lax.dynamic_index_in_dim(out_chunks, (own_slot + k) % nchunk, 0, keepdims=False)
+        route = []
+        for r in range(row_count):
+            for g in range(groups):
+                for h in range(splits):
+                    src_dev = r * seq_count + g * splits + h
+                    route.append((src_dev, g * nchunk + (r * splits + h + k) % nchunk))
+        grad_w_out = grad_w_out + lax.ppermute(piece, ("row", "seq"), route)
 
     grad_tok = to_tokens(jnp.concatenate([grad_q_own, grad_k_own, grad_v_own], axis=1))
     grad_tok = grad_tok.reshape(groups, blk, 3, pw)

time: 619 us -> 613 us (level)
  the two profiles are of different devices: /device:TPU:2 before, /device:TPU:5 now
where the time goes in v12:
time: 613 us; the launch traced here: 604 us
  waiting for transfers between devices  206 us (34%)
  Pallas kernels  164 us (27%)
  matrix products  75.5 us (12%)
  local copies, waits for them, and re-layouts  54 us (9%)
  starting transfers between devices  41.9 us (7%)
  other arithmetic  32.2 us (5%)
  between operations  15.3 us (2%)
  blocking collectives  14.3 us (2%)
    pallas_call x1, Pallas kernels, attention_backward(): pl.pallas_call(lambda *refs: bwd_kernel(*refs, nw=nw, length=length, nb=n...  107 us
    pallas_call x1, Pallas kernels, attention_forward(): pl.pallas_call(lambda *refs: fwd_kernel(*refs, nw=nw, length=length), gri...  57.4 us
    ppermute x3, waiting for transfers between devices, shards_body(): pieces.append(lax.ppermute(packed, 'row', route))  46.1 us
    reduce_scatter x1, waiting for transfers between devices, shards_body(): lax.psum_scatter(gnf_part, 'seq', scatter_dimension=0, tiled=True)  36.9 us
    all_gather x1, waiting for transfers between devices, shards_body(): normed_all = lax.all_gather(normed, 'seq', axis=0, tiled=True)  34.9 us
    ppermute x3, waiting for transfers between devices, shards_body(): ffn_grad = ffn_grad + lax.ppermute(sent, 'row', route).astype(jnp.float32)  32.3 us
    dot_general x6, matrix products, project(): return jnp.dot(values, weight, preferred_element_type=jnp.float32)  28 us
    dot_general x6, matrix products, contract_cols(): lax.dot_general(left, right, (((1,), (1,)), ((), ())), preferred_element_...  27.3 us
  transfers between devices with their start and end apart: 24, of which 15 were waited for; matrix products, arithmetic and copies ran while one was open for 20% of the time, Pallas kernels for 18%

profile of v12, /device:TPU:5, one launch (start us, length us, event | category | flops | bytes accessed | tf_op | source)
XLA Modules:
  0.0 603.6 jit_solution(7215492133419970783)
XLA Ops:
  15.7 34.9 %all-gather.5.cloned.1.call-done = bf16[1024,1536]{1,0:T(8,128)(2,1)} async-done(((bf16[128,1536]{1,0:T(8,128)(2,1)}), bf16[1024,1536]{1,0:T(8,128)(2,1)}) %all-gather.5.cloned.1.call-update) | async-done | bytes 3145744 | tf_op jit(solution)/shard_map/all_gather | solution.py:366
  64.8 57.4 %shard_map.237 = (bf16[8,2,128,96]{3,2,1,0:T(8,128)(2,1)}, f32[8,2,128,768]{3,2,1,0:T(8,128)}) custom-call(s32[1]{0:T(128)} %constant.122.clone.1.refs_0_, f32[132]{0:T(256)} %reshape.246.refs_1_, f32[4]{0:T(128)} %reshape.247.refs_2_, bf16[8,2,136,96]{3,2,1,0:T(8,128)(2,1)} %copy.99.refs_3_, bf16[2,1024,96]{2,1,0:T(8,128)(2,1)} %bitcast.239, ...), custom_call_target="tpu_custom_call" | custom-call | flops 862322688 | bytes 7077888 | tf_op jit(solution)/shard_map/pallas_call | solution.py:148
  123.5 14.3 %all_to_all.30 = bf16[8,128,192]{1,2,0:T(8,128)(2,1)S(1)} all-to-all(bf16[8,128,192]{1,2,0:T(8,128)(2,1)S(1)} %bitcast.255), channel_id=1, replica_groups=mesh['row'=4,'seq'=8] {'seq'}, dimensions={0} | all-to-all | bytes 786432 | tf_op jit(solution)/shard_map/all_to_all | solution.py:413
  148.3 22.2 %collective-permute-done = bf16[384,1536]{1,0:T(8,128)(2,1)S(1)} collective-permute-done((bf16[384,1536]{1,0:T(8,128)(2,1)}, bf16[384,1536]{1,0:T(8,128)(2,1)S(1)}, u32[]{:S(2)}, u32[]{:S(2)}) %collective-permute-start) | collective-permute-done | bytes 1179680 | tf_op jit(solution)/shard_map/ppermute | solution.py:430
  173.7 22.2 %collective-permute-done.2 = bf16[384,1536]{1,0:T(8,128)(2,1)} collective-permute-done((bf16[384,1536]{1,0:T(8,128)(2,1)}, bf16[384,1536]{1,0:T(8,128)(2,1)}, u32[]{:S(2)}, u32[]{:S(2)}) %collective-permute-start.2) | collective-permute-done | bytes 1179680 | tf_op jit(solution)/shard_map/ppermute | solution.py:430
  202.7 8.4 %fusion.5 = f32[1024,1024]{0,1:T(8,128)} fusion(bf16[1024,1536]{1,0:T(8,128)(2,1)} %all-gather.7.cloned.1.call-done, bf16[1536,1536]{1,0:T(8,128)(2,1)} %bitcast.228), kind=kOutput, calls=%fused_computation.11 | convolution fusion | flops 3221225472 | bytes 10485760 | tf_op jit(solution)/shard_map/dot_general | solution.py:26
  211.1 8.3 %all-gather.9.cloned.1.call-done = bf16[1024,1536]{1,0:T(8,128)(2,1)} async-done(((bf16[128,1536]{1,0:T(8,128)(2,1)}), bf16[1024,1536]{1,0:T(8,128)(2,1)}) %all-gather.9.cloned.1.call-update) | async-done | bytes 3145744 | tf_op jit(solution)/shard_map/all_gather | solution.py:444
  219.3 7.3 %fusion.15 = (bf16[1024,512]{0,1:T(8,128)(2,1)S(1)}, bf16[1024,512]{0,1:T(8,128)(2,1)S(1)}, bf16[1024,512]{0,1:T(8,128)(2,1)}) fusion(f32[1024,1024]{0,1:T(8,128)} %fusion.5, bf16[1024,1536]{1,0:T(8,128)(2,1)} %all-gather.9.cloned.1.call-done, bf16[1536,1536]{1,0:T(8,128)(2,1)} %bitcast.229), kind=kOutput, calls=%fused_computation.28 | convolution fusion | flops 1619001344 | bytes 12058624 | tf_op jit(solution)/shard_map/dot_general | solution.py:36
  228.0 4.9 convolution_convert_fusion.2
  233.0 36.9 %reduce-scatter.3.cloned.1.call-done = bf16[128,1536]{1,0:T(8,128)(2,1)} async-done(((bf16[1024,1536]{1,0:T(8,128)(2,1)}), bf16[128,1536]{1,0:T(8,128)(2,1)}) %reduce-scatter.3.cloned.1.call-update) | async-done | bytes 393232 | tf_op jit(solution)/shard_map/reduce_scatter | solution.py:452
  279.2 5.4 convolution_convert_fusion
  284.6 4.9 fusion.7
  294.6 6.5 %all-to-all-start.1 = ((bf16[8,128,192]{1,2,0:T(8,128)(2,1)}), bf16[8,128,192]{1,2,0:T(8,128)(2,1)S(1)}, u32[]{:S(2)}, u32[]{:S(2)}) async-start(bf16[8,128,192]{1,2,0:T(8,128)(2,1)} %bitcast.32), calls=%async_computation.3 | async-start | bytes 786432 | tf_op jit(solution)/shard_map/all_to_all | solution.py:480
  301.0 7.4 %convolution_convert_fusion.1 = bf16[1536,1024]{0,1:T(8,128)(2,1)} fusion(bf16[1024,1536]{1,0:T(8,128)(2,1)} %all-gather.7.cloned.1.call-done, bf16[1024,512]{0,1:T(8,128)(2,1)} %copy-done.29, bf16[1024,512]{0,1:T(8,128)(2,1)S(1)} %copy-done.28), kind=kOutput, calls=%fused_computation.3 | convolution fusion | flops 3226992640 | bytes 8388608 | tf_op jit(solution)/shard_map/dot_general | solution.py:30
  308.4 12.0 %all-to-all-done.1 = bf16[8,128,192]{1,2,0:T(8,128)(2,1)S(1)} async-done(((bf16[8,128,192]{1,2,0:T(8,128)(2,1)}), bf16[8,128,192]{1,2,0:T(8,128)(2,1)S(1)}, u32[]{:S(2)}, u32[]{:S(2)}) %all-to-all-start.1) | async-done | bytes 393248 | tf_op jit(solution)/shard_map/all_to_all | solution.py:480
  321.4 106.6 %shard_map.238 = (bf16[8,2,128,96]{3,2,1,0:T(8,128)(2,1)}, f32[2,96,1024]{2,1,0:T(8,128)}, f32[2,96,1024]{2,1,0:T(8,128)}, f32[132,8,128]{2,1,0:T(8,128)}, f32[4,768]{1,0:T(4,128)}) custom-call(s32[1]{0:T(128)} %constant.122.clone.1.refs_0_, f32[132]{0:T(256)} %reshape.246.refs_1_, f32[4]{0:T(128)} %reshape.247.refs_2_, ...), custom_call_target="tpu_custom_call" | custom-call | flops 1869742080 | bytes 9437184 | tf_op jit(solution)/shard_map/pallas_call | solution.py:283
  440.7 6.7 %copy.127 = bf16[1536,1536]{1,0:T(8,128)(2,1)} copy(bf16[1536,1536]{0,1:T(8,128)(2,1)} %pad_maximum_fusion) | data formatting | bytes 9437184 | tf_op jit(solution)/shard_map/convert_element_type | solution.py:456
  466.6 7.5 %all-to-all-start.3 = ((bf16[32,144,192]{2,1,0:T(8,128)(2,1)}), bf16[32,144,192]{2,1,0:T(8,128)(2,1)}, u32[]{:S(2)}, u32[]{:S(2)}) async-start(bf16[32,144,192]{2,1,0:T(8,128)(2,1)} %bitcast.221), calls=%async_computation.5 | async-start | bytes 4718592 | tf_op jit(solution)/shard_map/all_to_all | solution.py:525
  480.2 5.1 fusion.39
  491.3 29.2 %collective-permute-done.12 = bf16[384,1536]{1,0:T(8,128)(2,1)} collective-permute-done((bf16[384,1536]{1,0:T(8,128)(2,1)}, bf16[384,1536]{1,0:T(8,128)(2,1)}, u32[]{:S(2)}, u32[]{:S(2)}) %collective-permute-start.12) | collective-permute-done | bytes 1179680 | tf_op jit(solution)/shard_map/ppermute | solution.py:461
  523.4 6.9 %collective-permute-done.8 = f32[4160]{0:T(1024)S(1)} collective-permute-done((f32[4160]{0:T(1024)S(1)}, f32[4160]{0:T(1024)S(1)}, u32[]{:S(2)}, u32[]{:S(2)}) %collective-permute-start.8) | collective-permute-done | bytes 16672 | tf_op jit(solution)/shard_map/ppermute | solution.py:572
  536.3 9.9 %collective-permute-done.9 = f32[4160]{0:T(1024)S(1)} collective-permute-done((f32[4160]{0:T(1024)S(1)}, f32[4160]{0:T(1024)S(1)}, u32[]{:S(2)}, u32[]{:S(2)}) %collective-permute-start.9) | collective-permute-done | bytes 16672 | tf_op jit(solution)/shard_map/ppermute | solution.py:572
  561.2 6.1 %collective-permute-start.3 = (f32[48,1536]{1,0:T(8,128)S(1)}, f32[48,1536]{1,0:T(8,128)}, u32[]{:S(2)}, u32[]{:S(2)}) collective-permute-start(f32[48,1536]{1,0:T(8,128)S(1)} %get-tuple-element.101), channel_id=1, source_target_pairs={{0,0},{1,4},{2,8},{3,12},{4,16},{5,20},{6,24},{7,28},{8,1},{9,5},{... | collective-permute-start | bytes 884744 | tf_op jit(solution)/shard_map/ppermute | solution.py:542
  579.0 13.5 %collective-permute-done.3 = f32[48,1536]{1,0:T(8,128)} collective-permute-done((f32[48,1536]{1,0:T(8,128)S(1)}, f32[48,1536]{1,0:T(8,128)}, u32[]{:S(2)}, u32[]{:S(2)}) %collective-permute-start.3) | collective-permute-done | bytes 294944 | tf_op jit(solution)/shard_map/ppermute | solution.py:542
  (219 shorter events, 144.0 us)
Async XLA Ops:
  7.2 43.3 %all-gather.5.cloned.1.call-start = ((), (), s32[]{:S(2)}) async-start(), calls=%async_computation.6 | async-start | bytes 3538944 | tf_op jit(solution)/shard_map/all_gather | solution.py:366
  10.6 192.2 %all-gather.7.cloned.1.call-start = ((), (), s32[]{:S(2)}) async-start(), calls=%async_computation.7 | async-start | bytes 3538944 | tf_op jit(solution)/shard_map/all_gather | solution.py:436
  142.1 77.2 %all-gather.9.cloned.1.call-start = ((), (), s32[]{:S(2)}) async-start(), calls=%async_computation.8 | async-start | bytes 3538944 | tf_op jit(solution)/shard_map/all_gather | solution.py:444
  143.5 27.0 %collective-permute-start = (bf16[384,1536]{1,0:T(8,128)(2,1)}, bf16[384,1536]{1,0:T(8,128)(2,1)S(1)}, u32[]{:S(2)}, u32[]{:S(2)}) collective-permute-start(bf16[384,1536]{1,0:T(8,128)(2,1)} %pad_maximum_fusion.4), channel_id=1, source_target_pairs={{0,24},{8,0},{16,8},{24,16},{1,25},{9,1},{17,9},{25,17},{2,26},{10... | collective-permute-start | bytes 3538952 | tf_op jit(solution)/shard_map/ppermute | solution.py:430
  144.7 27.6 %collective-permute-start.1 = (bf16[384,1536]{1,0:T(8,128)(2,1)}, bf16[384,1536]{1,0:T(8,128)(2,1)}, u32[]{:S(2)}, u32[]{:S(2)}) collective-permute-start(bf16[384,1536]{1,0:T(8,128)(2,1)} %pad_maximum_fusion.4), channel_id=1, source_target_pairs={{0,16},{8,24},{16,0},{24,8},{1,17},{9,25},{17,1},{25,9},{2,18},{10... | collective-permute-start | bytes 3538952 | tf_op jit(solution)/shard_map/ppermute | solution.py:430
  147.8 122.0 %reduce-scatter.3.cloned.1.call-start = ((), (), s32[]{:S(2)}) async-start(), calls=%async_computation.9 | async-start | bytes 3538944 | tf_op jit(solution)/shard_map/reduce_scatter | solution.py:452
  147.9 47.9 %collective-permute-start.2 = (bf16[384,1536]{1,0:T(8,128)(2,1)}, bf16[384,1536]{1,0:T(8,128)(2,1)}, u32[]{:S(2)}, u32[]{:S(2)}) collective-permute-start(bf16[384,1536]{1,0:T(8,128)(2,1)} %pad_maximum_fusion.4), channel_id=1, source_target_pairs={{0,8},{8,16},{16,24},{24,0},{1,9},{9,17},{17,25},{25,1},{2,10},{10... | collective-permute-start | bytes 3538952 | tf_op jit(solution)/shard_map/ppermute | solution.py:430
  232.9 320.9 %all-gather.11.cloned.1.call-start = ((), (), s32[]{:S(2)}) async-start(), calls=%async_computation.11 | async-start | bytes 3538944 | tf_op jit(solution)/shard_map/all_gather | solution.py:473
  294.6 25.8 %all-to-all-start.1 = ((bf16[8,128,192]{1,2,0:T(8,128)(2,1)}), bf16[8,128,192]{1,2,0:T(8,128)(2,1)S(1)}, u32[]{:S(2)}, u32[]{:S(2)}) async-start(bf16[8,128,192]{1,2,0:T(8,128)(2,1)} %bitcast.32), calls=%async_computation.3 | async-start | bytes 786432 | tf_op jit(solution)/shard_map/all_to_all | solution.py:480
  431.7 34.9 %all-to-all-start.2 = ((bf16[8,128,576]{1,2,0:T(8,128)(2,1)}), bf16[8,128,576]{1,2,0:T(8,128)(2,1)S(1)}, u32[]{:S(2)}, u32[]{:S(2)}) async-start(bf16[8,128,576]{1,2,0:T(8,128)(2,1)} %pad_maximum_fusion.5), calls=%async_computation.4 | async-start | bytes 2359296 | tf_op jit(solution)/shard_map/all_to_all | solution.py:413
  435.6 158.7 %reduce-scatter.5.cloned.1.call-start = ((), (), s32[]{:S(2)}) async-start(), calls=%async_computation.10 | async-start | bytes 3538944 | tf_op jit(solution)/shard_map/reduce_scatter | solution.py:475
  451.2 36.9 %collective-permute-start.14 = (bf16[384,1536]{1,0:T(8,128)(2,1)}, bf16[384,1536]{1,0:T(8,128)(2,1)}, u32[]{:S(2)}, u32[]{:S(2)}) collective-permute-start(bf16[384,1536]{1,0:T(8,128)(2,1)} %get-tuple-element.92), channel_id=1, source_target_pairs={{0,24},{8,0},{16,8},{24,16},{1,25},{9,1},{17,9},{25,17},{2,26},{10... | collective-permute-start | bytes 3538952 | tf_op jit(solution)/shard_map/ppermute | solution.py:461
  452.4 38.9 %collective-permute-start.13 = (bf16[384,1536]{1,0:T(8,128)(2,1)}, bf16[384,1536]{1,0:T(8,128)(2,1)}, u32[]{:S(2)}, u32[]{:S(2)}) collective-permute-start(bf16[384,1536]{1,0:T(8,128)(2,1)} %get-tuple-element.93), channel_id=1, source_target_pairs={{0,16},{8,24},{16,0},{24,8},{1,17},{9,25},{17,1},{25,9},{2,18},{10... | collective-permute-start | bytes 3538952 | tf_op jit(solution)/shard_map/ppermute | solution.py:461
  453.6 66.9 %collective-permute-start.12 = (bf16[384,1536]{1,0:T(8,128)(2,1)}, bf16[384,1536]{1,0:T(8,128)(2,1)}, u32[]{:S(2)}, u32[]{:S(2)}) collective-permute-start(bf16[384,1536]{1,0:T(8,128)(2,1)} %get-tuple-element.91), channel_id=1, source_target_pairs={{0,8},{8,16},{16,24},{24,0},{1,9},{9,17},{17,25},{25,1},{2,10},{10... | collective-permute-start | bytes 3538952 | tf_op jit(solution)/shard_map/ppermute | solution.py:461
  466.6 102.9 %all-to-all-start.3 = ((bf16[32,144,192]{2,1,0:T(8,128)(2,1)}), bf16[32,144,192]{2,1,0:T(8,128)(2,1)}, u32[]{:S(2)}, u32[]{:S(2)}) async-start(bf16[32,144,192]{2,1,0:T(8,128)(2,1)} %bitcast.221), calls=%async_computation.5 | async-start | bytes 4718592 | tf_op jit(solution)/shard_map/all_to_all | solution.py:525
  485.4 1.5 collective-permute-start.7
  486.9 43.4 %collective-permute-start.8 = (f32[4160]{0:T(1024)S(1)}, f32[4160]{0:T(1024)S(1)}, u32[]{:S(2)}, u32[]{:S(2)}) collective-permute-start(f32[4160]{0:T(1024)S(1)} %add.208), channel_id=1, source_target_pairs={{0,2},{1,3},{2,0},{3,1},{4,6},{5,7},{6,4},{7,5},{8,10},{9,11},{10,... | collective-permute-start | bytes 49928 | tf_op jit(solution)/shard_map/ppermute | solution.py:572
  530.4 15.8 %collective-permute-start.9 = (f32[4160]{0:T(1024)S(1)}, f32[4160]{0:T(1024)S(1)}, u32[]{:S(2)}, u32[]{:S(2)}) collective-permute-start(f32[4160]{0:T(1024)S(1)} %add.209), channel_id=1, source_target_pairs={{0,4},{1,5},{2,6},{3,7},{4,0},{5,1},{6,2},{7,3},{8,12},{9,13},{10,... | collective-permute-start | bytes 49928 | tf_op jit(solution)/shard_map/ppermute | solution.py:572
  546.2 2.6 collective-permute-start.10
  548.8 2.6 collective-permute-start.11
  557.4 17.6 %collective-permute-start.6 = (f32[48,1536]{1,0:T(8,128)}, f32[48,1536]{1,0:T(8,128)S(1)}, u32[]{:S(2)}, u32[]{:S(2)}) collective-permute-start(f32[48,1536]{1,0:T(8,128)} %get-tuple-element.99), channel_id=1, source_target_pairs={{0,3},{1,7},{2,11},{3,15},{4,19},{5,23},{6,27},{7,31},{8,0},{9,4},... | collective-permute-start | bytes 884744 | tf_op jit(solution)/shard_map/ppermute | solution.py:542
  559.3 19.6 %collective-permute-start.5 = (f32[48,1536]{1,0:T(8,128)S(1)}, f32[48,1536]{1,0:T(8,128)S(1)}, u32[]{:S(2)}, u32[]{:S(2)}) collective-permute-start(f32[48,1536]{1,0:T(8,128)S(1)} %get-tuple-element.100), channel_id=1, source_target_pairs={{0,2},{1,6},{2,10},{3,14},{4,18},{5,22},{6,26},{7,30},{8,3},{9,7},... | collective-permute-start | bytes 884744 | tf_op jit(solution)/shard_map/ppermute | solution.py:542
  561.2 31.2 %collective-permute-start.3 = (f32[48,1536]{1,0:T(8,128)S(1)}, f32[48,1536]{1,0:T(8,128)}, u32[]{:S(2)}, u32[]{:S(2)}) collective-permute-start(f32[48,1536]{1,0:T(8,128)S(1)} %get-tuple-element.101), channel_id=1, source_target_pairs={{0,0},{1,4},{2,8},{3,12},{4,16},{5,20},{6,24},{7,28},{8,1},{9,5},{... | collective-permute-start | bytes 884744 | tf_op jit(solution)/shard_map/ppermute | solution.py:542
  567.3 25.1 %collective-permute-start.4 = (f32[48,1536]{1,0:T(8,128)S(1)}, f32[48,1536]{1,0:T(8,128)}, u32[]{:S(2)}, u32[]{:S(2)}) collective-permute-start(f32[48,1536]{1,0:T(8,128)S(1)} %get-tuple-element.98), channel_id=1, source_target_pairs={{0,1},{1,5},{2,9},{3,13},{4,17},{5,21},{6,25},{7,29},{8,2},{9,6},{... | collective-permute-start | bytes 884744 | tf_op jit(solution)/shard_map/ppermute | solution.py:542
  (32 other events, 357.7 us)
Sparse Core Ops, SparseCore 0:
  10.7 39.7 all-gather.4
  142.3 37.6 all-gather.6
  182.2 37.1 all-gather.8
  233.0 36.7 reduce-scatter.2
  273.6 47.8 all-gather.10
  453.7 66.9 reduce-scatter.4

commit v13 on v11

--- a/solution.py
+++ b/solution.py
@@ -471,13 +471,15 @@
     )
     grad_attn = grad_middle.astype(jnp.bfloat16)
     grad_attn_all = lax.all_gather(grad_attn, "seq", axis=0, tiled=True)
-    ffn_part, grad_attn_all = lax.optimization_barrier((ffn_part, grad_attn_all))
+    ffn_part, grad_attn = lax.optimization_barrier((ffn_part, grad_attn))
     ffn_out = lax.psum_scatter(ffn_part, "seq", scatter_dimension=0, tiled=True).astype(jnp.float32)
     outputs = middle + ffn_out
-    grad_attn_tail = jnp.pad(grad_attn_all, ((0, TQ * extra), (0, 0)))
-    grad_heads_x = contract_cols(
-        lax.dynamic_slice_in_dim(grad_attn_tail, q0, nb_all * TQ, 0), wo_g
-    ).astype(jnp.bfloat16)
+    gh_tok = contract_cols(grad_attn, w_out).astype(jnp.bfloat16)
+    gh_send = jnp.repeat(gh_tok.reshape(blk, groups, pw), splits, axis=1)
+    gh_send = jnp.transpose(gh_send, (1, 0, 2)).reshape(seq_count * blk, pw)
+    gh_all = lax.all_to_all(gh_send, "seq", 0, 0, tiled=True)
+    gh_tail = jnp.pad(gh_all, ((0, TQ * extra), (0, 0)))
+    grad_heads_x = lax.dynamic_slice_in_dim(gh_tail, q0, nb_all * TQ, 0)
     gh_blocks = jnp.transpose(grad_heads_x.reshape(nb_all, TQ, 2, HD), (0, 2, 1, 3))
     grad_out_part = contract_rows(heads_own, lax.dynamic_slice_in_dim(grad_attn_all, q0, span, 0))
     gq_blk, gk_heads, gv_heads, tap_acc, mix_acc = attention_backward(

time: 619 us -> 619 us (level)
    ppermute x3, waiting for transfers between devices: 16.6 us -> 38.4 us  [shards_body(): ffn_grad = ffn_grad + lax.ppermute(sent, 'row', route).astype(jnp.float32)]
    ppermute x5, waiting for transfers between devices: 23.5 us -> 2.9 us  [shards_body(): small = small + lax.ppermute(small, ('row', 'seq'), route)]
    all_to_all x1, waiting for transfers between devices: 15.8 us -> 0.01 us  [to_tokens(): got = lax.all_to_all(full, 'seq', 0, 0, tiled=True)]
    reduce_scatter x1, starting transfers between devices: 10.5 us -> 0.21 us  [shards_body(): lax.psum_scatter(ffn_part, 'seq', scatter_dimension=0, tiled=True)]
  transfers between devices with their start and end apart: 21 -> 22, of which waited for: 14 -> 13; matrix products, arithmetic and copies ran while one was open for 18% -> 19% of each run, Pallas kernels for 17% -> 17%
where the time goes in v13:
time: 619 us; the launch traced here: 610 us
  waiting for transfers between devices  222 us (36%)
  Pallas kernels  164 us (26%)
  matrix products  76.3 us (12%)
  local copies, waits for them, and re-layouts  52.4 us (8%)
  starting transfers between devices  34.6 us (6%)
  other arithmetic  30.4 us (5%)
  between operations  15.3 us (2%)
  blocking collectives  14.9 us (2%)
    pallas_call x1, Pallas kernels, attention_backward(): pl.pallas_call(lambda *refs: bwd_kernel(*refs, nw=nw, length=length, nb=n...  107 us
    pallas_call x1, Pallas kernels, attention_forward(): pl.pallas_call(lambda *refs: fwd_kernel(*refs, nw=nw, length=length), gri...  57.4 us
    ppermute x3, waiting for transfers between devices, shards_body(): pieces.append(lax.ppermute(packed, 'row', route))  46.5 us
    reduce_scatter x1, waiting for transfers between devices, shards_body(): lax.psum_scatter(gnf_part, 'seq', scatter_dimension=0, tiled=True)  39.4 us
    ppermute x3, waiting for transfers between devices, shards_body(): ffn_grad = ffn_grad + lax.ppermute(sent, 'row', route).astype(jnp.float32)  38.4 us
    all_gather x1, waiting for transfers between devices, shards_body(): grad_attn_all = lax.all_gather(grad_attn, 'seq', axis=0, tiled=True)  37.4 us
    all_gather x1, waiting for transfers between devices, shards_body(): normed_all = lax.all_gather(normed, 'seq', axis=0, tiled=True)  35.2 us
    dot_general x6, matrix products, project(): return jnp.dot(values, weight, preferred_element_type=jnp.float32)  28 us
  transfers between devices with their start and end apart: 22, of which 13 were waited for; matrix products, arithmetic and copies ran while one was open for 19% of the time, Pallas kernels for 17%

profile of v13, /device:TPU:2, one launch (start us, length us, event | category | flops | bytes accessed | tf_op | source)
XLA Modules:
  0.0 609.6 jit_solution(15925217250931911284)
XLA Ops:
  15.0 35.2 %all-gather.5.cloned.1.call-done = bf16[1024,1536]{1,0:T(8,128)(2,1)} async-done(((bf16[128,1536]{1,0:T(8,128)(2,1)}), bf16[1024,1536]{1,0:T(8,128)(2,1)}) %all-gather.5.cloned.1.call-update) | async-done | bytes 3145744 | tf_op jit(solution)/shard_map/all_gather | solution.py:366
  64.4 57.4 %shard_map.237 = (bf16[8,2,128,96]{3,2,1,0:T(8,128)(2,1)}, f32[8,2,128,768]{3,2,1,0:T(8,128)}) custom-call(s32[1]{0:T(128)} %constant.96.clone.1.refs_0_, f32[132]{0:T(256)} %reshape.244.refs_1_, f32[4]{0:T(128)} %reshape.245.refs_2_, bf16[8,2,136,96]{3,2,1,0:T(8,128)(2,1)} %copy.99.refs_3_, bf16[2,1024,96]{2,1,0:T(8,128)(2,1)} %bitcast.225, ...), custom_call_target="tpu_custom_call" | custom-call | flops 862322688 | bytes 7077888 | tf_op jit(solution)/shard_map/pallas_call | solution.py:148
  123.1 14.9 %all_to_all.30 = bf16[8,128,192]{1,2,0:T(8,128)(2,1)S(1)} all-to-all(bf16[8,128,192]{1,2,0:T(8,128)(2,1)S(1)} %bitcast.240), channel_id=1, replica_groups=mesh['row'=4,'seq'=8] {'seq'}, dimensions={0} | all-to-all | bytes 786432 | tf_op jit(solution)/shard_map/all_to_all | solution.py:413
  150.5 23.1 %collective-permute-done = bf16[384,1536]{1,0:T(8,128)(2,1)S(1)} collective-permute-done((bf16[384,1536]{1,0:T(8,128)(2,1)}, bf16[384,1536]{1,0:T(8,128)(2,1)S(1)}, u32[]{:S(2)}, u32[]{:S(2)}) %collective-permute-start) | collective-permute-done | bytes 1179680 | tf_op jit(solution)/shard_map/ppermute | solution.py:430
  173.7 23.4 %collective-permute-done.1 = bf16[384,1536]{1,0:T(8,128)(2,1)} collective-permute-done((bf16[384,1536]{1,0:T(8,128)(2,1)}, bf16[384,1536]{1,0:T(8,128)(2,1)}, u32[]{:S(2)}, u32[]{:S(2)}) %collective-permute-start.1) | collective-permute-done | bytes 1179680 | tf_op jit(solution)/shard_map/ppermute | solution.py:430
  205.4 8.4 %fusion.3 = f32[1024,1024]{0,1:T(8,128)} fusion(bf16[1024,1536]{1,0:T(8,128)(2,1)} %all-gather.7.cloned.1.call-done, bf16[1536,1536]{1,0:T(8,128)(2,1)} %bitcast.214), kind=kOutput, calls=%fused_computation.9 | convolution fusion | flops 3221225472 | bytes 10485760 | tf_op jit(solution)/shard_map/dot_general | solution.py:26
  213.8 4.6 all-gather.9.cloned.1.call-done
  218.4 7.3 %fusion.13 = (bf16[1024,512]{0,1:T(8,128)(2,1)S(1)}, bf16[1024,512]{0,1:T(8,128)(2,1)S(1)}, bf16[1024,512]{0,1:T(8,128)(2,1)}) fusion(f32[1024,1024]{0,1:T(8,128)} %fusion.3, bf16[1024,1536]{1,0:T(8,128)(2,1)} %all-gather.9.cloned.1.call-done, bf16[1536,1536]{1,0:T(8,128)(2,1)} %bitcast.215), kind=kOutput, calls=%fused_computation.26 | convolution fusion | flops 1619001344 | bytes 12058624 | tf_op jit(solution)/shard_map/dot_general | solution.py:36
  227.1 4.9 convolution_convert_fusion.2
  232.1 39.4 %reduce-scatter.4.cloned.1.call-done = bf16[128,1536]{1,0:T(8,128)(2,1)} async-done(((bf16[1024,1536]{1,0:T(8,128)(2,1)}), bf16[128,1536]{1,0:T(8,128)(2,1)}) %reduce-scatter.4.cloned.1.call-update) | async-done | bytes 393232 | tf_op jit(solution)/shard_map/reduce_scatter | solution.py:452
  275.5 37.4 %all-gather.11.cloned.1.call-done = bf16[1024,1536]{1,0:T(8,128)(2,1)} async-done(((bf16[128,1536]{1,0:T(8,128)(2,1)}), bf16[1024,1536]{1,0:T(8,128)(2,1)}) %all-gather.11.cloned.1.call-update) | async-done | bytes 3145744 | tf_op jit(solution)/shard_map/all_gather | solution.py:473
  316.7 4.8 copy.113
  322.4 5.4 convolution_convert_fusion
  327.8 5.0 fusion.5
  341.5 7.4 %convolution_convert_fusion.1 = bf16[1536,1024]{0,1:T(8,128)(2,1)} fusion(bf16[1024,1536]{1,0:T(8,128)(2,1)} %all-gather.7.cloned.1.call-done, bf16[1024,512]{0,1:T(8,128)(2,1)} %copy-done.30, bf16[1024,512]{0,1:T(8,128)(2,1)S(1)} %copy-done.29), kind=kOutput, calls=%fused_computation.3 | convolution fusion | flops 3226992640 | bytes 8388608 | tf_op jit(solution)/shard_map/dot_general | solution.py:30
  348.9 4.8 all-to-all-done.1
  354.7 106.7 %shard_map.238 = (bf16[8,2,128,96]{3,2,1,0:T(8,128)(2,1)}, f32[2,96,1024]{2,1,0:T(8,128)}, f32[2,96,1024]{2,1,0:T(8,128)}, f32[132,8,128]{2,1,0:T(8,128)}, f32[4,768]{1,0:T(4,128)}) custom-call(s32[1]{0:T(128)} %constant.96.clone.1.refs_0_, f32[132]{0:T(256)} %reshape.244.refs_1_, f32[4]{0:T(128)} %reshape.245.refs_2_, ...), custom_call_target="tpu_custom_call" | custom-call | flops 1869742080 | bytes 9437184 | tf_op jit(solution)/shard_map/pallas_call | solution.py:283
  468.8 4.9 pad_maximum_fusion
  473.7 6.6 %copy.127 = bf16[1536,1536]{1,0:T(8,128)(2,1)} copy(bf16[1536,1536]{0,1:T(8,128)(2,1)} %pad_maximum_fusion) | data formatting | bytes 9437184 | tf_op jit(solution)/shard_map/convert_element_type | solution.py:456
  501.3 5.9 all-to-all-start.3
  513.4 5.0 fusion.37
  521.1 34.9 %collective-permute-done.10 = bf16[384,1536]{1,0:T(8,128)(2,1)} collective-permute-done((bf16[384,1536]{1,0:T(8,128)(2,1)}, bf16[384,1536]{1,0:T(8,128)(2,1)}, u32[]{:S(2)}, u32[]{:S(2)}) %collective-permute-start.10) | collective-permute-done | bytes 1179680 | tf_op jit(solution)/shard_map/ppermute | solution.py:461
  562.5 4.4 collective-permute-start.6
  589.4 12.2 %collective-permute-done.3 = f32[48,1536]{1,0:T(8,128)S(1)} collective-permute-done((f32[48,1536]{1,0:T(8,128)}, f32[48,1536]{1,0:T(8,128)S(1)}, u32[]{:S(2)}, u32[]{:S(2)}) %collective-permute-start.3) | collective-permute-done | bytes 294944 | tf_op jit(solution)/shard_map/ppermute | solution.py:541
  (216 shorter events, 130.3 us)
Async XLA Ops:
  7.2 43.0 %all-gather.5.cloned.1.call-start = ((), (), s32[]{:S(2)}) async-start(), calls=%async_computation.7 | async-start | bytes 3538944 | tf_op jit(solution)/shard_map/all_gather | solution.py:366
  10.6 194.8 %all-gather.7.cloned.1.call-start = ((), (), s32[]{:S(2)}) async-start(), calls=%async_computation.8 | async-start | bytes 3538944 | tf_op jit(solution)/shard_map/all_gather | solution.py:436
  63.4 74.7 %copy-start.2 = (f32[1,128,1536]{2,1,0:T(8,128)S(1)}, f32[1,128,1536]{2,1,0:T(8,128)}, u32[]{:S(2)}) copy-start(f32[1,128,1536]{2,1,0:T(8,128)} %param.14) | copy-start | bytes 2359300
  142.3 76.0 %all-gather.9.cloned.1.call-start = ((), (), s32[]{:S(2)}) async-start(), calls=%async_computation.9 | async-start | bytes 3538944 | tf_op jit(solution)/shard_map/all_gather | solution.py:444
  143.7 30.0 %collective-permute-start = (bf16[384,1536]{1,0:T(8,128)(2,1)}, bf16[384,1536]{1,0:T(8,128)(2,1)S(1)}, u32[]{:S(2)}, u32[]{:S(2)}) collective-permute-start(bf16[384,1536]{1,0:T(8,128)(2,1)} %pad_maximum_fusion.4), channel_id=1, source_target_pairs={{0,24},{8,0},{16,8},{24,16},{1,25},{9,1},{17,9},{25,17},{2,26},{10... | collective-permute-start | bytes 3538952 | tf_op jit(solution)/shard_map/ppermute | solution.py:430
  144.3 52.8 %collective-permute-start.1 = (bf16[384,1536]{1,0:T(8,128)(2,1)}, bf16[384,1536]{1,0:T(8,128)(2,1)}, u32[]{:S(2)}, u32[]{:S(2)}) collective-permute-start(bf16[384,1536]{1,0:T(8,128)(2,1)} %pad_maximum_fusion.4), channel_id=1, source_target_pairs={{0,16},{8,24},{16,0},{24,8},{1,17},{9,25},{17,1},{25,9},{2,18},{10... | collective-permute-start | bytes 3538952 | tf_op jit(solution)/shard_map/ppermute | solution.py:430
  147.7 123.8 %reduce-scatter.4.cloned.1.call-start = ((), (), s32[]{:S(2)}) async-start(), calls=%async_computation.10 | async-start | bytes 3538944 | tf_op jit(solution)/shard_map/reduce_scatter | solution.py:452
  147.8 50.7 %collective-permute-start.2 = (bf16[384,1536]{1,0:T(8,128)(2,1)}, bf16[384,1536]{1,0:T(8,128)(2,1)}, u32[]{:S(2)}, u32[]{:S(2)}) collective-permute-start(bf16[384,1536]{1,0:T(8,128)(2,1)} %pad_maximum_fusion.4), channel_id=1, source_target_pairs={{0,8},{8,16},{16,24},{24,0},{1,9},{9,17},{17,25},{25,1},{2,10},{10... | collective-permute-start | bytes 3538952 | tf_op jit(solution)/shard_map/ppermute | solution.py:430
  150.5 49.3 %copy-start.8 = (bf16[384,512]{1,0:T(8,128)(2,1)S(1)}, bf16[384,512]{1,0:T(8,128)(2,1)}, u32[]{:S(2)}) copy-start(bf16[384,512]{1,0:T(8,128)(2,1)} %param.24) | copy-start | bytes 1179652
  232.1 80.8 %all-gather.11.cloned.1.call-start = ((), (), s32[]{:S(2)}) async-start(), calls=%async_computation.12 | async-start | bytes 3538944 | tf_op jit(solution)/shard_map/all_gather | solution.py:473
  275.1 310.3 %reduce-scatter.8.cloned.1.call-start = ((), (), s32[]{:S(2)}) async-start(), calls=%async_computation.13 | async-start | bytes 1474560 | tf_op jit(solution)/shard_map/reduce_scatter | solution.py:530
  337.8 15.9 %all-to-all-start.1 = ((bf16[8,128,192]{1,2,0:T(8,128)(2,1)}), bf16[8,128,192]{1,2,0:T(8,128)(2,1)S(1)}, u32[]{:S(2)}, u32[]{:S(2)}) async-start(bf16[8,128,192]{1,2,0:T(8,128)(2,1)} %bitcast.32), calls=%async_computation.3 | async-start | bytes 786432 | tf_op jit(solution)/shard_map/all_to_all | solution.py:480
  341.3 246.1 %reduce-scatter.6.cloned.1.call-start = ((), (), s32[]{:S(2)}) async-start(), calls=%async_computation.11 | async-start | bytes 3538944 | tf_op jit(solution)/shard_map/reduce_scatter | solution.py:475
  465.0 36.3 %all-to-all-start.2 = ((bf16[8,128,576]{1,2,0:T(8,128)(2,1)}), bf16[8,128,576]{1,2,0:T(8,128)(2,1)S(1)}, u32[]{:S(2)}, u32[]{:S(2)}) async-start(bf16[8,128,576]{1,2,0:T(8,128)(2,1)} %pad_maximum_fusion.5), calls=%async_computation.4 | async-start | bytes 2359296 | tf_op jit(solution)/shard_map/all_to_all | solution.py:413
  484.2 71.8 %collective-permute-start.10 = (bf16[384,1536]{1,0:T(8,128)(2,1)}, bf16[384,1536]{1,0:T(8,128)(2,1)}, u32[]{:S(2)}, u32[]{:S(2)}) collective-permute-start(bf16[384,1536]{1,0:T(8,128)(2,1)} %get-tuple-element.93), channel_id=1, source_target_pairs={{0,16},{8,24},{16,0},{24,8},{1,17},{9,25},{17,1},{25,9},{2,18},{10... | collective-permute-start | bytes 3538952 | tf_op jit(solution)/shard_map/ppermute | solution.py:461
  485.6 70.4 %collective-permute-start.11 = (bf16[384,1536]{1,0:T(8,128)(2,1)}, bf16[384,1536]{1,0:T(8,128)(2,1)}, u32[]{:S(2)}, u32[]{:S(2)}) collective-permute-start(bf16[384,1536]{1,0:T(8,128)(2,1)} %get-tuple-element.92), channel_id=1, source_target_pairs={{0,24},{8,0},{16,8},{24,16},{1,25},{9,1},{17,9},{25,17},{2,26},{10... | collective-permute-start | bytes 3538952 | tf_op jit(solution)/shard_map/ppermute | solution.py:461
  486.2 73.3 %collective-permute-start.9 = (bf16[384,1536]{1,0:T(8,128)(2,1)}, bf16[384,1536]{1,0:T(8,128)(2,1)}, u32[]{:S(2)}, u32[]{:S(2)}) collective-permute-start(bf16[384,1536]{1,0:T(8,128)(2,1)} %get-tuple-element.91), channel_id=1, source_target_pairs={{0,8},{8,16},{16,24},{24,0},{1,9},{9,17},{17,25},{25,1},{2,10},{10... | collective-permute-start | bytes 3538952 | tf_op jit(solution)/shard_map/ppermute | solution.py:461
  501.3 78.5 %all-to-all-start.3 = ((bf16[32,144,192]{2,1,0:T(8,128)(2,1)}), bf16[32,144,192]{2,1,0:T(8,128)(2,1)}, u32[]{:S(2)}, u32[]{:S(2)}) async-start(bf16[32,144,192]{2,1,0:T(8,128)(2,1)} %bitcast.207), calls=%async_computation.5 | async-start | bytes 4718592 | tf_op jit(solution)/shard_map/all_to_all | solution.py:525
  518.4 1.2 collective-permute-start.4
  519.6 42.8 %collective-permute-start.5 = (f32[4160]{0:T(1024)S(1)}, f32[4160]{0:T(1024)S(1)}, u32[]{:S(2)}, u32[]{:S(2)}) collective-permute-start(f32[4160]{0:T(1024)S(1)} %add.170), channel_id=1, source_target_pairs={{0,2},{1,3},{2,0},{3,1},{4,6},{5,7},{6,4},{7,5},{8,10},{9,11},{10,... | collective-permute-start | bytes 49928 | tf_op jit(solution)/shard_map/ppermute | solution.py:571
  562.5 6.9 %collective-permute-start.6 = (f32[4160]{0:T(1024)S(1)}, f32[4160]{0:T(1024)S(1)}, u32[]{:S(2)}, u32[]{:S(2)}) collective-permute-start(f32[4160]{0:T(1024)S(1)} %add.171), channel_id=1, source_target_pairs={{0,4},{1,5},{2,6},{3,7},{4,0},{5,1},{6,2},{7,3},{8,12},{9,13},{10,... | collective-permute-start | bytes 49928 | tf_op jit(solution)/shard_map/ppermute | solution.py:571
  569.4 4.3 collective-permute-start.7
  573.7 3.8 collective-permute-start.8
  585.5 16.1 %collective-permute-start.3 = (f32[48,1536]{1,0:T(8,128)}, f32[48,1536]{1,0:T(8,128)S(1)}, u32[]{:S(2)}, u32[]{:S(2)}) collective-permute-start(f32[48,1536]{1,0:T(8,128)} %reduce-scatter.8.cloned.1.call-done), channel_id=1, source_target_pairs={{0,0},{1,4},{2,8},{3,12},{4,16},{5,20},{6,24},{7,28},{8,1},{9,5},{... | collective-permute-start | bytes 884744 | tf_op jit(solution)/shard_map/ppermute | solution.py:541
  (31 other events, 279.6 us)
Sparse Core Ops, SparseCore 0:
  10.7 39.4 all-gather.4
  142.5 37.0 all-gather.6
  181.2 37.1 all-gather.8
  232.2 39.2 reduce-scatter.3
  275.3 37.6 all-gather.10
  316.8 27.6 reduce-scatter.7
  349.0 41.5 reduce-scatter.5
